TPU v7x, 32 devices: a whole 2x2x4 slice. The times are simulated.
32 devices in a mesh: tile: 8 (over z, y), pat: 4 (over x, core).
Axes of the slice: x: 2, y: 2, z: 4, core: 2. Of those that a mesh axis runs over, the one named last changes fastest.
Arguments:
- amplitudes: bfloat16 [1024, 128, 128], P(('tile', 'pat')), may hold values from 0.5 to 4
- batch_ids: int32 [2, 384], P(None, ('tile', 'pat')), may hold values from 0 to 31
- scan_tile: int32 [2, 384, 1], P(None, ('tile', 'pat')), may hold values from 0 to 7; in each aligned block of 12 rows (0 to 11, 12 to 23, ..., all dimensions but the last counted through in order) at most 3 rows name the same one
- scan_offset: int32 [2, 384, 2], P(None, ('tile', 'pat')), may hold values from 0 to 256
- object_tiles: float32 [2, 8, 384, 384], P(None, 'tile'), may hold values from -6 to 6
- probe: float32 [4, 2, 128, 128], replicated, may hold values from -3 to 3
Outputs:
- object_out: float32 [2, 8, 384, 384], P(None, 'tile')
- probe_out: float32 [4, 2, 128, 128], replicated
Inputs may be any that keep to these rules, and one draw needn't show every extreme that they name: `scan_tile`: in each step, the 12 entries of one device name no tile more than 3 times, and some device's entries name one tile exactly 3 times.
All inputs are finite; a program needn't handle non-finite values.
Results may differ from a plain program's by a relative error of at most 0.019.
The roundings to bfloat16 on the way count: a program that leaves them out, or rounds other values in their place, can miss the bound.
Values may be sent and summed in bfloat16 or wider, within the bound.
No kernel may reach another device: no remote copies, remote signals or barrier semaphores. Data moves between devices by JAX's collectives and lax.ppermute only.
A program may use at most 64 MiB of HBM per device.

v0:
```python
import math

import jax
import jax.numpy as jnp
from jax import lax
from jax.experimental import pallas as pl
from jax.experimental.pallas import tpu as pltpu
from jax.sharding import PartitionSpec as P

probe_rate = 8.0


def dft_tables(length):
    counter = jnp.arange(length, dtype=jnp.int32)
    product = counter[:, None] * counter[None, :] % length
    angle_table = 2.0 * math.pi / length * product.astype(jnp.float32)
    norm_factor = 1.0 / math.sqrt(length)
    table_re = (jnp.cos(angle_table) * norm_factor).astype(jnp.bfloat16)
    table_im = (-jnp.sin(angle_table) * norm_factor).astype(jnp.bfloat16)
    return (table_re, table_im, -table_im)


def transform(src_re, src_im, table_re, table_im):
    half_re = jnp.einsum(
        "kj,bmjc->bmkc", table_re, src_re, preferred_element_type=jnp.float32
    ) - jnp.einsum("kj,bmjc->bmkc", table_im, src_im, preferred_element_type=jnp.float32)
    half_im = jnp.einsum(
        "kj,bmjc->bmkc", table_re, src_im, preferred_element_type=jnp.float32
    ) + jnp.einsum("kj,bmjc->bmkc", table_im, src_re, preferred_element_type=jnp.float32)
    half_re = half_re.astype(jnp.bfloat16)
    half_im = half_im.astype(jnp.bfloat16)
    out_re = jnp.einsum(
        "bmkc,cl->bmkl", half_re, table_re, preferred_element_type=jnp.float32
    ) - jnp.einsum("bmkc,cl->bmkl", half_im, table_im, preferred_element_type=jnp.float32)
    out_im = jnp.einsum(
        "bmkc,cl->bmkl", half_re, table_im, preferred_element_type=jnp.float32
    ) + jnp.einsum("bmkc,cl->bmkl", half_im, table_re, preferred_element_type=jnp.float32)
    return (out_re, out_im)


def block_tables(table_re, table_im):
    left = jnp.concatenate(
        [jnp.concatenate([table_re, -table_im], 1), jnp.concatenate([table_im, table_re], 1)], 0
    )
    right = jnp.concatenate(
        [jnp.concatenate([table_re, table_im], 1), jnp.concatenate([-table_im, table_re], 1)], 0
    )
    return left, right


def entry_kernel(patch_ref, amp_ref, probe_ref, left_ref, right_ref, update_ref, grad_ref):
    modes, length = probe_ref.shape[0], probe_ref.shape[-1]

    @pl.when(pl.program_id(0) == 0)
    def _():
        grad_ref[...] = jnp.zeros(grad_ref.shape, grad_ref.dtype)

    patch_re = patch_ref[0].astype(jnp.float32)
    patch_im = patch_ref[1].astype(jnp.float32)
    left = left_ref[...]
    right = right_ref[...]
    exits_re, exits_im = [], []
    for m in range(modes):
        probe_re = probe_ref[m, 0]
        probe_im = probe_ref[m, 1]
        exits_re.append((probe_re * patch_re - probe_im * patch_im).astype(jnp.bfloat16))
        exits_im.append((probe_re * patch_im + probe_im * patch_re).astype(jnp.bfloat16))
    stacked = jnp.concatenate(
        [jnp.concatenate(exits_re, 1), jnp.concatenate(exits_im, 1)], 0
    )
    half = jnp.dot(left, stacked, preferred_element_type=jnp.float32).astype(jnp.bfloat16)

    def by_mode(wide):
        return jnp.concatenate(
            [
                jnp.concatenate(
                    [
                        wide[:length, m * length : (m + 1) * length],
                        wide[length:, m * length : (m + 1) * length],
                    ],
                    1,
                )
                for m in range(modes)
            ],
            0,
        )

    def by_part(tall):
        return jnp.concatenate(
            [
                jnp.concatenate(
                    [tall[m * length : (m + 1) * length, :length] for m in range(modes)], 1
                ),
                jnp.concatenate(
                    [tall[m * length : (m + 1) * length, length:] for m in range(modes)], 1
                ),
            ],
            0,
        )

    far = jnp.dot(by_mode(half), right, preferred_element_type=jnp.float32)
    intensity = jnp.zeros((length, length), jnp.float32)
    for m in range(modes):
        far_re = far[m * length : (m + 1) * length, :length]
        far_im = far[m * length : (m + 1) * length, length:]
        intensity = intensity + (far_re * far_re + far_im * far_im)
    measured = amp_ref[...].astype(jnp.float32)
    factor = measured / jnp.sqrt(jnp.maximum(intensity, 1.0)) - 1.0
    factor = jnp.concatenate([factor, factor], 1)
    factor = jnp.concatenate([factor] * modes, 0)
    scaled = (factor * far).astype(jnp.bfloat16)
    back = jnp.dot(right, by_part(scaled), preferred_element_type=jnp.float32).astype(
        jnp.bfloat16
    )
    change = jnp.dot(by_mode(back), left, preferred_element_type=jnp.float32)
    update_re = jnp.zeros((length, length), jnp.float32)
    update_im = jnp.zeros((length, length), jnp.float32)
    for m in range(modes):
        change_re = change[m * length : (m + 1) * length, :length]
        change_im = change[m * length : (m + 1) * length, length:]
        probe_re = probe_ref[m, 0]
        probe_im = probe_ref[m, 1]
        update_re = update_re + (probe_re * change_re + probe_im * change_im)
        update_im = update_im + (probe_re * change_im - probe_im * change_re)
        grad_ref[m, 0] += patch_re * change_re + patch_im * change_im
        grad_ref[m, 1] += patch_re * change_im - patch_im * change_re
    update_ref[0] = update_re.astype(update_ref.dtype)
    update_ref[1] = update_im.astype(update_ref.dtype)


def entries_kernel(patch, amp_in, probe_now, left, right):
    slots, length = amp_in.shape[0], amp_in.shape[-1]
    modes = probe_now.shape[0]
    flops = slots * 4 * 2 * (2 * length) * (2 * length) * (modes * length)
    return pl.pallas_call(
        entry_kernel,
        grid=(slots,),
        in_specs=[
            pl.BlockSpec((2, None, length, length), lambda s: (0, s, 0, 0)),
            pl.BlockSpec((None, length, length), lambda s: (s, 0, 0)),
            pl.BlockSpec(probe_now.shape, lambda s: (0, 0, 0, 0)),
            pl.BlockSpec(left.shape, lambda s: (0, 0)),
            pl.BlockSpec(right.shape, lambda s: (0, 0)),
        ],
        out_specs=[
            pl.BlockSpec((2, None, length, length), lambda s: (0, s, 0, 0)),
            pl.BlockSpec(probe_now.shape, lambda s: (0, 0, 0, 0)),
        ],
        out_shape=[
            jax.ShapeDtypeStruct((2, slots, length, length), jnp.bfloat16),
            jax.ShapeDtypeStruct(probe_now.shape, jnp.float32),
        ],
        compiler_params=pltpu.CompilerParams(dimension_semantics=("arbitrary",)),
        cost_estimate=pl.CostEstimate(
            flops=flops,
            transcendentals=slots * length * length,
            bytes_accessed=slots * length * length * 10 + probe_now.size * 8,
        ),
    )(patch, amp_in, probe_now, left, right)


def route(amplitudes, batch_ids, scan_tile, scan_offset, tiles_here):
    tile_count = lax.axis_size("tile")
    steps, batch_rows = batch_ids.shape
    capacity = max(2, 2 * batch_rows // tile_count)
    slots = tile_count * capacity
    length = amplitudes.shape[-1]
    target = scan_tile[:, :, 0]
    owner = target // tiles_here
    local_tile = target - owner * tiles_here
    onehot = (owner[:, :, None] == jnp.arange(tile_count, dtype=jnp.int32)).astype(jnp.int32)
    place_in = jnp.sum((jnp.cumsum(onehot, axis=1) - 1) * onehot, axis=2)
    slot_of = owner * capacity + place_in
    chosen = slot_of[:, None, :] == jnp.arange(slots, dtype=jnp.int32)[None, :, None]
    valid = jnp.any(chosen, axis=2).astype(jnp.int32)
    entry = jnp.argmax(chosen, axis=2).astype(jnp.int32)
    meta = jnp.stack(
        [
            jnp.take_along_axis(local_tile, entry, axis=1),
            jnp.take_along_axis(scan_offset[:, :, 0], entry, axis=1),
            jnp.take_along_axis(scan_offset[:, :, 1], entry, axis=1),
            valid,
        ],
        axis=2,
    ).astype(jnp.bfloat16)
    meta = jnp.pad(meta[:, :, None, :], ((0, 0), (0, 0), (0, 7), (0, length - 4)))
    ids = jnp.take_along_axis(batch_ids, entry, axis=1)
    amp_send = amplitudes[ids.reshape(-1)].reshape(steps, slots, length, length)
    payload = jnp.concatenate([amp_send, meta], axis=2)
    return payload.reshape(steps, tile_count, capacity, length + 8, length)


def exchange(payload, size):
    tile_count, capacity, rows, length = payload.shape
    arrived = lax.all_to_all(payload, "tile", 0, 0, tiled=True).reshape(
        tile_count * capacity, rows, length
    )
    meta = arrived[:, length, :4].astype(jnp.int32)
    meta_in = jnp.stack([meta[:, 0] * size + meta[:, 1], meta[:, 2], meta[:, 3]], axis=1)
    return arrived, meta_in


def group_size(axes):
    count = 1
    for axis in axes:
        count *= lax.axis_size(axis)
    return count


def sum_over(value, axes, send_type):
    count = group_size(axes)
    parts = lax.all_to_all(value.astype(send_type).reshape(count, -1), axes, 0, 0, tiled=True)
    total = jnp.sum(parts.astype(jnp.float32), axis=0, keepdims=True).astype(send_type)
    return total, count


def all_sum_a2a(value, axes):
    total, count = sum_over(value, axes, value.dtype)
    spread = lax.all_to_all(jnp.broadcast_to(total, (count, total.shape[1])), axes, 0, 0, tiled=True)
    return spread.reshape(value.shape)


def all_sum_pairs(value, axis, send_type):
    count = lax.axis_size(axis)
    if count & (count - 1):
        return lax.psum(value.astype(send_type), axis).astype(jnp.float32)
    total = value.astype(send_type).astype(jnp.float32)
    step = 1
    while step < count:
        pairs = [(i, i ^ step) for i in range(count)]
        other = lax.ppermute(total.astype(send_type), axis, pairs)
        total = total.astype(send_type).astype(jnp.float32) + other.astype(jnp.float32)
        step *= 2
    return total


def entries_pass(stacked, probe_now, amp_in, meta_in, tables):
    table_re, table_im, table_neg = tables
    length = probe_now.shape[-1]
    rows_all, size = stacked.shape[1], stacked.shape[2]
    within = jnp.arange(length, dtype=jnp.int32)
    row_at, col_at, valid = meta_in[:, 0], meta_in[:, 1], meta_in[:, 2]
    pick_rows = (
        (row_at[:, None, None] + within[None, :, None])
        == jnp.arange(rows_all, dtype=jnp.int32)[None, None, :]
    ) & (valid[:, None, None] > 0)
    pick_rows = pick_rows.astype(jnp.bfloat16)
    pick_cols = (
        (col_at[:, None, None] + within[None, None, :])
        == jnp.arange(size, dtype=jnp.int32)[None, :, None]
    ).astype(jnp.bfloat16)
    rows = jnp.einsum(
        "skq,xqc->xskc", pick_rows, stacked, preferred_element_type=jnp.float32
    ).astype(jnp.bfloat16)
    patch = jnp.einsum("xskc,scl->xskl", rows, pick_cols, preferred_element_type=jnp.float32)
    left, right = block_tables(tables[0], tables[1])
    update, probe_grad = entries_kernel(patch.astype(jnp.bfloat16), amp_in, probe_now, left, right)
    spread = jnp.einsum(
        "xskl,scl->xskc", update, pick_cols, preferred_element_type=jnp.float32
    ).astype(jnp.bfloat16)
    local_sum = jnp.einsum("skq,xskc->xqc", pick_rows, spread, preferred_element_type=jnp.float32)
    return local_sum, probe_grad


def one_step(tiles_now, probe_now, amp_in, meta_in, tables, batch_total):
    tiles_here, size = tiles_now.shape[1], tiles_now.shape[2]
    slots, length = amp_in.shape[0], amp_in.shape[-1]
    stacked = tiles_now.astype(jnp.bfloat16).reshape(2, tiles_here * size, size)
    chunk = max(d for d in range(1, min(slots, 24) + 1) if slots % d == 0)
    if chunk == slots:
        local_sum, probe_grad = entries_pass(stacked, probe_now, amp_in, meta_in, tables)
    else:

        def body(carry, piece):
            part_sum, part_grad = entries_pass(stacked, probe_now, piece[0], piece[1], tables)
            return (carry[0] + part_sum, carry[1] + part_grad), None

        start = (jnp.zeros(stacked.shape, jnp.float32), jnp.zeros(probe_now.shape, jnp.float32))
        pieces = (
            amp_in.reshape(slots // chunk, chunk, length + 8, length),
            meta_in.reshape(slots // chunk, chunk, 3),
        )
        (local_sum, probe_grad), _ = lax.scan(body, start, pieces)
    local_sum = local_sum.reshape(tiles_now.shape)
    probe_re = probe_now[:, 0]
    probe_im = probe_now[:, 1]
    peak_power = jnp.max(jnp.sum(probe_re * probe_re + probe_im * probe_im, axis=0))
    summed = all_sum_pairs(local_sum, "pat", jnp.bfloat16)
    tiles_next = tiles_now + summed / peak_power
    grad_sum = all_sum_a2a(probe_grad, ("tile", "pat"))
    probe_next = probe_now + probe_rate * grad_sum / batch_total
    return (tiles_next, probe_next)


def on_device(amplitudes, batch_ids, scan_tile, scan_offset, object_tiles, probe):
    tables = dft_tables(probe.shape[-1])
    tiles_here, size = object_tiles.shape[1], object_tiles.shape[2]
    batch_total = batch_ids.shape[1] * lax.axis_size("tile") * lax.axis_size("pat")
    payload = route(amplitudes, batch_ids, scan_tile, scan_offset, tiles_here)
    tiles_now = object_tiles
    probe_now = probe
    for step_no in range(batch_ids.shape[0]):
        amp_in, meta_in = exchange(payload[step_no], size)
        tiles_now, probe_now = one_step(tiles_now, probe_now, amp_in, meta_in, tables, batch_total)
    return (tiles_now, probe_now)


def solution(mesh):
    in_specs = (
        P(("tile", "pat"), None, None),
        P(None, ("tile", "pat")),
        P(None, ("tile", "pat"), None),
        P(None, ("tile", "pat"), None),
        P(None, "tile", None, None),
        P(),
    )
    out_specs = (P(None, "tile", None, None), P())
    return jax.shard_map(
        on_device, mesh=mesh, in_specs=in_specs, out_specs=out_specs, check_vma=False
    )
```

profile of v0, /device:TPU:0, one launch (start us, length us, event | category | flops | bytes accessed | tf_op | source)
XLA Modules:
  0.0 199.1 jit_solution(803747588862589614)
XLA Ops:
  12.5 7.4 %all-to-all-start = ((bf16[8,3,136,128]{3,2,1,0:T(8,128)(2,1)}), bf16[8,3,136,128]{3,2,1,0:T(8,128)(2,1)}, u32[]{:S(2)}, u32[]{:S(2)}) async-start(bf16[8,3,136,128]{3,2,1,0:T(8,128)(2,1)} %bitcast.13), calls=%async_computation | async-start | bytes 1671168 | tf_op jit(solution)/shard_map/all_to_all | solution.py:195
  21.2 20.1 %all-to-all-done = bf16[8,3,136,128]{3,2,1,0:T(8,128)(2,1)} async-done(((bf16[8,3,136,128]{3,2,1,0:T(8,128)(2,1)}), bf16[8,3,136,128]{3,2,1,0:T(8,128)(2,1)}, u32[]{:S(2)}, u32[]{:S(2)}) %all-to-all-start) | async-done | bytes 835616 | tf_op jit(solution)/shard_map/all_to_all | solution.py:195
  41.3 4.2 %all-to-all-start.1 = ((bf16[8,3,136,128]{3,2,1,0:T(8,128)(2,1)}), bf16[8,3,136,128]{3,2,1,0:T(8,128)(2,1)}, u32[]{:S(2)}, u32[]{:S(2)}) async-start(bf16[8,3,136,128]{3,2,1,0:T(8,128)(2,1)} %bitcast.33), calls=%async_computation.1 | async-start | bytes 1671168 | tf_op jit(solution)/shard_map/all_to_all | solution.py:195
  46.5 3.1 %convert_bitcast_fusion.1 = bf16[2,24,128,384]{3,2,0,1:T(8,128)(2,1)S(1)} fusion(s32[24,128]{1,0:T(8,128)S(1)} %get-tuple-element.40, pred[24]{0:T(512)(128)(4,1)S(1)} %compare_bitcast_fusion.1, f32[2,1,384,384]{3,2,1,0:T(8,128)S(1)} %copy-done.3), kind=kOutput, calls=%fused_computation.18 | convolution fusion | flops 1816952832 | bytes 5910552 | tf_op jit(solution)/shard_map/skq,xqc->xskc/dot_general | solution.py:252
  49.6 2.6 %fusion.73.patch_ref = bf16[2,24,128,128]{3,2,1,0:T(8,128)(2,1)} fusion(bf16[2,24,128,384]{3,2,0,1:T(8,128)(2,1)S(1)} %convert_bitcast_fusion.1, s32[24,128]{1,0:T(8,128)S(1)} %get-tuple-element.41), kind=kOutput, calls=%fused_computation.51 | convolution fusion | flops 605945856 | bytes 6303744 | tf_op jit(solution)/shard_map/xskc,scl->xskl/dot_general | solution.py:255
  52.2 25.1 %shard_map.77 = (bf16[2,24,128,128]{3,2,1,0:T(8,128)(2,1)}, f32[4,2,128,128]{3,2,1,0:T(8,128)}) custom-call(bf16[2,24,128,128]{3,2,1,0:T(8,128)(2,1)} %fusion.73.patch_ref, bf16[24,136,128]{2,1,0:T(8,128)(2,1)} %bitcast.14.amp_ref, f32[4,2,128,128]{3,2,1,0:T(8,128)} %probe_ref.1, bf16[256,256]{1,0:T(8,128)(2,1)} %get-tuple-element.28.left_ref, ...), custom_call_target="tpu_custom_call" | custom-call | flops 6442450944 | bytes 4980736 | tf_op jit(solution)/shard_map/pallas_call | solution.py:135
  77.3 5.3 %fusion.106 = bf16[2,1,384,384]{2,3,0,1:T(8,128)(2,1)S(1)} fusion(s32[24,128]{1,0:T(8,128)S(1)} %get-tuple-element.40, pred[24]{0:T(512)(128)(4,1)S(1)} %compare_bitcast_fusion.1, bf16[2,24,128,128]{3,2,1,0:T(8,128)(2,1)} %get-tuple-element.9, s32[24,128]{1,0:T(8,128)S(1)} %get-tuple-element.41), kind=kOutput, calls=%fused_computation.56 | convolution fusion | flops 2422112256 | bytes 2187288 | tf_op jit(solution)/shard_map/skq,xskc->xqc/dot_general | solution.py:261
  82.8 1.9 copy.52
  85.4 6.2 %all-to-all-start.2 = ((f32[32,1,4096]{2,1,0:T(1,128)}), f32[32,1,4096]{2,1,0:T(1,128)}, u32[]{:S(2)}, u32[]{:S(2)}) async-start(f32[32,1,4096]{2,1,0:T(1,128)} %bitcast.174), calls=%async_computation.2 | async-start | bytes 1048576 | tf_op jit(solution)/shard_map/all_to_all | solution.py:212
  95.6 11.3 %all-to-all-done.2 = f32[32,1,4096]{2,1,0:T(1,128)} async-done(((f32[32,1,4096]{2,1,0:T(1,128)}), f32[32,1,4096]{2,1,0:T(1,128)}, u32[]{:S(2)}, u32[]{:S(2)}) %all-to-all-start.2) | async-done | bytes 524320 | tf_op jit(solution)/shard_map/all_to_all | solution.py:212
  109.6 3.3 %all-to-all-start.3 = ((f32[32,1,4096]{2,1,0:T(1,128)}), f32[32,1,4096]{2,1,0:T(1,128)}, u32[]{:S(2)}, u32[]{:S(2)}) async-start(f32[32,1,4096]{2,1,0:T(1,128)} %broadcast_in_dim.6), calls=%async_computation.3 | async-start | bytes 1048576 | tf_op jit(solution)/shard_map/all_to_all | solution.py:219
  113.0 5.1 %convert_bitcast_fusion = bf16[2,24,128,384]{2,3,0,1:T(8,128)(2,1)S(1)} fusion(s32[24,128]{1,0:T(8,128)S(1)} %iota_add_fusion, pred[24]{0:T(512)(128)(4,1)S(1)} %compare_bitcast_fusion, f32[2,1,384,384]{2,3,0,1:T(8,128)S(1)} %copy.52, bf16[2,1,384,384]{2,3,0,1:T(8,128)(2,1)} %collective-permute-done.1, bf16[2,1,384,384]{2,3,0,1:T(8,128)(2,1)S(1)} %add_convert_fusion.1, ...), kind=kOutput, calls=%fused_computation.14 | convolution fusion | flops 1818427392 | bytes 7090204 | tf_op jit(solution)/shard_map/skq,xqc->xskc/dot_general | solution.py:252
  118.1 3.3 %fusion.68.patch_ref = bf16[2,24,128,128]{3,2,1,0:T(8,128)(2,1)} fusion(bf16[2,24,128,384]{2,3,0,1:T(8,128)(2,1)S(1)} %convert_bitcast_fusion, s32[24,128]{1,0:T(8,128)S(1)} %iota_add_fusion.1), kind=kOutput, calls=%fused_computation.50 | convolution fusion | flops 605945856 | bytes 6303744 | tf_op jit(solution)/shard_map/xskc,scl->xskl/dot_general | solution.py:255
  121.4 7.1 %all-to-all-done.3 = f32[32,1,4096]{2,1,0:T(1,128)} async-done(((f32[32,1,4096]{2,1,0:T(1,128)}), f32[32,1,4096]{2,1,0:T(1,128)}, u32[]{:S(2)}, u32[]{:S(2)}) %all-to-all-start.3) | async-done | bytes 524320 | tf_op jit(solution)/shard_map/all_to_all | solution.py:219
  131.0 25.1 %shard_map.78 = (bf16[2,24,128,128]{3,2,1,0:T(8,128)(2,1)}, f32[4,2,128,128]{3,2,1,0:T(8,128)}) custom-call(bf16[2,24,128,128]{3,2,1,0:T(8,128)(2,1)} %fusion.68.patch_ref, bf16[24,136,128]{2,1,0:T(8,128)(2,1)} %bitcast.34.amp_ref, f32[4,2,128,128]{3,2,1,0:T(8,128)} %add.206.probe_ref, bf16[256,256]{1,0:T(8,128)(2,1)} %get-tuple-element.28.left_ref, ...), custom_call_target="tpu_custom_call" | custom-call | flops 6442450944 | bytes 4980736 | tf_op jit(solution)/shard_map/pallas_call | solution.py:135
  156.2 3.3 %all-to-all-start.4 = ((f32[32,1,4096]{2,1,0:T(1,128)}), f32[32,1,4096]{2,1,0:T(1,128)}, u32[]{:S(2)}, u32[]{:S(2)}) async-start(f32[32,1,4096]{2,1,0:T(1,128)} %bitcast.175), calls=%async_computation.4 | async-start | bytes 1048576 | tf_op jit(solution)/shard_map/all_to_all | solution.py:212
  159.5 6.1 %fusion.113 = bf16[2,1,384,384]{2,3,0,1:T(8,128)(2,1)} fusion(s32[24,128]{1,0:T(8,128)S(1)} %iota_add_fusion, pred[24]{0:T(512)(128)(4,1)S(1)} %compare_bitcast_fusion, bf16[2,24,128,128]{3,2,1,0:T(8,128)(2,1)} %get-tuple-element.11, s32[24,128]{1,0:T(8,128)S(1)} %iota_add_fusion.1), kind=kOutput, calls=%fused_computation.57 | convolution fusion | flops 2422112256 | bytes 2187288 | tf_op jit(solution)/shard_map/skq,xskc->xqc/dot_general | solution.py:261
  165.7 2.2 %collective-permute-done.2 = bf16[2,1,384,384]{2,3,0,1:T(8,128)(2,1)S(1)} collective-permute-done((bf16[2,1,384,384]{2,3,0,1:T(8,128)(2,1)}, bf16[2,1,384,384]{2,3,0,1:T(8,128)(2,1)S(1)}, u32[]{:S(2)}, u32[]{:S(2)}) %collective-permute-start.2) | collective-permute-done | bytes 589856 | tf_op jit(solution)/shard_map/ppermute | solution.py:231
  167.8 2.0 %add_convert_fusion = bf16[2,1,384,384]{2,3,0,1:T(8,128)(2,1)} fusion(bf16[2,1,384,384]{2,3,0,1:T(8,128)(2,1)S(1)} %collective-permute-done.2, bf16[2,1,384,384]{2,3,0,1:T(8,128)(2,1)} %fusion.113), kind=kLoop, calls=%fused_computation.59 | loop fusion | flops 1179648 | bytes 1769472 | tf_op jit(solution)/shard_map/convert_element_type | solution.py:232
  171.4 3.6 %all-to-all-done.4 = f32[32,1,4096]{2,1,0:T(1,128)} async-done(((f32[32,1,4096]{2,1,0:T(1,128)}), f32[32,1,4096]{2,1,0:T(1,128)}, u32[]{:S(2)}, u32[]{:S(2)}) %all-to-all-start.4) | async-done | bytes 524320 | tf_op jit(solution)/shard_map/all_to_all | solution.py:212
  177.7 3.3 %all-to-all-start.5 = ((f32[32,1,4096]{2,1,0:T(1,128)}), f32[32,1,4096]{2,1,0:T(1,128)}, u32[]{:S(2)}, u32[]{:S(2)}) async-start(f32[32,1,4096]{2,1,0:T(1,128)} %broadcast_in_dim.8), calls=%async_computation.5 | async-start | bytes 1048576 | tf_op jit(solution)/shard_map/all_to_all | solution.py:219
  181.7 7.8 %collective-permute-done.3 = bf16[2,1,384,384]{2,3,0,1:T(8,128)(2,1)} collective-permute-done((bf16[2,1,384,384]{2,3,0,1:T(8,128)(2,1)}, bf16[2,1,384,384]{2,3,0,1:T(8,128)(2,1)}, u32[]{:S(2)}, u32[]{:S(2)}) %collective-permute-start.3) | collective-permute-done | bytes 589856 | tf_op jit(solution)/shard_map/ppermute | solution.py:231
  189.5 4.1 %divide_add_fusion = f32[2,1,384,384]{2,3,0,1:T(8,128)} fusion(bf16[2,1,384,384]{2,3,0,1:T(8,128)(2,1)} %collective-permute-done.3, bf16[2,1,384,384]{2,3,0,1:T(8,128)(2,1)} %add_convert_fusion, f32[]{:T(128)} %reduce_max.19, f32[2,1,384,384]{2,3,0,1:T(8,128)S(1)} %copy.52, f32[]{:T(128)} %reduce_max.18, bf16[2,1,384,384]{2,3,0,1:T(8,128)(2,1)} %collective-permute-done.1, ...), kind=kLoop, calls=%fused_computation.58 | loop fusion | flops 2949120 | bytes 4718600 | tf_op jit(solution)/shard_map/add | solution.py:289
  193.6 2.7 %copy.59 = f32[2,1,384,384]{3,2,1,0:T(8,128)} copy(f32[2,1,384,384]{2,3,0,1:T(8,128)} %divide_add_fusion) | data formatting | bytes 2359296
  (74 shorter events, 31.9 us)
Async XLA Ops:
  0.6 9.5 %copy-start = (bf16[32,128,128]{2,1,0:T(8,128)(2,1)S(1)}, bf16[32,128,128]{2,1,0:T(8,128)(2,1)}, u32[]{:S(2)}) copy-start(bf16[32,128,128]{2,1,0:T(8,128)(2,1)} %param.8) | copy-start | bytes 3145732
  12.5 34.0 %copy-start.3 = (f32[2,1,384,384]{3,2,1,0:T(8,128)S(1)}, f32[2,1,384,384]{3,2,1,0:T(8,128)}, u32[]{:S(2)}) copy-start(f32[2,1,384,384]{3,2,1,0:T(8,128)} %param.12) | copy-start | bytes 3538948
  12.5 28.8 %all-to-all-start = ((bf16[8,3,136,128]{3,2,1,0:T(8,128)(2,1)}), bf16[8,3,136,128]{3,2,1,0:T(8,128)(2,1)}, u32[]{:S(2)}, u32[]{:S(2)}) async-start(bf16[8,3,136,128]{3,2,1,0:T(8,128)(2,1)} %bitcast.13), calls=%async_computation | async-start | bytes 1671168 | tf_op jit(solution)/shard_map/all_to_all | solution.py:195
  41.3 44.1 %all-to-all-start.1 = ((bf16[8,3,136,128]{3,2,1,0:T(8,128)(2,1)}), bf16[8,3,136,128]{3,2,1,0:T(8,128)(2,1)}, u32[]{:S(2)}, u32[]{:S(2)}) async-start(bf16[8,3,136,128]{3,2,1,0:T(8,128)(2,1)} %bitcast.33), calls=%async_computation.1 | async-start | bytes 1671168 | tf_op jit(solution)/shard_map/all_to_all | solution.py:195
  82.7 2.7 %copy-start.4 = (bf16[2,1,384,384]{2,3,0,1:T(8,128)(2,1)}, bf16[2,1,384,384]{2,3,0,1:T(8,128)(2,1)S(1)}, u32[]{:S(2)}) copy-start(bf16[2,1,384,384]{2,3,0,1:T(8,128)(2,1)S(1)} %fusion.106) | copy-start | bytes 1769476
  82.7 2.0 %copy-start.2 = (f32[4,2,128,128]{3,2,1,0:T(8,128)S(1)}, f32[4,2,128,128]{3,2,1,0:T(8,128)}, u32[]{:S(2)}) copy-start(f32[4,2,128,128]{3,2,1,0:T(8,128)} %probe_ref.1) | copy-start | bytes 1572868
  82.7 9.8 %collective-permute-start = (bf16[2,1,384,384]{2,3,0,1:T(8,128)(2,1)S(1)}, bf16[2,1,384,384]{2,3,0,1:T(8,128)(2,1)}, u32[]{:S(2)}, u32[]{:S(2)}) collective-permute-start(bf16[2,1,384,384]{2,3,0,1:T(8,128)(2,1)S(1)} %fusion.106), channel_id=1, source_target_pairs={{0,1},{1,0},{2,3},{3,2},{4,5},{5,4},{6,7},{7,6},{8,9},{9,8},{10,11... | collective-permute-start | bytes 1769480 | tf_op jit(solution)/shard_map/ppermute | solution.py:231
  85.4 21.6 %all-to-all-start.2 = ((f32[32,1,4096]{2,1,0:T(1,128)}), f32[32,1,4096]{2,1,0:T(1,128)}, u32[]{:S(2)}, u32[]{:S(2)}) async-start(f32[32,1,4096]{2,1,0:T(1,128)} %bitcast.174), calls=%async_computation.2 | async-start | bytes 1048576 | tf_op jit(solution)/shard_map/all_to_all | solution.py:212
  93.9 19.1 %collective-permute-start.1 = (bf16[2,1,384,384]{2,3,0,1:T(8,128)(2,1)S(1)}, bf16[2,1,384,384]{2,3,0,1:T(8,128)(2,1)}, u32[]{:S(2)}, u32[]{:S(2)}) collective-permute-start(bf16[2,1,384,384]{2,3,0,1:T(8,128)(2,1)S(1)} %add_convert_fusion.1), channel_id=1, source_target_pairs={{0,2},{1,3},{2,0},{3,1},{4,6},{5,7},{6,4},{7,5},{8,10},{9,11},{10,... | collective-permute-start | bytes 1769480 | tf_op jit(solution)/shard_map/ppermute | solution.py:231
  109.6 18.9 %all-to-all-start.3 = ((f32[32,1,4096]{2,1,0:T(1,128)}), f32[32,1,4096]{2,1,0:T(1,128)}, u32[]{:S(2)}, u32[]{:S(2)}) async-start(f32[32,1,4096]{2,1,0:T(1,128)} %broadcast_in_dim.6), calls=%async_computation.3 | async-start | bytes 1048576 | tf_op jit(solution)/shard_map/all_to_all | solution.py:219
  156.2 18.9 %all-to-all-start.4 = ((f32[32,1,4096]{2,1,0:T(1,128)}), f32[32,1,4096]{2,1,0:T(1,128)}, u32[]{:S(2)}, u32[]{:S(2)}) async-start(f32[32,1,4096]{2,1,0:T(1,128)} %bitcast.175), calls=%async_computation.4 | async-start | bytes 1048576 | tf_op jit(solution)/shard_map/all_to_all | solution.py:212
  165.6 15.4 %copy-start.1 = (f32[4,2,128,128]{3,2,1,0:T(8,128)S(1)}, f32[4,2,128,128]{3,2,1,0:T(8,128)}, u32[]{:S(2)}) copy-start(f32[4,2,128,128]{3,2,1,0:T(8,128)} %add.206.probe_ref) | copy-start | bytes 1572868
  165.6 2.2 %collective-permute-start.2 = (bf16[2,1,384,384]{2,3,0,1:T(8,128)(2,1)}, bf16[2,1,384,384]{2,3,0,1:T(8,128)(2,1)S(1)}, u32[]{:S(2)}, u32[]{:S(2)}) collective-permute-start(bf16[2,1,384,384]{2,3,0,1:T(8,128)(2,1)} %fusion.113), channel_id=1, source_target_pairs={{0,1},{1,0},{2,3},{3,2},{4,5},{5,4},{6,7},{7,6},{8,9},{9,8},{10,11... | collective-permute-start | bytes 1769480 | tf_op jit(solution)/shard_map/ppermute | solution.py:231
  169.9 19.6 %collective-permute-start.3 = (bf16[2,1,384,384]{2,3,0,1:T(8,128)(2,1)}, bf16[2,1,384,384]{2,3,0,1:T(8,128)(2,1)}, u32[]{:S(2)}, u32[]{:S(2)}) collective-permute-start(bf16[2,1,384,384]{2,3,0,1:T(8,128)(2,1)} %add_convert_fusion), channel_id=1, source_target_pairs={{0,2},{1,3},{2,0},{3,1},{4,6},{5,7},{6,4},{7,5},{8,10},{9,11},{10,... | collective-permute-start | bytes 1769480 | tf_op jit(solution)/shard_map/ppermute | solution.py:231
  177.7 18.9 %all-to-all-start.5 = ((f32[32,1,4096]{2,1,0:T(1,128)}), f32[32,1,4096]{2,1,0:T(1,128)}, u32[]{:S(2)}, u32[]{:S(2)}) async-start(f32[32,1,4096]{2,1,0:T(1,128)} %broadcast_in_dim.8), calls=%async_computation.5 | async-start | bytes 1048576 | tf_op jit(solution)/shard_map/all_to_all | solution.py:219
where the time goes:
time: 200 us; the launch traced here: 199 us
  waiting for transfers between devices  52.5 us (26%)
  Pallas kernels  50.3 us (25%)
  starting transfers between devices  31.1 us (16%)
  matrix products  25.5 us (13%)
  other arithmetic  23.2 us (12%)
  local copies, waits for them, and re-layouts  15.7 us (8%)
    pallas_call x2, Pallas kernels, entries_kernel(): pl.pallas_call(entry_kernel, grid=(slots,), in_specs=[pl.BlockSpec((2, No...  50.3 us
    all_to_all x2, waiting for transfers between devices, exchange(): lax.all_to_all(payload, 'tile', 0, 0, tiled=True)  20.1 us
    all_to_all x2, waiting for transfers between devices, sum_over(): lax.all_to_all(value.astype(send_type).reshape(count, -1), axes, 0, 0, ti...  15 us
    all_to_all x2, starting transfers between devices, exchange(): lax.all_to_all(payload, 'tile', 0, 0, tiled=True)  11.6 us
    dot_general x2, matrix products, entries_pass(): jnp.einsum('skq,xskc->xqc', pick_rows, spread, preferred_element_type=jnp...  11.4 us
    ppermute x4, waiting for transfers between devices, all_sum_pairs(): other = lax.ppermute(total.astype(send_type), axis, pairs)  9.99 us
    all_to_all x2, starting transfers between devices, sum_over(): lax.all_to_all(value.astype(send_type).reshape(count, -1), axes, 0, 0, ti...  9.55 us
    dot_general x2, matrix products, entries_pass(): jnp.einsum('skq,xqc->xskc', pick_rows, stacked, preferred_element_type=jn...  8.14 us
  transfers between devices with their start and end apart: 10, of which 7 were waited for; matrix products, arithmetic and copies ran while one was open for 24% of the time, Pallas kernels for 13%

commit v1 on v0

--- a/solution.py
+++ b/solution.py
@@ -48,12 +48,24 @@
     return left, right
 
 
-def entry_kernel(patch_ref, amp_ref, probe_ref, left_ref, right_ref, update_ref, grad_ref):
-    modes, length = probe_ref.shape[0], probe_ref.shape[-1]
-
-    @pl.when(pl.program_id(0) == 0)
+def entry_kernel(valid_ref, patch_ref, amp_ref, probe_ref, left_ref, right_ref, update_ref, grad_ref):
+    slot = pl.program_id(0)
+
+    @pl.when(slot == 0)
     def _():
         grad_ref[...] = jnp.zeros(grad_ref.shape, grad_ref.dtype)
+
+    @pl.when(valid_ref[slot] == 0)
+    def _():
+        update_ref[...] = jnp.zeros(update_ref.shape, update_ref.dtype)
+
+    @pl.when(valid_ref[slot] != 0)
+    def _():
+        entry_body(patch_ref, amp_ref, probe_ref, left_ref, right_ref, update_ref, grad_ref)
+
+
+def entry_body(patch_ref, amp_ref, probe_ref, left_ref, right_ref, update_ref, grad_ref):
+    modes, length = probe_ref.shape[0], probe_ref.shape[-1]
 
     patch_re = patch_ref[0].astype(jnp.float32)
     patch_im = patch_ref[1].astype(jnp.float32)
@@ -128,24 +140,28 @@
     update_ref[1] = update_im.astype(update_ref.dtype)
 
 
-def entries_kernel(patch, amp_in, probe_now, left, right):
+def entries_kernel(valid, patch, amp_in, probe_now, left, right):
     slots, length = amp_in.shape[0], amp_in.shape[-1]
     modes = probe_now.shape[0]
     flops = slots * 4 * 2 * (2 * length) * (2 * length) * (modes * length)
+    grid_spec = pltpu.PrefetchScalarGridSpec(
+        num_scalar_prefetch=1,
+        grid=(slots,),
+        in_specs=[
+            pl.BlockSpec((2, None, length, length), lambda s, v: (0, s, 0, 0)),
+            pl.BlockSpec((None, length, length), lambda s, v: (s, 0, 0)),
+            pl.BlockSpec(probe_now.shape, lambda s, v: (0, 0, 0, 0)),
+            pl.BlockSpec(left.shape, lambda s, v: (0, 0)),
+            pl.BlockSpec(right.shape, lambda s, v: (0, 0)),
+        ],
+        out_specs=[
+            pl.BlockSpec((2, None, length, length), lambda s, v: (0, s, 0, 0)),
+            pl.BlockSpec(probe_now.shape, lambda s, v: (0, 0, 0, 0)),
+        ],
+    )
     return pl.pallas_call(
         entry_kernel,
-        grid=(slots,),
-        in_specs=[
-            pl.BlockSpec((2, None, length, length), lambda s: (0, s, 0, 0)),
-            pl.BlockSpec((None, length, length), lambda s: (s, 0, 0)),
-            pl.BlockSpec(probe_now.shape, lambda s: (0, 0, 0, 0)),
-            pl.BlockSpec(left.shape, lambda s: (0, 0)),
-            pl.BlockSpec(right.shape, lambda s: (0, 0)),
-        ],
-        out_specs=[
-            pl.BlockSpec((2, None, length, length), lambda s: (0, s, 0, 0)),
-            pl.BlockSpec(probe_now.shape, lambda s: (0, 0, 0, 0)),
-        ],
+        grid_spec=grid_spec,
         out_shape=[
             jax.ShapeDtypeStruct((2, slots, length, length), jnp.bfloat16),
             jax.ShapeDtypeStruct(probe_now.shape, jnp.float32),
@@ -156,7 +172,7 @@
             transcendentals=slots * length * length,
             bytes_accessed=slots * length * length * 10 + probe_now.size * 8,
         ),
-    )(patch, amp_in, probe_now, left, right)
+    )(valid, patch, amp_in, probe_now, left, right)
 
 
 def route(amplitudes, batch_ids, scan_tile, scan_offset, tiles_here):
@@ -254,7 +270,9 @@
     ).astype(jnp.bfloat16)
     patch = jnp.einsum("xskc,scl->xskl", rows, pick_cols, preferred_element_type=jnp.float32)
     left, right = block_tables(tables[0], tables[1])
-    update, probe_grad = entries_kernel(patch.astype(jnp.bfloat16), amp_in, probe_now, left, right)
+    update, probe_grad = entries_kernel(
+        valid, patch.astype(jnp.bfloat16), amp_in, probe_now, left, right
+    )
     spread = jnp.einsum(
         "xskl,scl->xskc", update, pick_cols, preferred_element_type=jnp.float32
     ).astype(jnp.bfloat16)

time: 200 us -> 201 us (level)
  starting transfers between devices: 31.1 us -> 40.9 us
  Pallas kernels: 50.3 us -> 42.5 us
    all_to_all x2, starting transfers between devices: 9.55 us -> 19.1 us  [sum_over(): lax.all_to_all(value.astype(send_type).reshape(count, -1), axes, 0, 0, ti...]
    pallas_call x2, Pallas kernels: 50.3 us -> 42.5 us  [entries_kernel(): pl.pallas_call(entry_kernel, grid_spec=grid_spec, out_shape=[jax.ShapeDty...]
    unnamed x13 -> x17, local copies, waits for them, and re-layouts: 4.69 us -> 4.7 us
  transfers between devices with their start and end apart: 10 -> 10, of which waited for: 7 -> 8; matrix products, arithmetic and copies ran while one was open for 24% -> 24% of each run, Pallas kernels for 13% -> 11%
where the time goes in v1:
time: 201 us; the launch traced here: 200 us
  waiting for transfers between devices  51.5 us (26%)
  Pallas kernels  42.5 us (21%)
  starting transfers between devices  40.9 us (20%)
  matrix products  25.5 us (13%)
  other arithmetic  23.5 us (12%)
  local copies, waits for them, and re-layouts  15 us (7%)
    pallas_call x2, Pallas kernels, entries_kernel(): pl.pallas_call(entry_kernel, grid_spec=grid_spec, out_shape=[jax.ShapeDty...  42.5 us
    all_to_all x2, waiting for transfers between devices, exchange(): lax.all_to_all(payload, 'tile', 0, 0, tiled=True)  20 us
    all_to_all x2, starting transfers between devices, sum_over(): lax.all_to_all(value.astype(send_type).reshape(count, -1), axes, 0, 0, ti...  19.1 us
    all_to_all x2, waiting for transfers between devices, sum_over(): lax.all_to_all(value.astype(send_type).reshape(count, -1), axes, 0, 0, ti...  14.3 us
    all_to_all x2, starting transfers between devices, exchange(): lax.all_to_all(payload, 'tile', 0, 0, tiled=True)  11.6 us
    dot_general x2, matrix products, entries_pass(): jnp.einsum('skq,xskc->xqc', pick_rows, spread, preferred_element_type=jnp...  11.4 us
    ppermute x4, waiting for transfers between devices, all_sum_pairs(): other = lax.ppermute(total.astype(send_type), axis, pairs)  10.1 us
    dot_general x2, matrix products, entries_pass(): jnp.einsum('skq,xqc->xskc', pick_rows, stacked, preferred_element_type=jn...  8.19 us
  transfers between devices with their start and end apart: 10, of which 8 were waited for; matrix products, arithmetic and copies ran while one was open for 24% of the time, Pallas kernels for 11%

profile of v1, /device:TPU:0, one launch (start us, length us, event | category | flops | bytes accessed | tf_op | source)
XLA Modules:
  0.0 199.8 jit_solution(13482355276417702057)
XLA Ops:
  11.7 7.4 %all-to-all-start = ((bf16[8,3,136,128]{3,2,1,0:T(8,128)(2,1)}), bf16[8,3,136,128]{3,2,1,0:T(8,128)(2,1)S(1)}, u32[]{:S(2)}, u32[]{:S(2)}) async-start(bf16[8,3,136,128]{3,2,1,0:T(8,128)(2,1)} %bitcast.13), calls=%async_computation | async-start | bytes 1671168 | tf_op jit(solution)/shard_map/all_to_all | solution.py:211
  20.4 20.0 %all-to-all-done = bf16[8,3,136,128]{3,2,1,0:T(8,128)(2,1)S(1)} async-done(((bf16[8,3,136,128]{3,2,1,0:T(8,128)(2,1)}), bf16[8,3,136,128]{3,2,1,0:T(8,128)(2,1)S(1)}, u32[]{:S(2)}, u32[]{:S(2)}) %all-to-all-start) | async-done | bytes 835616 | tf_op jit(solution)/shard_map/all_to_all | solution.py:211
  40.4 4.2 %all-to-all-start.1 = ((bf16[8,3,136,128]{3,2,1,0:T(8,128)(2,1)}), bf16[8,3,136,128]{3,2,1,0:T(8,128)(2,1)}, u32[]{:S(2)}, u32[]{:S(2)}) async-start(bf16[8,3,136,128]{3,2,1,0:T(8,128)(2,1)} %bitcast.33), calls=%async_computation.1 | async-start | bytes 1671168 | tf_op jit(solution)/shard_map/all_to_all | solution.py:211
  45.4 3.1 %convert_bitcast_fusion.1 = bf16[2,24,128,384]{3,2,0,1:T(8,128)(2,1)S(1)} fusion(s32[24,128]{1,0:T(8,128)S(1)} %get-tuple-element.42, pred[24]{0:T(512)(128)(4,1)S(1)} %broadcast_compare_fusion.1, f32[2,1,384,384]{3,2,1,0:T(8,128)S(1)} %copy-done.3), kind=kOutput, calls=%fused_computation.18 | convolution fusion | flops 1816952832 | bytes 5910552 | tf_op jit(solution)/shard_map/skq,xqc->xskc/dot_general | solution.py:268
  48.5 2.6 %fusion.73.patch_ref = bf16[2,24,128,128]{3,2,1,0:T(8,128)(2,1)} fusion(bf16[2,24,128,384]{3,2,0,1:T(8,128)(2,1)S(1)} %convert_bitcast_fusion.1, s32[24,128]{1,0:T(8,128)S(1)} %get-tuple-element.43), kind=kOutput, calls=%fused_computation.51 | convolution fusion | flops 605945856 | bytes 6303744 | tf_op jit(solution)/shard_map/xskc,scl->xskl/dot_general | solution.py:271
  51.1 21.2 %shard_map.77 = (bf16[2,24,128,128]{3,2,1,0:T(8,128)(2,1)}, f32[4,2,128,128]{3,2,1,0:T(8,128)}) custom-call(s32[24]{0:T(128)} %get-tuple-element.34.valid_ref, bf16[2,24,128,128]{3,2,1,0:T(8,128)(2,1)} %fusion.73.patch_ref, bf16[24,136,128]{2,1,0:T(8,128)(2,1)} %bitcast.179, f32[4,2,128,128]{3,2,1,0:T(8,128)} %probe_ref.1, ...), custom_call_target="tpu_custom_call" | custom-call | flops 6442450944 | bytes 4980736 | tf_op jit(solution)/shard_map/pallas_call | solution.py:162
  72.4 5.3 %fusion.106 = bf16[2,1,384,384]{2,3,0,1:T(8,128)(2,1)S(1)} fusion(s32[24,128]{1,0:T(8,128)S(1)} %get-tuple-element.42, pred[24]{0:T(512)(128)(4,1)S(1)} %broadcast_compare_fusion.1, bf16[2,24,128,128]{3,2,1,0:T(8,128)(2,1)} %get-tuple-element.9, s32[24,128]{1,0:T(8,128)S(1)} %get-tuple-element.43), kind=kOutput, calls=%fused_computation.56 | convolution fusion | flops 2422112256 | bytes 2187288 | tf_op jit(solution)/shard_map/skq,xskc->xqc/dot_general | solution.py:279
  77.8 1.9 copy.52
  80.4 11.1 %all-to-all-start.2 = ((f32[32,1,4096]{2,1,0:T(1,128)}), f32[32,1,4096]{2,1,0:T(1,128)}, u32[]{:S(2)}, u32[]{:S(2)}) async-start(f32[32,1,4096]{2,1,0:T(1,128)} %bitcast.180), calls=%async_computation.2 | async-start | bytes 1048576 | tf_op jit(solution)/shard_map/all_to_all | solution.py:228
  96.1 10.8 %all-to-all-done.2 = f32[32,1,4096]{2,1,0:T(1,128)} async-done(((f32[32,1,4096]{2,1,0:T(1,128)}), f32[32,1,4096]{2,1,0:T(1,128)}, u32[]{:S(2)}, u32[]{:S(2)}) %all-to-all-start.2) | async-done | bytes 524320 | tf_op jit(solution)/shard_map/all_to_all | solution.py:228
  109.6 3.3 %all-to-all-start.3 = ((f32[32,1,4096]{2,1,0:T(1,128)}), f32[32,1,4096]{2,1,0:T(1,128)}, u32[]{:S(2)}, u32[]{:S(2)}) async-start(f32[32,1,4096]{2,1,0:T(1,128)} %broadcast_in_dim.6), calls=%async_computation.3 | async-start | bytes 1048576 | tf_op jit(solution)/shard_map/all_to_all | solution.py:235
  113.2 5.1 %convert_bitcast_fusion = bf16[2,24,128,384]{2,3,0,1:T(8,128)(2,1)S(1)} fusion(s32[24,128]{1,0:T(8,128)S(1)} %iota_add_fusion, pred[24]{0:T(512)(128)(4,1)S(1)} %broadcast_compare_fusion, f32[2,1,384,384]{2,3,0,1:T(8,128)S(1)} %copy.52, bf16[2,1,384,384]{2,3,0,1:T(8,128)(2,1)} %collective-permute-done.1, ...), kind=kOutput, calls=%fused_computation.14 | convolution fusion | flops 1818427392 | bytes 7090204 | tf_op jit(solution)/shard_map/skq,xqc->xskc/dot_general | solution.py:268
  118.3 3.3 %fusion.68.patch_ref = bf16[2,24,128,128]{3,2,1,0:T(8,128)(2,1)} fusion(bf16[2,24,128,384]{2,3,0,1:T(8,128)(2,1)S(1)} %convert_bitcast_fusion, s32[24,128]{1,0:T(8,128)S(1)} %iota_add_fusion.1), kind=kOutput, calls=%fused_computation.50 | convolution fusion | flops 605945856 | bytes 6303744 | tf_op jit(solution)/shard_map/xskc,scl->xskl/dot_general | solution.py:271
  121.6 6.8 %all-to-all-done.3 = f32[32,1,4096]{2,1,0:T(1,128)} async-done(((f32[32,1,4096]{2,1,0:T(1,128)}), f32[32,1,4096]{2,1,0:T(1,128)}, u32[]{:S(2)}, u32[]{:S(2)}) %all-to-all-start.3) | async-done | bytes 524320 | tf_op jit(solution)/shard_map/all_to_all | solution.py:235
  131.0 21.3 %shard_map.78 = (bf16[2,24,128,128]{3,2,1,0:T(8,128)(2,1)}, f32[4,2,128,128]{3,2,1,0:T(8,128)}) custom-call(s32[24]{0:T(128)} %get-tuple-element.31.valid_ref, bf16[2,24,128,128]{3,2,1,0:T(8,128)(2,1)} %fusion.68.patch_ref, bf16[24,136,128]{2,1,0:T(8,128)(2,1)} %bitcast.34.amp_ref, f32[4,2,128,128]{3,2,1,0:T(8,128)} %add.206.probe_ref, ...), custom_call_target="tpu_custom_call" | custom-call | flops 6442450944 | bytes 4980736 | tf_op jit(solution)/shard_map/pallas_call | solution.py:162
  152.2 8.0 %all-to-all-start.4 = ((f32[32,1,4096]{2,1,0:T(1,128)}), f32[32,1,4096]{2,1,0:T(1,128)}, u32[]{:S(2)}, u32[]{:S(2)}) async-start(f32[32,1,4096]{2,1,0:T(1,128)} %bitcast.181), calls=%async_computation.4 | async-start | bytes 1048576 | tf_op jit(solution)/shard_map/all_to_all | solution.py:228
  160.2 6.1 %fusion.113 = bf16[2,1,384,384]{2,3,0,1:T(8,128)(2,1)} fusion(s32[24,128]{1,0:T(8,128)S(1)} %iota_add_fusion, pred[24]{0:T(512)(128)(4,1)S(1)} %broadcast_compare_fusion, bf16[2,24,128,128]{3,2,1,0:T(8,128)(2,1)} %get-tuple-element.11, s32[24,128]{1,0:T(8,128)S(1)} %iota_add_fusion.1), kind=kOutput, calls=%fused_computation.57 | convolution fusion | flops 2422112256 | bytes 2187288 | tf_op jit(solution)/shard_map/skq,xskc->xqc/dot_general | solution.py:279
  166.5 2.0 %collective-permute-done.2 = bf16[2,1,384,384]{2,3,0,1:T(8,128)(2,1)S(1)} collective-permute-done((bf16[2,1,384,384]{2,3,0,1:T(8,128)(2,1)}, bf16[2,1,384,384]{2,3,0,1:T(8,128)(2,1)S(1)}, u32[]{:S(2)}, u32[]{:S(2)}) %collective-permute-start.2) | collective-permute-done | bytes 589856 | tf_op jit(solution)/shard_map/ppermute | solution.py:247
  168.5 2.0 %add_convert_fusion = bf16[2,1,384,384]{2,3,0,1:T(8,128)(2,1)} fusion(bf16[2,1,384,384]{2,3,0,1:T(8,128)(2,1)S(1)} %collective-permute-done.2, bf16[2,1,384,384]{2,3,0,1:T(8,128)(2,1)} %fusion.113), kind=kLoop, calls=%fused_computation.59 | loop fusion | flops 1179648 | bytes 1769472 | tf_op jit(solution)/shard_map/convert_element_type | solution.py:248
  172.3 3.5 %all-to-all-done.4 = f32[32,1,4096]{2,1,0:T(1,128)} async-done(((f32[32,1,4096]{2,1,0:T(1,128)}), f32[32,1,4096]{2,1,0:T(1,128)}, u32[]{:S(2)}, u32[]{:S(2)}) %all-to-all-start.4) | async-done | bytes 524320 | tf_op jit(solution)/shard_map/all_to_all | solution.py:228
  178.4 3.3 %all-to-all-start.5 = ((f32[32,1,4096]{2,1,0:T(1,128)}), f32[32,1,4096]{2,1,0:T(1,128)}, u32[]{:S(2)}, u32[]{:S(2)}) async-start(f32[32,1,4096]{2,1,0:T(1,128)} %broadcast_in_dim.8), calls=%async_computation.5 | async-start | bytes 1048576 | tf_op jit(solution)/shard_map/all_to_all | solution.py:235
  182.4 7.8 %collective-permute-done.3 = bf16[2,1,384,384]{2,3,0,1:T(8,128)(2,1)} collective-permute-done((bf16[2,1,384,384]{2,3,0,1:T(8,128)(2,1)}, bf16[2,1,384,384]{2,3,0,1:T(8,128)(2,1)}, u32[]{:S(2)}, u32[]{:S(2)}) %collective-permute-start.3) | collective-permute-done | bytes 589856 | tf_op jit(solution)/shard_map/ppermute | solution.py:247
  190.2 4.1 %divide_add_fusion = f32[2,1,384,384]{2,3,0,1:T(8,128)} fusion(bf16[2,1,384,384]{2,3,0,1:T(8,128)(2,1)} %collective-permute-done.3, bf16[2,1,384,384]{2,3,0,1:T(8,128)(2,1)} %add_convert_fusion, f32[]{:T(128)} %reduce_max.19, f32[2,1,384,384]{2,3,0,1:T(8,128)S(1)} %copy.52, f32[]{:T(128)} %reduce_max.18, bf16[2,1,384,384]{2,3,0,1:T(8,128)(2,1)} %collective-permute-done.1, ...), kind=kLoop, calls=%fused_computation.58 | loop fusion | flops 2949120 | bytes 4718600 | tf_op jit(solution)/shard_map/add | solution.py:307
  194.3 2.7 %copy.59 = f32[2,1,384,384]{3,2,1,0:T(8,128)} copy(f32[2,1,384,384]{2,3,0,1:T(8,128)} %divide_add_fusion) | data formatting | bytes 2359296
  (78 shorter events, 31.9 us)
Async XLA Ops:
  0.6 8.8 %copy-start = (bf16[32,128,128]{2,1,0:T(8,128)(2,1)S(1)}, bf16[32,128,128]{2,1,0:T(8,128)(2,1)}, u32[]{:S(2)}) copy-start(bf16[32,128,128]{2,1,0:T(8,128)(2,1)} %param.8) | copy-start | bytes 3145732
  0.6 6.2 %copy-start.6 = (s32[2,12,2]{1,2,0:T(2,128)S(1)}, s32[2,12,2]{1,2,0:T(2,128)}, u32[]{:S(2)}) copy-start(s32[2,12,2]{1,2,0:T(2,128)} %param.11) | copy-start | bytes 580
  11.7 33.6 %copy-start.3 = (f32[2,1,384,384]{3,2,1,0:T(8,128)S(1)}, f32[2,1,384,384]{3,2,1,0:T(8,128)}, u32[]{:S(2)}) copy-start(f32[2,1,384,384]{3,2,1,0:T(8,128)} %param.12) | copy-start | bytes 3538948
  11.7 28.7 %all-to-all-start = ((bf16[8,3,136,128]{3,2,1,0:T(8,128)(2,1)}), bf16[8,3,136,128]{3,2,1,0:T(8,128)(2,1)S(1)}, u32[]{:S(2)}, u32[]{:S(2)}) async-start(bf16[8,3,136,128]{3,2,1,0:T(8,128)(2,1)} %bitcast.13), calls=%async_computation | async-start | bytes 1671168 | tf_op jit(solution)/shard_map/all_to_all | solution.py:211
  40.4 8.1 %copy-start.4 = (bf16[8,3,136,128]{3,2,1,0:T(8,128)(2,1)}, bf16[8,3,136,128]{3,2,1,0:T(8,128)(2,1)S(1)}, u32[]{:S(2)}) copy-start(bf16[8,3,136,128]{3,2,1,0:T(8,128)(2,1)S(1)} %all-to-all-done) | copy-start | bytes 2506756
  40.4 40.0 %all-to-all-start.1 = ((bf16[8,3,136,128]{3,2,1,0:T(8,128)(2,1)}), bf16[8,3,136,128]{3,2,1,0:T(8,128)(2,1)}, u32[]{:S(2)}, u32[]{:S(2)}) async-start(bf16[8,3,136,128]{3,2,1,0:T(8,128)(2,1)} %bitcast.33), calls=%async_computation.1 | async-start | bytes 1671168 | tf_op jit(solution)/shard_map/all_to_all | solution.py:211
  77.7 2.8 %copy-start.5 = (bf16[2,1,384,384]{2,3,0,1:T(8,128)(2,1)}, bf16[2,1,384,384]{2,3,0,1:T(8,128)(2,1)S(1)}, u32[]{:S(2)}) copy-start(bf16[2,1,384,384]{2,3,0,1:T(8,128)(2,1)S(1)} %fusion.106) | copy-start | bytes 1769476
  77.7 2.0 %copy-start.2 = (f32[4,2,128,128]{3,2,1,0:T(8,128)S(1)}, f32[4,2,128,128]{3,2,1,0:T(8,128)}, u32[]{:S(2)}) copy-start(f32[4,2,128,128]{3,2,1,0:T(8,128)} %probe_ref.1) | copy-start | bytes 1572868
  77.7 15.3 %collective-permute-start = (bf16[2,1,384,384]{2,3,0,1:T(8,128)(2,1)S(1)}, bf16[2,1,384,384]{2,3,0,1:T(8,128)(2,1)}, u32[]{:S(2)}, u32[]{:S(2)}) collective-permute-start(bf16[2,1,384,384]{2,3,0,1:T(8,128)(2,1)S(1)} %fusion.106), channel_id=1, source_target_pairs={{0,1},{1,0},{2,3},{3,2},{4,5},{5,4},{6,7},{7,6},{8,9},{9,8},{10,11... | collective-permute-start | bytes 1769480 | tf_op jit(solution)/shard_map/ppermute | solution.py:247
  80.4 26.5 %all-to-all-start.2 = ((f32[32,1,4096]{2,1,0:T(1,128)}), f32[32,1,4096]{2,1,0:T(1,128)}, u32[]{:S(2)}, u32[]{:S(2)}) async-start(f32[32,1,4096]{2,1,0:T(1,128)} %bitcast.180), calls=%async_computation.2 | async-start | bytes 1048576 | tf_op jit(solution)/shard_map/all_to_all | solution.py:228
  94.4 18.9 %collective-permute-start.1 = (bf16[2,1,384,384]{2,3,0,1:T(8,128)(2,1)S(1)}, bf16[2,1,384,384]{2,3,0,1:T(8,128)(2,1)}, u32[]{:S(2)}, u32[]{:S(2)}) collective-permute-start(bf16[2,1,384,384]{2,3,0,1:T(8,128)(2,1)S(1)} %add_convert_fusion.1), channel_id=1, source_target_pairs={{0,2},{1,3},{2,0},{3,1},{4,6},{5,7},{6,4},{7,5},{8,10},{9,11},{10,... | collective-permute-start | bytes 1769480 | tf_op jit(solution)/shard_map/ppermute | solution.py:247
  109.6 18.9 %all-to-all-start.3 = ((f32[32,1,4096]{2,1,0:T(1,128)}), f32[32,1,4096]{2,1,0:T(1,128)}, u32[]{:S(2)}, u32[]{:S(2)}) async-start(f32[32,1,4096]{2,1,0:T(1,128)} %broadcast_in_dim.6), calls=%async_computation.3 | async-start | bytes 1048576 | tf_op jit(solution)/shard_map/all_to_all | solution.py:235
  152.2 23.5 %all-to-all-start.4 = ((f32[32,1,4096]{2,1,0:T(1,128)}), f32[32,1,4096]{2,1,0:T(1,128)}, u32[]{:S(2)}, u32[]{:S(2)}) async-start(f32[32,1,4096]{2,1,0:T(1,128)} %bitcast.181), calls=%async_computation.4 | async-start | bytes 1048576 | tf_op jit(solution)/shard_map/all_to_all | solution.py:228
  166.3 15.4 %copy-start.1 = (f32[4,2,128,128]{3,2,1,0:T(8,128)S(1)}, f32[4,2,128,128]{3,2,1,0:T(8,128)}, u32[]{:S(2)}) copy-start(f32[4,2,128,128]{3,2,1,0:T(8,128)} %add.206.probe_ref) | copy-start | bytes 1572868
  166.3 2.2 %collective-permute-start.2 = (bf16[2,1,384,384]{2,3,0,1:T(8,128)(2,1)}, bf16[2,1,384,384]{2,3,0,1:T(8,128)(2,1)S(1)}, u32[]{:S(2)}, u32[]{:S(2)}) collective-permute-start(bf16[2,1,384,384]{2,3,0,1:T(8,128)(2,1)} %fusion.113), channel_id=1, source_target_pairs={{0,1},{1,0},{2,3},{3,2},{4,5},{5,4},{6,7},{7,6},{8,9},{9,8},{10,11... | collective-permute-start | bytes 1769480 | tf_op jit(solution)/shard_map/ppermute | solution.py:247
  170.6 19.6 %collective-permute-start.3 = (bf16[2,1,384,384]{2,3,0,1:T(8,128)(2,1)}, bf16[2,1,384,384]{2,3,0,1:T(8,128)(2,1)}, u32[]{:S(2)}, u32[]{:S(2)}) collective-permute-start(bf16[2,1,384,384]{2,3,0,1:T(8,128)(2,1)} %add_convert_fusion), channel_id=1, source_target_pairs={{0,2},{1,3},{2,0},{3,1},{4,6},{5,7},{6,4},{7,5},{8,10},{9,11},{10,... | collective-permute-start | bytes 1769480 | tf_op jit(solution)/shard_map/ppermute | solution.py:247
  178.4 18.9 %all-to-all-start.5 = ((f32[32,1,4096]{2,1,0:T(1,128)}), f32[32,1,4096]{2,1,0:T(1,128)}, u32[]{:S(2)}, u32[]{:S(2)}) async-start(f32[32,1,4096]{2,1,0:T(1,128)} %broadcast_in_dim.8), calls=%async_computation.5 | async-start | bytes 1048576 | tf_op jit(solution)/shard_map/all_to_all | solution.py:235

commit v2 on v1

--- a/solution.py
+++ b/solution.py
@@ -49,26 +49,27 @@
 
 
 def entry_kernel(valid_ref, patch_ref, amp_ref, probe_ref, left_ref, right_ref, update_ref, grad_ref):
-    slot = pl.program_id(0)
-
-    @pl.when(slot == 0)
-    def _():
-        grad_ref[...] = jnp.zeros(grad_ref.shape, grad_ref.dtype)
-
-    @pl.when(valid_ref[slot] == 0)
-    def _():
-        update_ref[...] = jnp.zeros(update_ref.shape, update_ref.dtype)
-
-    @pl.when(valid_ref[slot] != 0)
-    def _():
-        entry_body(patch_ref, amp_ref, probe_ref, left_ref, right_ref, update_ref, grad_ref)
-
-
-def entry_body(patch_ref, amp_ref, probe_ref, left_ref, right_ref, update_ref, grad_ref):
+    grad_ref[...] = jnp.zeros(grad_ref.shape, grad_ref.dtype)
+
+    def one_slot(slot, carry):
+        @pl.when(valid_ref[slot] == 0)
+        def _():
+            update_ref[:, slot] = jnp.zeros((2,) + update_ref.shape[2:], update_ref.dtype)
+
+        @pl.when(valid_ref[slot] != 0)
+        def _():
+            entry_body(slot, patch_ref, amp_ref, probe_ref, left_ref, right_ref, update_ref, grad_ref)
+
+        return carry
+
+    lax.fori_loop(0, valid_ref.shape[0], one_slot, 0)
+
+
+def entry_body(slot, patch_ref, amp_ref, probe_ref, left_ref, right_ref, update_ref, grad_ref):
     modes, length = probe_ref.shape[0], probe_ref.shape[-1]
 
-    patch_re = patch_ref[0].astype(jnp.float32)
-    patch_im = patch_ref[1].astype(jnp.float32)
+    patch_re = patch_ref[0, slot].astype(jnp.float32)
+    patch_im = patch_ref[1, slot].astype(jnp.float32)
     left = left_ref[...]
     right = right_ref[...]
     exits_re, exits_im = [], []
@@ -116,7 +117,7 @@
         far_re = far[m * length : (m + 1) * length, :length]
         far_im = far[m * length : (m + 1) * length, length:]
         intensity = intensity + (far_re * far_re + far_im * far_im)
-    measured = amp_ref[...].astype(jnp.float32)
+    measured = amp_ref[slot, :length, :].astype(jnp.float32)
     factor = measured / jnp.sqrt(jnp.maximum(intensity, 1.0)) - 1.0
     factor = jnp.concatenate([factor, factor], 1)
     factor = jnp.concatenate([factor] * modes, 0)
@@ -136,28 +137,20 @@
         update_im = update_im + (probe_re * change_im - probe_im * change_re)
         grad_ref[m, 0] += patch_re * change_re + patch_im * change_im
         grad_ref[m, 1] += patch_re * change_im - patch_im * change_re
-    update_ref[0] = update_re.astype(update_ref.dtype)
-    update_ref[1] = update_im.astype(update_ref.dtype)
+    update_ref[0, slot] = update_re.astype(update_ref.dtype)
+    update_ref[1, slot] = update_im.astype(update_ref.dtype)
 
 
 def entries_kernel(valid, patch, amp_in, probe_now, left, right):
     slots, length = amp_in.shape[0], amp_in.shape[-1]
     modes = probe_now.shape[0]
     flops = slots * 4 * 2 * (2 * length) * (2 * length) * (modes * length)
+    whole = pl.BlockSpec(memory_space=pltpu.VMEM)
     grid_spec = pltpu.PrefetchScalarGridSpec(
         num_scalar_prefetch=1,
-        grid=(slots,),
-        in_specs=[
-            pl.BlockSpec((2, None, length, length), lambda s, v: (0, s, 0, 0)),
-            pl.BlockSpec((None, length, length), lambda s, v: (s, 0, 0)),
-            pl.BlockSpec(probe_now.shape, lambda s, v: (0, 0, 0, 0)),
-            pl.BlockSpec(left.shape, lambda s, v: (0, 0)),
-            pl.BlockSpec(right.shape, lambda s, v: (0, 0)),
-        ],
-        out_specs=[
-            pl.BlockSpec((2, None, length, length), lambda s, v: (0, s, 0, 0)),
-            pl.BlockSpec(probe_now.shape, lambda s, v: (0, 0, 0, 0)),
-        ],
+        grid=(1,),
+        in_specs=[whole] * 5,
+        out_specs=[whole] * 2,
     )
     return pl.pallas_call(
         entry_kernel,

time: 201 us -> 198 us (0.985)
  Pallas kernels: 42.5 us -> 23.5 us
  starting transfers between devices: 40.9 us -> 56.1 us
    pallas_call x2, Pallas kernels: 42.5 us -> 23.5 us  [entries_kernel(): pl.pallas_call(entry_kernel, grid_spec=grid_spec, out_shape=[jax.ShapeDty...]
    all_to_all x2, starting transfers between devices: 19.1 us -> 34.3 us  [sum_over(): lax.all_to_all(value.astype(send_type).reshape(count, -1), axes, 0, 0, ti...]
  transfers between devices with their start and end apart: 10 -> 10, of which waited for: 8 -> 8; matrix products, arithmetic and copies ran while one was open for 24% -> 24% of each run, Pallas kernels for 11% -> 6%
where the time goes in v2:
time: 198 us; the launch traced here: 196 us
  starting transfers between devices  56.1 us (28%)
  waiting for transfers between devices  51.5 us (26%)
  matrix products  25.6 us (13%)
  other arithmetic  23.5 us (12%)
  Pallas kernels  23.5 us (12%)
  local copies, waits for them, and re-layouts  15 us (8%)
    all_to_all x2, starting transfers between devices, sum_over(): lax.all_to_all(value.astype(send_type).reshape(count, -1), axes, 0, 0, ti...  34.3 us
    pallas_call x2, Pallas kernels, entries_kernel(): pl.pallas_call(entry_kernel, grid_spec=grid_spec, out_shape=[jax.ShapeDty...  23.5 us
    all_to_all x2, waiting for transfers between devices, exchange(): lax.all_to_all(payload, 'tile', 0, 0, tiled=True)  20 us
    all_to_all x2, waiting for transfers between devices, sum_over(): lax.all_to_all(value.astype(send_type).reshape(count, -1), axes, 0, 0, ti...  14.3 us
    all_to_all x2, starting transfers between devices, exchange(): lax.all_to_all(payload, 'tile', 0, 0, tiled=True)  11.6 us
    dot_general x2, matrix products, entries_pass(): jnp.einsum('skq,xskc->xqc', pick_rows, spread, preferred_element_type=jnp...  11.4 us
    ppermute x4, waiting for transfers between devices, all_sum_pairs(): other = lax.ppermute(total.astype(send_type), axis, pairs)  10.1 us
    dot_general x2, matrix products, entries_pass(): jnp.einsum('skq,xqc->xskc', pick_rows, stacked, preferred_element_type=jn...  8.21 us
  transfers between devices with their start and end apart: 10, of which 8 were waited for; matrix products, arithmetic and copies ran while one was open for 24% of the time, Pallas kernels for 6%

profile of v2, /device:TPU:0, one launch (start us, length us, event | category | flops | bytes accessed | tf_op | source)
XLA Modules:
  0.0 196.0 jit_solution(1645443232254426758)
XLA Ops:
  11.7 7.4 %all-to-all-start = ((bf16[8,3,136,128]{3,2,1,0:T(8,128)(2,1)}), bf16[8,3,136,128]{3,2,1,0:T(8,128)(2,1)S(1)}, u32[]{:S(2)}, u32[]{:S(2)}) async-start(bf16[8,3,136,128]{3,2,1,0:T(8,128)(2,1)} %bitcast.13), calls=%async_computation | async-start | bytes 1671168 | tf_op jit(solution)/shard_map/all_to_all | solution.py:204
  20.4 20.0 %all-to-all-done = bf16[8,3,136,128]{3,2,1,0:T(8,128)(2,1)S(1)} async-done(((bf16[8,3,136,128]{3,2,1,0:T(8,128)(2,1)}), bf16[8,3,136,128]{3,2,1,0:T(8,128)(2,1)S(1)}, u32[]{:S(2)}, u32[]{:S(2)}) %all-to-all-start) | async-done | bytes 835616 | tf_op jit(solution)/shard_map/all_to_all | solution.py:204
  40.4 4.2 %all-to-all-start.1 = ((bf16[8,3,136,128]{3,2,1,0:T(8,128)(2,1)}), bf16[8,3,136,128]{3,2,1,0:T(8,128)(2,1)}, u32[]{:S(2)}, u32[]{:S(2)}) async-start(bf16[8,3,136,128]{3,2,1,0:T(8,128)(2,1)} %bitcast.33), calls=%async_computation.1 | async-start | bytes 1671168 | tf_op jit(solution)/shard_map/all_to_all | solution.py:204
  45.4 3.1 %convert_bitcast_fusion.1 = bf16[2,24,128,384]{3,2,0,1:T(8,128)(2,1)S(1)} fusion(s32[24,128]{1,0:T(8,128)S(1)} %get-tuple-element.42, pred[24]{0:T(512)(128)(4,1)S(1)} %broadcast_compare_fusion.1, f32[2,1,384,384]{3,2,1,0:T(8,128)S(1)} %copy-done.3), kind=kOutput, calls=%fused_computation.18 | convolution fusion | flops 1816952832 | bytes 5910552 | tf_op jit(solution)/shard_map/skq,xqc->xskc/dot_general | solution.py:261
  48.5 2.6 %fusion.73.patch_ref = bf16[2,24,128,128]{3,2,1,0:T(8,128)(2,1)} fusion(bf16[2,24,128,384]{3,2,0,1:T(8,128)(2,1)S(1)} %convert_bitcast_fusion.1, s32[24,128]{1,0:T(8,128)S(1)} %get-tuple-element.43), kind=kOutput, calls=%fused_computation.51 | convolution fusion | flops 605945856 | bytes 6303744 | tf_op jit(solution)/shard_map/xskc,scl->xskl/dot_general | solution.py:264
  51.1 11.7 %shard_map.77 = (bf16[2,24,128,128]{3,2,1,0:T(8,128)(2,1)}, f32[4,2,128,128]{3,2,1,0:T(8,128)}) custom-call(s32[24]{0:T(128)} %get-tuple-element.34.valid_ref, bf16[2,24,128,128]{3,2,1,0:T(8,128)(2,1)} %fusion.73.patch_ref, bf16[24,136,128]{2,1,0:T(8,128)(2,1)} %bitcast.179, f32[4,2,128,128]{3,2,1,0:T(8,128)} %probe_ref.1, ...), custom_call_target="tpu_custom_call" | custom-call | flops 6442450944 | bytes 4980736 | tf_op jit(solution)/shard_map/pallas_call | solution.py:155
  62.8 5.3 %fusion.106 = bf16[2,1,384,384]{2,3,0,1:T(8,128)(2,1)S(1)} fusion(s32[24,128]{1,0:T(8,128)S(1)} %get-tuple-element.42, pred[24]{0:T(512)(128)(4,1)S(1)} %broadcast_compare_fusion.1, bf16[2,24,128,128]{3,2,1,0:T(8,128)(2,1)} %get-tuple-element.9, s32[24,128]{1,0:T(8,128)S(1)} %get-tuple-element.43), kind=kOutput, calls=%fused_computation.56 | convolution fusion | flops 2422112256 | bytes 2187288 | tf_op jit(solution)/shard_map/skq,xskc->xqc/dot_general | solution.py:272
  68.3 1.9 copy.52
  70.9 18.0 %all-to-all-start.2 = ((f32[32,1,4096]{2,1,0:T(1,128)}), f32[32,1,4096]{2,1,0:T(1,128)}, u32[]{:S(2)}, u32[]{:S(2)}) async-start(f32[32,1,4096]{2,1,0:T(1,128)} %bitcast.180), calls=%async_computation.2 | async-start | bytes 1048576 | tf_op jit(solution)/shard_map/all_to_all | solution.py:221
  93.5 10.8 %all-to-all-done.2 = f32[32,1,4096]{2,1,0:T(1,128)} async-done(((f32[32,1,4096]{2,1,0:T(1,128)}), f32[32,1,4096]{2,1,0:T(1,128)}, u32[]{:S(2)}, u32[]{:S(2)}) %all-to-all-start.2) | async-done | bytes 524320 | tf_op jit(solution)/shard_map/all_to_all | solution.py:221
  107.0 3.3 %all-to-all-start.3 = ((f32[32,1,4096]{2,1,0:T(1,128)}), f32[32,1,4096]{2,1,0:T(1,128)}, u32[]{:S(2)}, u32[]{:S(2)}) async-start(f32[32,1,4096]{2,1,0:T(1,128)} %broadcast_in_dim.6), calls=%async_computation.3 | async-start | bytes 1048576 | tf_op jit(solution)/shard_map/all_to_all | solution.py:228
  110.6 5.1 %convert_bitcast_fusion = bf16[2,24,128,384]{2,3,0,1:T(8,128)(2,1)S(1)} fusion(s32[24,128]{1,0:T(8,128)S(1)} %iota_add_fusion, pred[24]{0:T(512)(128)(4,1)S(1)} %broadcast_compare_fusion, f32[2,1,384,384]{2,3,0,1:T(8,128)S(1)} %copy.52, bf16[2,1,384,384]{2,3,0,1:T(8,128)(2,1)} %collective-permute-done.1, ...), kind=kOutput, calls=%fused_computation.14 | convolution fusion | flops 1818427392 | bytes 7090204 | tf_op jit(solution)/shard_map/skq,xqc->xskc/dot_general | solution.py:261
  115.8 3.3 %fusion.68.patch_ref = bf16[2,24,128,128]{3,2,1,0:T(8,128)(2,1)} fusion(bf16[2,24,128,384]{2,3,0,1:T(8,128)(2,1)S(1)} %convert_bitcast_fusion, s32[24,128]{1,0:T(8,128)S(1)} %iota_add_fusion.1), kind=kOutput, calls=%fused_computation.50 | convolution fusion | flops 605945856 | bytes 6303744 | tf_op jit(solution)/shard_map/xskc,scl->xskl/dot_general | solution.py:264
  119.0 6.8 %all-to-all-done.3 = f32[32,1,4096]{2,1,0:T(1,128)} async-done(((f32[32,1,4096]{2,1,0:T(1,128)}), f32[32,1,4096]{2,1,0:T(1,128)}, u32[]{:S(2)}, u32[]{:S(2)}) %all-to-all-start.3) | async-done | bytes 524320 | tf_op jit(solution)/shard_map/all_to_all | solution.py:228
  128.4 11.8 %shard_map.78 = (bf16[2,24,128,128]{3,2,1,0:T(8,128)(2,1)}, f32[4,2,128,128]{3,2,1,0:T(8,128)}) custom-call(s32[24]{0:T(128)} %get-tuple-element.31.valid_ref, bf16[2,24,128,128]{3,2,1,0:T(8,128)(2,1)} %fusion.68.patch_ref, bf16[24,136,128]{2,1,0:T(8,128)(2,1)} %bitcast.34.amp_ref, f32[4,2,128,128]{3,2,1,0:T(8,128)} %add.206.probe_ref, ...), custom_call_target="tpu_custom_call" | custom-call | flops 6442450944 | bytes 4980736 | tf_op jit(solution)/shard_map/pallas_call | solution.py:155
  140.1 16.3 %all-to-all-start.4 = ((f32[32,1,4096]{2,1,0:T(1,128)}), f32[32,1,4096]{2,1,0:T(1,128)}, u32[]{:S(2)}, u32[]{:S(2)}) async-start(f32[32,1,4096]{2,1,0:T(1,128)} %bitcast.181), calls=%async_computation.4 | async-start | bytes 1048576 | tf_op jit(solution)/shard_map/all_to_all | solution.py:221
  156.4 6.1 %fusion.113 = bf16[2,1,384,384]{2,3,0,1:T(8,128)(2,1)} fusion(s32[24,128]{1,0:T(8,128)S(1)} %iota_add_fusion, pred[24]{0:T(512)(128)(4,1)S(1)} %broadcast_compare_fusion, bf16[2,24,128,128]{3,2,1,0:T(8,128)(2,1)} %get-tuple-element.11, s32[24,128]{1,0:T(8,128)S(1)} %iota_add_fusion.1), kind=kOutput, calls=%fused_computation.57 | convolution fusion | flops 2422112256 | bytes 2187288 | tf_op jit(solution)/shard_map/skq,xskc->xqc/dot_general | solution.py:272
  162.7 2.0 %collective-permute-done.2 = bf16[2,1,384,384]{2,3,0,1:T(8,128)(2,1)S(1)} collective-permute-done((bf16[2,1,384,384]{2,3,0,1:T(8,128)(2,1)}, bf16[2,1,384,384]{2,3,0,1:T(8,128)(2,1)S(1)}, u32[]{:S(2)}, u32[]{:S(2)}) %collective-permute-start.2) | collective-permute-done | bytes 589856 | tf_op jit(solution)/shard_map/ppermute | solution.py:240
  164.7 2.0 %add_convert_fusion = bf16[2,1,384,384]{2,3,0,1:T(8,128)(2,1)} fusion(bf16[2,1,384,384]{2,3,0,1:T(8,128)(2,1)S(1)} %collective-permute-done.2, bf16[2,1,384,384]{2,3,0,1:T(8,128)(2,1)} %fusion.113), kind=kLoop, calls=%fused_computation.59 | loop fusion | flops 1179648 | bytes 1769472 | tf_op jit(solution)/shard_map/convert_element_type | solution.py:241
  168.4 3.5 %all-to-all-done.4 = f32[32,1,4096]{2,1,0:T(1,128)} async-done(((f32[32,1,4096]{2,1,0:T(1,128)}), f32[32,1,4096]{2,1,0:T(1,128)}, u32[]{:S(2)}, u32[]{:S(2)}) %all-to-all-start.4) | async-done | bytes 524320 | tf_op jit(solution)/shard_map/all_to_all | solution.py:221
  174.6 3.3 %all-to-all-start.5 = ((f32[32,1,4096]{2,1,0:T(1,128)}), f32[32,1,4096]{2,1,0:T(1,128)}, u32[]{:S(2)}, u32[]{:S(2)}) async-start(f32[32,1,4096]{2,1,0:T(1,128)} %broadcast_in_dim.8), calls=%async_computation.5 | async-start | bytes 1048576 | tf_op jit(solution)/shard_map/all_to_all | solution.py:228
  178.6 7.8 %collective-permute-done.3 = bf16[2,1,384,384]{2,3,0,1:T(8,128)(2,1)} collective-permute-done((bf16[2,1,384,384]{2,3,0,1:T(8,128)(2,1)}, bf16[2,1,384,384]{2,3,0,1:T(8,128)(2,1)}, u32[]{:S(2)}, u32[]{:S(2)}) %collective-permute-start.3) | collective-permute-done | bytes 589856 | tf_op jit(solution)/shard_map/ppermute | solution.py:240
  186.4 4.1 %divide_add_fusion = f32[2,1,384,384]{2,3,0,1:T(8,128)} fusion(bf16[2,1,384,384]{2,3,0,1:T(8,128)(2,1)} %collective-permute-done.3, bf16[2,1,384,384]{2,3,0,1:T(8,128)(2,1)} %add_convert_fusion, f32[]{:T(128)} %reduce_max.19, f32[2,1,384,384]{2,3,0,1:T(8,128)S(1)} %copy.52, f32[]{:T(128)} %reduce_max.18, bf16[2,1,384,384]{2,3,0,1:T(8,128)(2,1)} %collective-permute-done.1, ...), kind=kLoop, calls=%fused_computation.58 | loop fusion | flops 2949120 | bytes 4718600 | tf_op jit(solution)/shard_map/add | solution.py:300
  190.5 2.7 %copy.59 = f32[2,1,384,384]{3,2,1,0:T(8,128)} copy(f32[2,1,384,384]{2,3,0,1:T(8,128)} %divide_add_fusion) | data formatting | bytes 2359296
  (78 shorter events, 31.9 us)
Async XLA Ops:
  0.6 8.8 %copy-start = (bf16[32,128,128]{2,1,0:T(8,128)(2,1)S(1)}, bf16[32,128,128]{2,1,0:T(8,128)(2,1)}, u32[]{:S(2)}) copy-start(bf16[32,128,128]{2,1,0:T(8,128)(2,1)} %param.8) | copy-start | bytes 3145732
  0.6 6.2 %copy-start.6 = (s32[2,12,2]{1,2,0:T(2,128)S(1)}, s32[2,12,2]{1,2,0:T(2,128)}, u32[]{:S(2)}) copy-start(s32[2,12,2]{1,2,0:T(2,128)} %param.11) | copy-start | bytes 580
  11.7 33.6 %copy-start.3 = (f32[2,1,384,384]{3,2,1,0:T(8,128)S(1)}, f32[2,1,384,384]{3,2,1,0:T(8,128)}, u32[]{:S(2)}) copy-start(f32[2,1,384,384]{3,2,1,0:T(8,128)} %param.12) | copy-start | bytes 3538948
  11.7 28.7 %all-to-all-start = ((bf16[8,3,136,128]{3,2,1,0:T(8,128)(2,1)}), bf16[8,3,136,128]{3,2,1,0:T(8,128)(2,1)S(1)}, u32[]{:S(2)}, u32[]{:S(2)}) async-start(bf16[8,3,136,128]{3,2,1,0:T(8,128)(2,1)} %bitcast.13), calls=%async_computation | async-start | bytes 1671168 | tf_op jit(solution)/shard_map/all_to_all | solution.py:204
  40.4 8.1 %copy-start.4 = (bf16[8,3,136,128]{3,2,1,0:T(8,128)(2,1)}, bf16[8,3,136,128]{3,2,1,0:T(8,128)(2,1)S(1)}, u32[]{:S(2)}) copy-start(bf16[8,3,136,128]{3,2,1,0:T(8,128)(2,1)S(1)} %all-to-all-done) | copy-start | bytes 2506756
  40.4 30.5 %all-to-all-start.1 = ((bf16[8,3,136,128]{3,2,1,0:T(8,128)(2,1)}), bf16[8,3,136,128]{3,2,1,0:T(8,128)(2,1)}, u32[]{:S(2)}, u32[]{:S(2)}) async-start(bf16[8,3,136,128]{3,2,1,0:T(8,128)(2,1)} %bitcast.33), calls=%async_computation.1 | async-start | bytes 1671168 | tf_op jit(solution)/shard_map/all_to_all | solution.py:204
  68.2 2.8 %copy-start.5 = (bf16[2,1,384,384]{2,3,0,1:T(8,128)(2,1)}, bf16[2,1,384,384]{2,3,0,1:T(8,128)(2,1)S(1)}, u32[]{:S(2)}) copy-start(bf16[2,1,384,384]{2,3,0,1:T(8,128)(2,1)S(1)} %fusion.106) | copy-start | bytes 1769476
  68.2 2.0 %copy-start.2 = (f32[4,2,128,128]{3,2,1,0:T(8,128)S(1)}, f32[4,2,128,128]{3,2,1,0:T(8,128)}, u32[]{:S(2)}) copy-start(f32[4,2,128,128]{3,2,1,0:T(8,128)} %probe_ref.1) | copy-start | bytes 1572868
  68.2 22.2 %collective-permute-start = (bf16[2,1,384,384]{2,3,0,1:T(8,128)(2,1)S(1)}, bf16[2,1,384,384]{2,3,0,1:T(8,128)(2,1)}, u32[]{:S(2)}, u32[]{:S(2)}) collective-permute-start(bf16[2,1,384,384]{2,3,0,1:T(8,128)(2,1)S(1)} %fusion.106), channel_id=1, source_target_pairs={{0,1},{1,0},{2,3},{3,2},{4,5},{5,4},{6,7},{7,6},{8,9},{9,8},{10,11... | collective-permute-start | bytes 1769480 | tf_op jit(solution)/shard_map/ppermute | solution.py:240
  70.9 33.4 %all-to-all-start.2 = ((f32[32,1,4096]{2,1,0:T(1,128)}), f32[32,1,4096]{2,1,0:T(1,128)}, u32[]{:S(2)}, u32[]{:S(2)}) async-start(f32[32,1,4096]{2,1,0:T(1,128)} %bitcast.180), calls=%async_computation.2 | async-start | bytes 1048576 | tf_op jit(solution)/shard_map/all_to_all | solution.py:221
  91.7 18.9 %collective-permute-start.1 = (bf16[2,1,384,384]{2,3,0,1:T(8,128)(2,1)S(1)}, bf16[2,1,384,384]{2,3,0,1:T(8,128)(2,1)}, u32[]{:S(2)}, u32[]{:S(2)}) collective-permute-start(bf16[2,1,384,384]{2,3,0,1:T(8,128)(2,1)S(1)} %add_convert_fusion.1), channel_id=1, source_target_pairs={{0,2},{1,3},{2,0},{3,1},{4,6},{5,7},{6,4},{7,5},{8,10},{9,11},{10,... | collective-permute-start | bytes 1769480 | tf_op jit(solution)/shard_map/ppermute | solution.py:240
  107.0 18.9 %all-to-all-start.3 = ((f32[32,1,4096]{2,1,0:T(1,128)}), f32[32,1,4096]{2,1,0:T(1,128)}, u32[]{:S(2)}, u32[]{:S(2)}) async-start(f32[32,1,4096]{2,1,0:T(1,128)} %broadcast_in_dim.6), calls=%async_computation.3 | async-start | bytes 1048576 | tf_op jit(solution)/shard_map/all_to_all | solution.py:228
  140.1 31.8 %all-to-all-start.4 = ((f32[32,1,4096]{2,1,0:T(1,128)}), f32[32,1,4096]{2,1,0:T(1,128)}, u32[]{:S(2)}, u32[]{:S(2)}) async-start(f32[32,1,4096]{2,1,0:T(1,128)} %bitcast.181), calls=%async_computation.4 | async-start | bytes 1048576 | tf_op jit(solution)/shard_map/all_to_all | solution.py:221
  162.5 15.4 %copy-start.1 = (f32[4,2,128,128]{3,2,1,0:T(8,128)S(1)}, f32[4,2,128,128]{3,2,1,0:T(8,128)}, u32[]{:S(2)}) copy-start(f32[4,2,128,128]{3,2,1,0:T(8,128)} %add.206.probe_ref) | copy-start | bytes 1572868
  162.5 2.2 %collective-permute-start.2 = (bf16[2,1,384,384]{2,3,0,1:T(8,128)(2,1)}, bf16[2,1,384,384]{2,3,0,1:T(8,128)(2,1)S(1)}, u32[]{:S(2)}, u32[]{:S(2)}) collective-permute-start(bf16[2,1,384,384]{2,3,0,1:T(8,128)(2,1)} %fusion.113), channel_id=1, source_target_pairs={{0,1},{1,0},{2,3},{3,2},{4,5},{5,4},{6,7},{7,6},{8,9},{9,8},{10,11... | collective-permute-start | bytes 1769480 | tf_op jit(solution)/shard_map/ppermute | solution.py:240
  166.7 19.6 %collective-permute-start.3 = (bf16[2,1,384,384]{2,3,0,1:T(8,128)(2,1)}, bf16[2,1,384,384]{2,3,0,1:T(8,128)(2,1)}, u32[]{:S(2)}, u32[]{:S(2)}) collective-permute-start(bf16[2,1,384,384]{2,3,0,1:T(8,128)(2,1)} %add_convert_fusion), channel_id=1, source_target_pairs={{0,2},{1,3},{2,0},{3,1},{4,6},{5,7},{6,4},{7,5},{8,10},{9,11},{10,... | collective-permute-start | bytes 1769480 | tf_op jit(solution)/shard_map/ppermute | solution.py:240
  174.6 18.9 %all-to-all-start.5 = ((f32[32,1,4096]{2,1,0:T(1,128)}), f32[32,1,4096]{2,1,0:T(1,128)}, u32[]{:S(2)}, u32[]{:S(2)}) async-start(f32[32,1,4096]{2,1,0:T(1,128)} %broadcast_in_dim.8), calls=%async_computation.5 | async-start | bytes 1048576 | tf_op jit(solution)/shard_map/all_to_all | solution.py:228

commit v3 on v2

--- a/solution.py
+++ b/solution.py
@@ -180,20 +180,15 @@
     onehot = (owner[:, :, None] == jnp.arange(tile_count, dtype=jnp.int32)).astype(jnp.int32)
     place_in = jnp.sum((jnp.cumsum(onehot, axis=1) - 1) * onehot, axis=2)
     slot_of = owner * capacity + place_in
-    chosen = slot_of[:, None, :] == jnp.arange(slots, dtype=jnp.int32)[None, :, None]
-    valid = jnp.any(chosen, axis=2).astype(jnp.int32)
-    entry = jnp.argmax(chosen, axis=2).astype(jnp.int32)
-    meta = jnp.stack(
-        [
-            jnp.take_along_axis(local_tile, entry, axis=1),
-            jnp.take_along_axis(scan_offset[:, :, 0], entry, axis=1),
-            jnp.take_along_axis(scan_offset[:, :, 1], entry, axis=1),
-            valid,
-        ],
-        axis=2,
-    ).astype(jnp.bfloat16)
+    chosen = (slot_of[:, None, :] == jnp.arange(slots, dtype=jnp.int32)[None, :, None]).astype(
+        jnp.int32
+    )
+    fields = jnp.stack(
+        [local_tile, scan_offset[:, :, 0], scan_offset[:, :, 1], jnp.ones_like(local_tile)], axis=2
+    )
+    meta = jnp.sum(chosen[:, :, :, None] * fields[:, None, :, :], axis=2).astype(jnp.bfloat16)
     meta = jnp.pad(meta[:, :, None, :], ((0, 0), (0, 0), (0, 7), (0, length - 4)))
-    ids = jnp.take_along_axis(batch_ids, entry, axis=1)
+    ids = jnp.sum(chosen * batch_ids[:, None, :], axis=2)
     amp_send = amplitudes[ids.reshape(-1)].reshape(steps, slots, length, length)
     payload = jnp.concatenate([amp_send, meta], axis=2)
     return payload.reshape(steps, tile_count, capacity, length + 8, length)
@@ -300,7 +295,7 @@
     tiles_next = tiles_now + summed / peak_power
     grad_sum = all_sum_a2a(probe_grad, ("tile", "pat"))
     probe_next = probe_now + probe_rate * grad_sum / batch_total
-    return (tiles_next, probe_next)
+    return (tiles_next, probe_next, probe_grad)
 
 
 def on_device(amplitudes, batch_ids, scan_tile, scan_offset, object_tiles, probe):
@@ -311,8 +306,13 @@
     tiles_now = object_tiles
     probe_now = probe
     for step_no in range(batch_ids.shape[0]):
-        amp_in, meta_in = exchange(payload[step_no], size)
-        tiles_now, probe_now = one_step(tiles_now, probe_now, amp_in, meta_in, tables, batch_total)
+        sending = payload[step_no]
+        if step_no > 0:
+            sending, _ = lax.optimization_barrier((sending, local_grad))
+        amp_in, meta_in = exchange(sending, size)
+        tiles_now, probe_now, local_grad = one_step(
+            tiles_now, probe_now, amp_in, meta_in, tables, batch_total
+        )
     return (tiles_now, probe_now)
 
 

time: 198 us -> 206 us (1.040); the launches traced: 196 us -> 206 us
  Pallas kernels: 23.5 us -> 38 us
  starting transfers between devices: 56.1 us -> 43.2 us
  waiting for transfers between devices: 51.5 us -> 64.2 us
  local copies, waits for them, and re-layouts: 15 us -> 10.7 us
    pallas_call x2, Pallas kernels: 23.5 us -> 38 us  [entries_kernel(): pl.pallas_call(entry_kernel, grid_spec=grid_spec, out_shape=[jax.ShapeDty...]
    all_to_all x2, starting transfers between devices: 34.3 us -> 21.2 us  [sum_over(): lax.all_to_all(value.astype(send_type).reshape(count, -1), axes, 0, 0, ti...]
    all_to_all x2, waiting for transfers between devices: 20 us -> 29.6 us  [exchange(): lax.all_to_all(payload, 'tile', 0, 0, tiled=True)]
    gather x9 -> x0, local copies, waits for them, and re-layouts: 5.35 us -> none  [the longest x3 1.91 us: route(): ids = jnp.take_along_axis(batch_ids, entry, axis=1)]
    all_to_all x2, waiting for transfers between devices: 14.3 us -> 19 us  [sum_over(): lax.all_to_all(value.astype(send_type).reshape(count, -1), axes, 0, 0, ti...]
    unnamed x17 -> x18, local copies, waits for them, and re-layouts: 4.7 us -> 5.47 us
  transfers between devices with their start and end apart: 10 -> 10, of which waited for: 8 -> 8; matrix products, arithmetic and copies ran while one was open for 24% -> 20% of each run, Pallas kernels for 6% -> 0%
where the time goes in v3:
time: 206 us
  waiting for transfers between devices  64.2 us (31%)
  starting transfers between devices  43.2 us (21%)
  Pallas kernels  38 us (18%)
  matrix products  25.5 us (12%)
  other arithmetic  23.8 us (12%)
  local copies, waits for them, and re-layouts  10.7 us (5%)
    pallas_call x2, Pallas kernels, entries_kernel(): pl.pallas_call(entry_kernel, grid_spec=grid_spec, out_shape=[jax.ShapeDty...  38 us
    all_to_all x2, waiting for transfers between devices, exchange(): lax.all_to_all(payload, 'tile', 0, 0, tiled=True)  29.6 us
    all_to_all x2, starting transfers between devices, sum_over(): lax.all_to_all(value.astype(send_type).reshape(count, -1), axes, 0, 0, ti...  21.2 us
    all_to_all x2, waiting for transfers between devices, sum_over(): lax.all_to_all(value.astype(send_type).reshape(count, -1), axes, 0, 0, ti...  19 us
    all_to_all x2, starting transfers between devices, exchange(): lax.all_to_all(payload, 'tile', 0, 0, tiled=True)  11.6 us
    dot_general x2, matrix products, entries_pass(): jnp.einsum('skq,xskc->xqc', pick_rows, spread, preferred_element_type=jnp...  11.4 us
    ppermute x4, waiting for transfers between devices, all_sum_pairs(): other = lax.ppermute(total.astype(send_type), axis, pairs)  9.8 us
    dot_general x2, matrix products, entries_pass(): jnp.einsum('skq,xqc->xskc', pick_rows, stacked, preferred_element_type=jn...  8.14 us
  transfers between devices with their start and end apart: 10, of which 8 were waited for; matrix products, arithmetic and copies ran while one was open for 20% of the time, Pallas kernels for 0%

profile of v3, /device:TPU:0, one launch (start us, length us, event | category | flops | bytes accessed | tf_op | source)
XLA Modules:
  0.0 206.3 jit_solution(4142704677012479265)
XLA Ops:
  7.8 7.4 %all-to-all-start = ((bf16[8,3,136,128]{3,2,1,0:T(8,128)(2,1)}), bf16[8,3,136,128]{3,2,1,0:T(8,128)(2,1)S(1)}, u32[]{:S(2)}, u32[]{:S(2)}) async-start(bf16[8,3,136,128]{3,2,1,0:T(8,128)(2,1)} %bitcast.4), calls=%async_computation | async-start | bytes 1671168 | tf_op jit(solution)/shard_map/all_to_all | solution.py:199
  16.5 20.0 %all-to-all-done = bf16[8,3,136,128]{3,2,1,0:T(8,128)(2,1)S(1)} async-done(((bf16[8,3,136,128]{3,2,1,0:T(8,128)(2,1)}), bf16[8,3,136,128]{3,2,1,0:T(8,128)(2,1)S(1)}, u32[]{:S(2)}, u32[]{:S(2)}) %all-to-all-start) | async-done | bytes 835616 | tf_op jit(solution)/shard_map/all_to_all | solution.py:199
  37.3 3.1 %convert_bitcast_fusion.1 = bf16[2,24,128,384]{3,2,0,1:T(8,128)(2,1)S(1)} fusion(s32[24,128]{1,0:T(8,128)S(1)} %get-tuple-element.32, pred[24]{0:T(512)(128)(4,1)S(1)} %broadcast_compare_fusion.1, f32[2,1,384,384]{3,2,1,0:T(8,128)S(1)} %copy-done.4), kind=kOutput, calls=%fused_computation.14 | convolution fusion | flops 1816952832 | bytes 5910552 | tf_op jit(solution)/shard_map/skq,xqc->xskc/dot_general | solution.py:256
  40.4 2.6 %fusion.73.patch_ref = bf16[2,24,128,128]{3,2,1,0:T(8,128)(2,1)} fusion(bf16[2,24,128,384]{3,2,0,1:T(8,128)(2,1)S(1)} %convert_bitcast_fusion.1, s32[24,128]{1,0:T(8,128)S(1)} %get-tuple-element.33), kind=kOutput, calls=%fused_computation.47 | convolution fusion | flops 605945856 | bytes 6303744 | tf_op jit(solution)/shard_map/xskc,scl->xskl/dot_general | solution.py:259
  43.0 19.0 %shard_map.77 = (bf16[2,24,128,128]{3,2,1,0:T(8,128)(2,1)}, f32[4,2,128,128]{3,2,1,0:T(8,128)}) custom-call(s32[24]{0:T(128)} %get-tuple-element.31.valid_ref, bf16[2,24,128,128]{3,2,1,0:T(8,128)(2,1)} %fusion.73.patch_ref, bf16[24,136,128]{2,1,0:T(8,128)(2,1)} %bitcast.164, f32[4,2,128,128]{3,2,1,0:T(8,128)} %probe_ref.1, ...), custom_call_target="tpu_custom_call" | custom-call | flops 6442450944 | bytes 4980736 | tf_op jit(solution)/shard_map/pallas_call | solution.py:155
  62.0 10.8 %all-to-all-start.2 = ((f32[32,1,4096]{2,1,0:T(1,128)}), f32[32,1,4096]{2,1,0:T(1,128)S(1)}, u32[]{:S(2)}, u32[]{:S(2)}) async-start(f32[32,1,4096]{2,1,0:T(1,128)} %bitcast.166), calls=%async_computation.2 | async-start | bytes 1048576 | tf_op jit(solution)/shard_map/all_to_all | solution.py:216
  72.8 15.5 %all-to-all-done.2 = f32[32,1,4096]{2,1,0:T(1,128)S(1)} async-done(((f32[32,1,4096]{2,1,0:T(1,128)}), f32[32,1,4096]{2,1,0:T(1,128)S(1)}, u32[]{:S(2)}, u32[]{:S(2)}) %all-to-all-start.2) | async-done | bytes 524320 | tf_op jit(solution)/shard_map/all_to_all | solution.py:216
  88.4 4.2 %all-to-all-start.1 = ((bf16[8,3,136,128]{3,2,1,0:T(8,128)(2,1)}), bf16[8,3,136,128]{3,2,1,0:T(8,128)(2,1)}, u32[]{:S(2)}, u32[]{:S(2)}) async-start(bf16[8,3,136,128]{3,2,1,0:T(8,128)(2,1)} %bitcast.24), calls=%async_computation.1 | async-start | bytes 1671168 | tf_op jit(solution)/shard_map/all_to_all | solution.py:199
  92.6 5.3 %fusion.106 = bf16[2,1,384,384]{2,3,0,1:T(8,128)(2,1)S(1)} fusion(s32[24,128]{1,0:T(8,128)S(1)} %get-tuple-element.32, pred[24]{0:T(512)(128)(4,1)S(1)} %broadcast_compare_fusion.1, bf16[2,24,128,128]{3,2,1,0:T(8,128)(2,1)} %get-tuple-element.7, s32[24,128]{1,0:T(8,128)S(1)} %get-tuple-element.33), kind=kOutput, calls=%fused_computation.52 | convolution fusion | flops 2422112256 | bytes 2187288 | tf_op jit(solution)/shard_map/skq,xskc->xqc/dot_general | solution.py:267
  104.5 9.6 %all-to-all-done.1 = bf16[8,3,136,128]{3,2,1,0:T(8,128)(2,1)} async-done(((bf16[8,3,136,128]{3,2,1,0:T(8,128)(2,1)}), bf16[8,3,136,128]{3,2,1,0:T(8,128)(2,1)}, u32[]{:S(2)}, u32[]{:S(2)}) %all-to-all-start.1) | async-done | bytes 835616 | tf_op jit(solution)/shard_map/all_to_all | solution.py:199
  115.4 3.9 %all-to-all-start.3 = ((f32[32,1,4096]{2,1,0:T(1,128)}), f32[32,1,4096]{2,1,0:T(1,128)}, u32[]{:S(2)}, u32[]{:S(2)}) async-start(f32[32,1,4096]{2,1,0:T(1,128)} %broadcast_in_dim.4), calls=%async_computation.3 | async-start | bytes 1048576 | tf_op jit(solution)/shard_map/all_to_all | solution.py:223
  120.9 5.1 %convert_bitcast_fusion = bf16[2,24,128,384]{2,3,0,1:T(8,128)(2,1)S(1)} fusion(s32[24,128]{1,0:T(8,128)S(1)} %iota_add_fusion, pred[24]{0:T(512)(128)(4,1)S(1)} %broadcast_compare_fusion, f32[2,1,384,384]{2,3,0,1:T(8,128)S(1)} %copy.60, bf16[2,1,384,384]{2,3,0,1:T(8,128)(2,1)} %collective-permute-done.1, ...), kind=kOutput, calls=%fused_computation.10 | convolution fusion | flops 1818427392 | bytes 7090204 | tf_op jit(solution)/shard_map/skq,xqc->xskc/dot_general | solution.py:256
  125.9 3.3 %fusion.68.patch_ref = bf16[2,24,128,128]{3,2,1,0:T(8,128)(2,1)} fusion(bf16[2,24,128,384]{2,3,0,1:T(8,128)(2,1)S(1)} %convert_bitcast_fusion, s32[24,128]{1,0:T(8,128)S(1)} %iota_add_fusion.1), kind=kOutput, calls=%fused_computation.46 | convolution fusion | flops 605945856 | bytes 6303744 | tf_op jit(solution)/shard_map/xskc,scl->xskl/dot_general | solution.py:259
  129.2 5.4 %all-to-all-done.3 = f32[32,1,4096]{2,1,0:T(1,128)} async-done(((f32[32,1,4096]{2,1,0:T(1,128)}), f32[32,1,4096]{2,1,0:T(1,128)}, u32[]{:S(2)}, u32[]{:S(2)}) %all-to-all-start.3) | async-done | bytes 524320 | tf_op jit(solution)/shard_map/all_to_all | solution.py:223
  137.2 19.0 %shard_map.78 = (bf16[2,24,128,128]{3,2,1,0:T(8,128)(2,1)}, f32[4,2,128,128]{3,2,1,0:T(8,128)}) custom-call(s32[24]{0:T(128)} %get-tuple-element.28.valid_ref, bf16[2,24,128,128]{3,2,1,0:T(8,128)(2,1)} %fusion.68.patch_ref, bf16[24,136,128]{2,1,0:T(8,128)(2,1)} %bitcast.25.amp_ref, f32[4,2,128,128]{3,2,1,0:T(8,128)} %add.201.probe_ref, ...), custom_call_target="tpu_custom_call" | custom-call | flops 6442450944 | bytes 4980736 | tf_op jit(solution)/shard_map/pallas_call | solution.py:155
  156.2 10.5 %all-to-all-start.4 = ((f32[32,1,4096]{2,1,0:T(1,128)}), f32[32,1,4096]{2,1,0:T(1,128)}, u32[]{:S(2)}, u32[]{:S(2)}) async-start(f32[32,1,4096]{2,1,0:T(1,128)} %bitcast.165), calls=%async_computation.4 | async-start | bytes 1048576 | tf_op jit(solution)/shard_map/all_to_all | solution.py:216
  166.6 6.1 %fusion.113 = bf16[2,1,384,384]{2,3,0,1:T(8,128)(2,1)} fusion(s32[24,128]{1,0:T(8,128)S(1)} %iota_add_fusion, pred[24]{0:T(512)(128)(4,1)S(1)} %broadcast_compare_fusion, bf16[2,24,128,128]{3,2,1,0:T(8,128)(2,1)} %get-tuple-element.10, s32[24,128]{1,0:T(8,128)S(1)} %iota_add_fusion.1), kind=kOutput, calls=%fused_computation.53 | convolution fusion | flops 2422112256 | bytes 2187288 | tf_op jit(solution)/shard_map/skq,xskc->xqc/dot_general | solution.py:267
  172.9 2.0 collective-permute-done.2
  175.0 2.0 add_convert_fusion
  178.7 3.5 %all-to-all-done.4 = f32[32,1,4096]{2,1,0:T(1,128)} async-done(((f32[32,1,4096]{2,1,0:T(1,128)}), f32[32,1,4096]{2,1,0:T(1,128)}, u32[]{:S(2)}, u32[]{:S(2)}) %all-to-all-start.4) | async-done | bytes 524320 | tf_op jit(solution)/shard_map/all_to_all | solution.py:216
  184.8 3.3 %all-to-all-start.5 = ((f32[32,1,4096]{2,1,0:T(1,128)}), f32[32,1,4096]{2,1,0:T(1,128)}, u32[]{:S(2)}, u32[]{:S(2)}) async-start(f32[32,1,4096]{2,1,0:T(1,128)} %broadcast_in_dim.5), calls=%async_computation.5 | async-start | bytes 1048576 | tf_op jit(solution)/shard_map/all_to_all | solution.py:223
  188.9 7.8 %collective-permute-done.3 = bf16[2,1,384,384]{2,3,0,1:T(8,128)(2,1)} collective-permute-done((bf16[2,1,384,384]{2,3,0,1:T(8,128)(2,1)}, bf16[2,1,384,384]{2,3,0,1:T(8,128)(2,1)}, u32[]{:S(2)}, u32[]{:S(2)}) %collective-permute-start.3) | collective-permute-done | bytes 589856 | tf_op jit(solution)/shard_map/ppermute | solution.py:235
  196.6 4.1 %divide_add_fusion = f32[2,1,384,384]{2,3,0,1:T(8,128)} fusion(bf16[2,1,384,384]{2,3,0,1:T(8,128)(2,1)} %collective-permute-done.3, bf16[2,1,384,384]{2,3,0,1:T(8,128)(2,1)} %add_convert_fusion, f32[]{:T(128)} %reduce_max.19, f32[2,1,384,384]{2,3,0,1:T(8,128)S(1)} %copy.60, f32[]{:T(128)} %reduce_max.18, bf16[2,1,384,384]{2,3,0,1:T(8,128)(2,1)} %collective-permute-done.1, ...), kind=kLoop, calls=%fused_computation.54 | loop fusion | flops 2949120 | bytes 4718600 | tf_op jit(solution)/shard_map/add | solution.py:295
  200.7 2.7 %copy.67 = f32[2,1,384,384]{3,2,1,0:T(8,128)} copy(f32[2,1,384,384]{2,3,0,1:T(8,128)} %divide_add_fusion) | data formatting | bytes 2359296
  (71 shorter events, 29.2 us)
Async XLA Ops:
  0.6 4.8 %copy-start = (bf16[32,128,128]{2,1,0:T(8,128)(2,1)S(1)}, bf16[32,128,128]{2,1,0:T(8,128)(2,1)}, u32[]{:S(2)}) copy-start(bf16[32,128,128]{2,1,0:T(8,128)(2,1)} %param.6) | copy-start | bytes 3145732
  7.8 29.5 %copy-start.4 = (f32[2,1,384,384]{3,2,1,0:T(8,128)S(1)}, f32[2,1,384,384]{3,2,1,0:T(8,128)}, u32[]{:S(2)}) copy-start(f32[2,1,384,384]{3,2,1,0:T(8,128)} %param.10) | copy-start | bytes 3538948
  7.8 28.7 %all-to-all-start = ((bf16[8,3,136,128]{3,2,1,0:T(8,128)(2,1)}), bf16[8,3,136,128]{3,2,1,0:T(8,128)(2,1)S(1)}, u32[]{:S(2)}, u32[]{:S(2)}) async-start(bf16[8,3,136,128]{3,2,1,0:T(8,128)(2,1)} %bitcast.4), calls=%async_computation | async-start | bytes 1671168 | tf_op jit(solution)/shard_map/all_to_all | solution.py:199
  36.4 3.9 %copy-start.5 = (bf16[8,3,136,128]{3,2,1,0:T(8,128)(2,1)}, bf16[8,3,136,128]{3,2,1,0:T(8,128)(2,1)S(1)}, u32[]{:S(2)}) copy-start(bf16[8,3,136,128]{3,2,1,0:T(8,128)(2,1)S(1)} %all-to-all-done) | copy-start | bytes 2506756
  62.0 26.3 %all-to-all-start.2 = ((f32[32,1,4096]{2,1,0:T(1,128)}), f32[32,1,4096]{2,1,0:T(1,128)S(1)}, u32[]{:S(2)}, u32[]{:S(2)}) async-start(f32[32,1,4096]{2,1,0:T(1,128)} %bitcast.166), calls=%async_computation.2 | async-start | bytes 1048576 | tf_op jit(solution)/shard_map/all_to_all | solution.py:216
  88.4 9.5 %copy-start.3 = (f32[32,1,4096]{2,1,0:T(1,128)}, f32[32,1,4096]{2,1,0:T(1,128)S(1)}, u32[]{:S(2)}) copy-start(f32[32,1,4096]{2,1,0:T(1,128)S(1)} %all-to-all-done.2) | copy-start | bytes 1572868
  88.4 25.8 %all-to-all-start.1 = ((bf16[8,3,136,128]{3,2,1,0:T(8,128)(2,1)}), bf16[8,3,136,128]{3,2,1,0:T(8,128)(2,1)}, u32[]{:S(2)}, u32[]{:S(2)}) async-start(bf16[8,3,136,128]{3,2,1,0:T(8,128)(2,1)} %bitcast.24), calls=%async_computation.1 | async-start | bytes 1671168 | tf_op jit(solution)/shard_map/all_to_all | solution.py:199
  97.9 2.7 %copy-start.6 = (bf16[2,1,384,384]{2,3,0,1:T(8,128)(2,1)}, bf16[2,1,384,384]{2,3,0,1:T(8,128)(2,1)S(1)}, u32[]{:S(2)}) copy-start(bf16[2,1,384,384]{2,3,0,1:T(8,128)(2,1)S(1)} %fusion.106) | copy-start | bytes 1769476
  97.9 2.0 copy-start.2
  97.9 2.7 %collective-permute-start = (bf16[2,1,384,384]{2,3,0,1:T(8,128)(2,1)S(1)}, bf16[2,1,384,384]{2,3,0,1:T(8,128)(2,1)}, u32[]{:S(2)}, u32[]{:S(2)}) collective-permute-start(bf16[2,1,384,384]{2,3,0,1:T(8,128)(2,1)S(1)} %fusion.106), channel_id=1, source_target_pairs={{0,1},{1,0},{2,3},{3,2},{4,5},{5,4},{6,7},{7,6},{8,9},{9,8},{10,11... | collective-permute-start | bytes 1769480 | tf_op jit(solution)/shard_map/ppermute | solution.py:235
  102.0 18.9 %collective-permute-start.1 = (bf16[2,1,384,384]{2,3,0,1:T(8,128)(2,1)S(1)}, bf16[2,1,384,384]{2,3,0,1:T(8,128)(2,1)}, u32[]{:S(2)}, u32[]{:S(2)}) collective-permute-start(bf16[2,1,384,384]{2,3,0,1:T(8,128)(2,1)S(1)} %add_convert_fusion.1), channel_id=1, source_target_pairs={{0,2},{1,3},{2,0},{3,1},{4,6},{5,7},{6,4},{7,5},{8,10},{9,11},{10,... | collective-permute-start | bytes 1769480 | tf_op jit(solution)/shard_map/ppermute | solution.py:235
  115.4 19.2 %all-to-all-start.3 = ((f32[32,1,4096]{2,1,0:T(1,128)}), f32[32,1,4096]{2,1,0:T(1,128)}, u32[]{:S(2)}, u32[]{:S(2)}) async-start(f32[32,1,4096]{2,1,0:T(1,128)} %broadcast_in_dim.4), calls=%async_computation.3 | async-start | bytes 1048576 | tf_op jit(solution)/shard_map/all_to_all | solution.py:223
  156.2 26.0 %all-to-all-start.4 = ((f32[32,1,4096]{2,1,0:T(1,128)}), f32[32,1,4096]{2,1,0:T(1,128)}, u32[]{:S(2)}, u32[]{:S(2)}) async-start(f32[32,1,4096]{2,1,0:T(1,128)} %bitcast.165), calls=%async_computation.4 | async-start | bytes 1048576 | tf_op jit(solution)/shard_map/all_to_all | solution.py:216
  172.7 15.4 %copy-start.1 = (f32[4,2,128,128]{3,2,1,0:T(8,128)S(1)}, f32[4,2,128,128]{3,2,1,0:T(8,128)}, u32[]{:S(2)}) copy-start(f32[4,2,128,128]{3,2,1,0:T(8,128)} %add.201.probe_ref) | copy-start | bytes 1572868
  172.7 2.2 %collective-permute-start.2 = (bf16[2,1,384,384]{2,3,0,1:T(8,128)(2,1)}, bf16[2,1,384,384]{2,3,0,1:T(8,128)(2,1)S(1)}, u32[]{:S(2)}, u32[]{:S(2)}) collective-permute-start(bf16[2,1,384,384]{2,3,0,1:T(8,128)(2,1)} %fusion.113), channel_id=1, source_target_pairs={{0,1},{1,0},{2,3},{3,2},{4,5},{5,4},{6,7},{7,6},{8,9},{9,8},{10,11... | collective-permute-start | bytes 1769480 | tf_op jit(solution)/shard_map/ppermute | solution.py:235
  177.0 19.6 %collective-permute-start.3 = (bf16[2,1,384,384]{2,3,0,1:T(8,128)(2,1)}, bf16[2,1,384,384]{2,3,0,1:T(8,128)(2,1)}, u32[]{:S(2)}, u32[]{:S(2)}) collective-permute-start(bf16[2,1,384,384]{2,3,0,1:T(8,128)(2,1)} %add_convert_fusion), channel_id=1, source_target_pairs={{0,2},{1,3},{2,0},{3,1},{4,6},{5,7},{6,4},{7,5},{8,10},{9,11},{10,... | collective-permute-start | bytes 1769480 | tf_op jit(solution)/shard_map/ppermute | solution.py:235
  184.8 18.9 %all-to-all-start.5 = ((f32[32,1,4096]{2,1,0:T(1,128)}), f32[32,1,4096]{2,1,0:T(1,128)}, u32[]{:S(2)}, u32[]{:S(2)}) async-start(f32[32,1,4096]{2,1,0:T(1,128)} %broadcast_in_dim.5), calls=%async_computation.5 | async-start | bytes 1048576 | tf_op jit(solution)/shard_map/all_to_all | solution.py:223

commit v4 on v3

--- a/solution.py
+++ b/solution.py
@@ -306,13 +306,8 @@
     tiles_now = object_tiles
     probe_now = probe
     for step_no in range(batch_ids.shape[0]):
-        sending = payload[step_no]
-        if step_no > 0:
-            sending, _ = lax.optimization_barrier((sending, local_grad))
-        amp_in, meta_in = exchange(sending, size)
-        tiles_now, probe_now, local_grad = one_step(
-            tiles_now, probe_now, amp_in, meta_in, tables, batch_total
-        )
+        amp_in, meta_in = exchange(payload[step_no], size)
+        tiles_now, probe_now, _ = one_step(tiles_now, probe_now, amp_in, meta_in, tables, batch_total)
     return (tiles_now, probe_now)
 
 

time: 206 us -> 195 us (0.947); the launches traced: 206 us -> 192 us
  waiting for transfers between devices: 64.2 us -> 51.5 us
    all_to_all x2, waiting for transfers between devices: 29.6 us -> 20 us  [exchange(): lax.all_to_all(payload, 'tile', 0, 0, tiled=True)]
    all_to_all x2, waiting for transfers between devices: 19 us -> 14.3 us  [sum_over(): lax.all_to_all(value.astype(send_type).reshape(count, -1), axes, 0, 0, ti...]
    unnamed x18 -> x16, local copies, waits for them, and re-layouts: 5.47 us -> 5.46 us
  transfers between devices with their start and end apart: 10 -> 10, of which waited for: 8 -> 8; matrix products, arithmetic and copies ran while one was open for 20% -> 25% of each run, Pallas kernels for 0% -> 10%
where the time goes in v4:
time: 195 us; the launch traced here: 192 us
  waiting for transfers between devices  51.5 us (26%)
  starting transfers between devices  41.7 us (21%)
  Pallas kernels  38 us (19%)
  matrix products  25.5 us (13%)
  other arithmetic  23.8 us (12%)
  local copies, waits for them, and re-layouts  10.7 us (5%)
    pallas_call x2, Pallas kernels, entries_kernel(): pl.pallas_call(entry_kernel, grid_spec=grid_spec, out_shape=[jax.ShapeDty...  38 us
    all_to_all x2, waiting for transfers between devices, exchange(): lax.all_to_all(payload, 'tile', 0, 0, tiled=True)  20 us
    all_to_all x2, starting transfers between devices, sum_over(): lax.all_to_all(value.astype(send_type).reshape(count, -1), axes, 0, 0, ti...  19.6 us
    all_to_all x2, waiting for transfers between devices, sum_over(): lax.all_to_all(value.astype(send_type).reshape(count, -1), axes, 0, 0, ti...  14.3 us
    all_to_all x2, starting transfers between devices, exchange(): lax.all_to_all(payload, 'tile', 0, 0, tiled=True)  11.6 us
    dot_general x2, matrix products, entries_pass(): jnp.einsum('skq,xskc->xqc', pick_rows, spread, preferred_element_type=jnp...  11.4 us
    ppermute x4, waiting for transfers between devices, all_sum_pairs(): other = lax.ppermute(total.astype(send_type), axis, pairs)  9.99 us
    dot_general x2, matrix products, entries_pass(): jnp.einsum('skq,xqc->xskc', pick_rows, stacked, preferred_element_type=jn...  8.09 us
  transfers between devices with their start and end apart: 10, of which 8 were waited for; matrix products, arithmetic and copies ran while one was open for 25% of the time, Pallas kernels for 10%

profile of v4, /device:TPU:0, one launch (start us, length us, event | category | flops | bytes accessed | tf_op | source)
XLA Modules:
  0.0 192.0 jit_solution(16951228233690277094)
XLA Ops:
  7.8 7.4 %all-to-all-start = ((bf16[8,3,136,128]{3,2,1,0:T(8,128)(2,1)}), bf16[8,3,136,128]{3,2,1,0:T(8,128)(2,1)S(1)}, u32[]{:S(2)}, u32[]{:S(2)}) async-start(bf16[8,3,136,128]{3,2,1,0:T(8,128)(2,1)} %bitcast.4), calls=%async_computation | async-start | bytes 1671168 | tf_op jit(solution)/shard_map/all_to_all | solution.py:199
  16.4 20.0 %all-to-all-done = bf16[8,3,136,128]{3,2,1,0:T(8,128)(2,1)S(1)} async-done(((bf16[8,3,136,128]{3,2,1,0:T(8,128)(2,1)}), bf16[8,3,136,128]{3,2,1,0:T(8,128)(2,1)S(1)}, u32[]{:S(2)}, u32[]{:S(2)}) %all-to-all-start) | async-done | bytes 835616 | tf_op jit(solution)/shard_map/all_to_all | solution.py:199
  36.4 4.2 %all-to-all-start.1 = ((bf16[8,3,136,128]{3,2,1,0:T(8,128)(2,1)}), bf16[8,3,136,128]{3,2,1,0:T(8,128)(2,1)}, u32[]{:S(2)}, u32[]{:S(2)}) async-start(bf16[8,3,136,128]{3,2,1,0:T(8,128)(2,1)} %bitcast.24), calls=%async_computation.1 | async-start | bytes 1671168 | tf_op jit(solution)/shard_map/all_to_all | solution.py:199
  41.4 3.1 %convert_bitcast_fusion.1 = bf16[2,24,128,384]{3,2,0,1:T(8,128)(2,1)S(1)} fusion(s32[24,128]{1,0:T(8,128)S(1)} %get-tuple-element.30, pred[24]{0:T(512)(128)(4,1)S(1)} %broadcast_compare_fusion.1, f32[2,1,384,384]{3,2,1,0:T(8,128)S(1)} %copy-done.3), kind=kOutput, calls=%fused_computation.14 | convolution fusion | flops 1816952832 | bytes 5910552 | tf_op jit(solution)/shard_map/skq,xqc->xskc/dot_general | solution.py:256
  44.5 2.7 %fusion.73.patch_ref = bf16[2,24,128,128]{3,2,1,0:T(8,128)(2,1)} fusion(bf16[2,24,128,384]{3,2,0,1:T(8,128)(2,1)S(1)} %convert_bitcast_fusion.1, s32[24,128]{1,0:T(8,128)S(1)} %get-tuple-element.31), kind=kOutput, calls=%fused_computation.47 | convolution fusion | flops 605945856 | bytes 6303744 | tf_op jit(solution)/shard_map/xskc,scl->xskl/dot_general | solution.py:259
  47.2 19.0 %shard_map.77 = (bf16[2,24,128,128]{3,2,1,0:T(8,128)(2,1)}, f32[4,2,128,128]{3,2,1,0:T(8,128)}) custom-call(s32[24]{0:T(128)} %get-tuple-element.29.valid_ref, bf16[2,24,128,128]{3,2,1,0:T(8,128)(2,1)} %fusion.73.patch_ref, bf16[24,136,128]{2,1,0:T(8,128)(2,1)} %bitcast.164, f32[4,2,128,128]{3,2,1,0:T(8,128)} %probe_ref.1, ...), custom_call_target="tpu_custom_call" | custom-call | flops 6442450944 | bytes 4980736 | tf_op jit(solution)/shard_map/pallas_call | solution.py:155
  66.2 5.3 %fusion.106 = bf16[2,1,384,384]{2,3,0,1:T(8,128)(2,1)S(1)} fusion(s32[24,128]{1,0:T(8,128)S(1)} %get-tuple-element.30, pred[24]{0:T(512)(128)(4,1)S(1)} %broadcast_compare_fusion.1, bf16[2,24,128,128]{3,2,1,0:T(8,128)(2,1)} %get-tuple-element.6, s32[24,128]{1,0:T(8,128)S(1)} %get-tuple-element.31), kind=kOutput, calls=%fused_computation.52 | convolution fusion | flops 2422112256 | bytes 2187288 | tf_op jit(solution)/shard_map/skq,xskc->xqc/dot_general | solution.py:267
  71.6 1.9 copy.60
  74.2 10.6 %all-to-all-start.2 = ((f32[32,1,4096]{2,1,0:T(1,128)}), f32[32,1,4096]{2,1,0:T(1,128)}, u32[]{:S(2)}, u32[]{:S(2)}) async-start(f32[32,1,4096]{2,1,0:T(1,128)} %bitcast.165), calls=%async_computation.2 | async-start | bytes 1048576 | tf_op jit(solution)/shard_map/all_to_all | solution.py:216
  89.5 10.8 %all-to-all-done.2 = f32[32,1,4096]{2,1,0:T(1,128)} async-done(((f32[32,1,4096]{2,1,0:T(1,128)}), f32[32,1,4096]{2,1,0:T(1,128)}, u32[]{:S(2)}, u32[]{:S(2)}) %all-to-all-start.2) | async-done | bytes 524320 | tf_op jit(solution)/shard_map/all_to_all | solution.py:216
  102.9 3.5 %all-to-all-start.3 = ((f32[32,1,4096]{2,1,0:T(1,128)}), f32[32,1,4096]{2,1,0:T(1,128)}, u32[]{:S(2)}, u32[]{:S(2)}) async-start(f32[32,1,4096]{2,1,0:T(1,128)} %broadcast_in_dim.4), calls=%async_computation.3 | async-start | bytes 1048576 | tf_op jit(solution)/shard_map/all_to_all | solution.py:223
  106.7 5.0 %convert_bitcast_fusion = bf16[2,24,128,384]{2,3,0,1:T(8,128)(2,1)S(1)} fusion(s32[24,128]{1,0:T(8,128)S(1)} %iota_add_fusion, pred[24]{0:T(512)(128)(4,1)S(1)} %broadcast_compare_fusion, f32[2,1,384,384]{2,3,0,1:T(8,128)S(1)} %copy.60, bf16[2,1,384,384]{2,3,0,1:T(8,128)(2,1)} %collective-permute-done.1, ...), kind=kOutput, calls=%fused_computation.10 | convolution fusion | flops 1818427392 | bytes 7090204 | tf_op jit(solution)/shard_map/skq,xqc->xskc/dot_general | solution.py:256
  111.7 3.3 %fusion.68.patch_ref = bf16[2,24,128,128]{3,2,1,0:T(8,128)(2,1)} fusion(bf16[2,24,128,384]{2,3,0,1:T(8,128)(2,1)S(1)} %convert_bitcast_fusion, s32[24,128]{1,0:T(8,128)S(1)} %iota_add_fusion.1), kind=kOutput, calls=%fused_computation.46 | convolution fusion | flops 605945856 | bytes 6303744 | tf_op jit(solution)/shard_map/xskc,scl->xskl/dot_general | solution.py:259
  115.0 6.8 %all-to-all-done.3 = f32[32,1,4096]{2,1,0:T(1,128)} async-done(((f32[32,1,4096]{2,1,0:T(1,128)}), f32[32,1,4096]{2,1,0:T(1,128)}, u32[]{:S(2)}, u32[]{:S(2)}) %all-to-all-start.3) | async-done | bytes 524320 | tf_op jit(solution)/shard_map/all_to_all | solution.py:223
  124.3 19.0 %shard_map.78 = (bf16[2,24,128,128]{3,2,1,0:T(8,128)(2,1)}, f32[4,2,128,128]{3,2,1,0:T(8,128)}) custom-call(s32[24]{0:T(128)} %get-tuple-element.26.valid_ref, bf16[2,24,128,128]{3,2,1,0:T(8,128)(2,1)} %fusion.68.patch_ref, bf16[24,136,128]{2,1,0:T(8,128)(2,1)} %bitcast.25.amp_ref, f32[4,2,128,128]{3,2,1,0:T(8,128)} %add.201.probe_ref, ...), custom_call_target="tpu_custom_call" | custom-call | flops 6442450944 | bytes 4980736 | tf_op jit(solution)/shard_map/pallas_call | solution.py:155
  143.4 9.0 %all-to-all-start.4 = ((f32[32,1,4096]{2,1,0:T(1,128)}), f32[32,1,4096]{2,1,0:T(1,128)}, u32[]{:S(2)}, u32[]{:S(2)}) async-start(f32[32,1,4096]{2,1,0:T(1,128)} %bitcast.166), calls=%async_computation.4 | async-start | bytes 1048576 | tf_op jit(solution)/shard_map/all_to_all | solution.py:216
  152.4 6.1 %fusion.113 = bf16[2,1,384,384]{2,3,0,1:T(8,128)(2,1)} fusion(s32[24,128]{1,0:T(8,128)S(1)} %iota_add_fusion, pred[24]{0:T(512)(128)(4,1)S(1)} %broadcast_compare_fusion, bf16[2,24,128,128]{3,2,1,0:T(8,128)(2,1)} %get-tuple-element.8, s32[24,128]{1,0:T(8,128)S(1)} %iota_add_fusion.1), kind=kOutput, calls=%fused_computation.53 | convolution fusion | flops 2422112256 | bytes 2187288 | tf_op jit(solution)/shard_map/skq,xskc->xqc/dot_general | solution.py:267
  158.7 2.0 %collective-permute-done.2 = bf16[2,1,384,384]{2,3,0,1:T(8,128)(2,1)S(1)} collective-permute-done((bf16[2,1,384,384]{2,3,0,1:T(8,128)(2,1)}, bf16[2,1,384,384]{2,3,0,1:T(8,128)(2,1)S(1)}, u32[]{:S(2)}, u32[]{:S(2)}) %collective-permute-start.2) | collective-permute-done | bytes 589856 | tf_op jit(solution)/shard_map/ppermute | solution.py:235
  160.7 2.0 %add_convert_fusion = bf16[2,1,384,384]{2,3,0,1:T(8,128)(2,1)} fusion(bf16[2,1,384,384]{2,3,0,1:T(8,128)(2,1)S(1)} %collective-permute-done.2, bf16[2,1,384,384]{2,3,0,1:T(8,128)(2,1)} %fusion.113), kind=kLoop, calls=%fused_computation.55 | loop fusion | flops 1179648 | bytes 1769472 | tf_op jit(solution)/shard_map/convert_element_type | solution.py:236
  164.4 3.5 %all-to-all-done.4 = f32[32,1,4096]{2,1,0:T(1,128)} async-done(((f32[32,1,4096]{2,1,0:T(1,128)}), f32[32,1,4096]{2,1,0:T(1,128)}, u32[]{:S(2)}, u32[]{:S(2)}) %all-to-all-start.4) | async-done | bytes 524320 | tf_op jit(solution)/shard_map/all_to_all | solution.py:216
  170.6 3.3 %all-to-all-start.5 = ((f32[32,1,4096]{2,1,0:T(1,128)}), f32[32,1,4096]{2,1,0:T(1,128)}, u32[]{:S(2)}, u32[]{:S(2)}) async-start(f32[32,1,4096]{2,1,0:T(1,128)} %broadcast_in_dim.5), calls=%async_computation.5 | async-start | bytes 1048576 | tf_op jit(solution)/shard_map/all_to_all | solution.py:223
  174.6 7.7 %collective-permute-done.3 = bf16[2,1,384,384]{2,3,0,1:T(8,128)(2,1)} collective-permute-done((bf16[2,1,384,384]{2,3,0,1:T(8,128)(2,1)}, bf16[2,1,384,384]{2,3,0,1:T(8,128)(2,1)}, u32[]{:S(2)}, u32[]{:S(2)}) %collective-permute-start.3) | collective-permute-done | bytes 589856 | tf_op jit(solution)/shard_map/ppermute | solution.py:235
  182.4 4.0 %divide_add_fusion = f32[2,1,384,384]{2,3,0,1:T(8,128)} fusion(bf16[2,1,384,384]{2,3,0,1:T(8,128)(2,1)} %collective-permute-done.3, bf16[2,1,384,384]{2,3,0,1:T(8,128)(2,1)} %add_convert_fusion, f32[]{:T(128)} %reduce_max.19, f32[2,1,384,384]{2,3,0,1:T(8,128)S(1)} %copy.60, f32[]{:T(128)} %reduce_max.18, bf16[2,1,384,384]{2,3,0,1:T(8,128)(2,1)} %collective-permute-done.1, ...), kind=kLoop, calls=%fused_computation.54 | loop fusion | flops 2949120 | bytes 4718600 | tf_op jit(solution)/shard_map/add | solution.py:295
  186.4 2.7 %copy.67 = f32[2,1,384,384]{3,2,1,0:T(8,128)} copy(f32[2,1,384,384]{2,3,0,1:T(8,128)} %divide_add_fusion) | data formatting | bytes 2359296
  (69 shorter events, 28.2 us)
Async XLA Ops:
  0.6 4.8 %copy-start = (bf16[32,128,128]{2,1,0:T(8,128)(2,1)S(1)}, bf16[32,128,128]{2,1,0:T(8,128)(2,1)}, u32[]{:S(2)}) copy-start(bf16[32,128,128]{2,1,0:T(8,128)(2,1)} %param.6) | copy-start | bytes 3145732
  7.8 33.7 %copy-start.3 = (f32[2,1,384,384]{3,2,1,0:T(8,128)S(1)}, f32[2,1,384,384]{3,2,1,0:T(8,128)}, u32[]{:S(2)}) copy-start(f32[2,1,384,384]{3,2,1,0:T(8,128)} %param.10) | copy-start | bytes 3538948
  7.8 28.7 %all-to-all-start = ((bf16[8,3,136,128]{3,2,1,0:T(8,128)(2,1)}), bf16[8,3,136,128]{3,2,1,0:T(8,128)(2,1)S(1)}, u32[]{:S(2)}, u32[]{:S(2)}) async-start(bf16[8,3,136,128]{3,2,1,0:T(8,128)(2,1)} %bitcast.4), calls=%async_computation | async-start | bytes 1671168 | tf_op jit(solution)/shard_map/all_to_all | solution.py:199
  36.4 8.1 %copy-start.4 = (bf16[8,3,136,128]{3,2,1,0:T(8,128)(2,1)}, bf16[8,3,136,128]{3,2,1,0:T(8,128)(2,1)S(1)}, u32[]{:S(2)}) copy-start(bf16[8,3,136,128]{3,2,1,0:T(8,128)(2,1)S(1)} %all-to-all-done) | copy-start | bytes 2506756
  36.4 37.7 %all-to-all-start.1 = ((bf16[8,3,136,128]{3,2,1,0:T(8,128)(2,1)}), bf16[8,3,136,128]{3,2,1,0:T(8,128)(2,1)}, u32[]{:S(2)}, u32[]{:S(2)}) async-start(bf16[8,3,136,128]{3,2,1,0:T(8,128)(2,1)} %bitcast.24), calls=%async_computation.1 | async-start | bytes 1671168 | tf_op jit(solution)/shard_map/all_to_all | solution.py:199
  71.5 2.7 %copy-start.5 = (bf16[2,1,384,384]{2,3,0,1:T(8,128)(2,1)}, bf16[2,1,384,384]{2,3,0,1:T(8,128)(2,1)S(1)}, u32[]{:S(2)}) copy-start(bf16[2,1,384,384]{2,3,0,1:T(8,128)(2,1)S(1)} %fusion.106) | copy-start | bytes 1769476
  71.5 2.0 %copy-start.2 = (f32[4,2,128,128]{3,2,1,0:T(8,128)S(1)}, f32[4,2,128,128]{3,2,1,0:T(8,128)}, u32[]{:S(2)}) copy-start(f32[4,2,128,128]{3,2,1,0:T(8,128)} %probe_ref.1) | copy-start | bytes 1572868
  71.5 14.7 %collective-permute-start = (bf16[2,1,384,384]{2,3,0,1:T(8,128)(2,1)S(1)}, bf16[2,1,384,384]{2,3,0,1:T(8,128)(2,1)}, u32[]{:S(2)}, u32[]{:S(2)}) collective-permute-start(bf16[2,1,384,384]{2,3,0,1:T(8,128)(2,1)S(1)} %fusion.106), channel_id=1, source_target_pairs={{0,1},{1,0},{2,3},{3,2},{4,5},{5,4},{6,7},{7,6},{8,9},{9,8},{10,11... | collective-permute-start | bytes 1769480 | tf_op jit(solution)/shard_map/ppermute | solution.py:235
  74.2 26.1 %all-to-all-start.2 = ((f32[32,1,4096]{2,1,0:T(1,128)}), f32[32,1,4096]{2,1,0:T(1,128)}, u32[]{:S(2)}, u32[]{:S(2)}) async-start(f32[32,1,4096]{2,1,0:T(1,128)} %bitcast.165), calls=%async_computation.2 | async-start | bytes 1048576 | tf_op jit(solution)/shard_map/all_to_all | solution.py:216
  87.6 19.0 %collective-permute-start.1 = (bf16[2,1,384,384]{2,3,0,1:T(8,128)(2,1)S(1)}, bf16[2,1,384,384]{2,3,0,1:T(8,128)(2,1)}, u32[]{:S(2)}, u32[]{:S(2)}) collective-permute-start(bf16[2,1,384,384]{2,3,0,1:T(8,128)(2,1)S(1)} %add_convert_fusion.1), channel_id=1, source_target_pairs={{0,2},{1,3},{2,0},{3,1},{4,6},{5,7},{6,4},{7,5},{8,10},{9,11},{10,... | collective-permute-start | bytes 1769480 | tf_op jit(solution)/shard_map/ppermute | solution.py:235
  102.9 18.9 %all-to-all-start.3 = ((f32[32,1,4096]{2,1,0:T(1,128)}), f32[32,1,4096]{2,1,0:T(1,128)}, u32[]{:S(2)}, u32[]{:S(2)}) async-start(f32[32,1,4096]{2,1,0:T(1,128)} %broadcast_in_dim.4), calls=%async_computation.3 | async-start | bytes 1048576 | tf_op jit(solution)/shard_map/all_to_all | solution.py:223
  143.4 24.6 %all-to-all-start.4 = ((f32[32,1,4096]{2,1,0:T(1,128)}), f32[32,1,4096]{2,1,0:T(1,128)}, u32[]{:S(2)}, u32[]{:S(2)}) async-start(f32[32,1,4096]{2,1,0:T(1,128)} %bitcast.166), calls=%async_computation.4 | async-start | bytes 1048576 | tf_op jit(solution)/shard_map/all_to_all | solution.py:216
  158.5 15.4 %copy-start.1 = (f32[4,2,128,128]{3,2,1,0:T(8,128)S(1)}, f32[4,2,128,128]{3,2,1,0:T(8,128)}, u32[]{:S(2)}) copy-start(f32[4,2,128,128]{3,2,1,0:T(8,128)} %add.201.probe_ref) | copy-start | bytes 1572868
  158.5 2.2 %collective-permute-start.2 = (bf16[2,1,384,384]{2,3,0,1:T(8,128)(2,1)}, bf16[2,1,384,384]{2,3,0,1:T(8,128)(2,1)S(1)}, u32[]{:S(2)}, u32[]{:S(2)}) collective-permute-start(bf16[2,1,384,384]{2,3,0,1:T(8,128)(2,1)} %fusion.113), channel_id=1, source_target_pairs={{0,1},{1,0},{2,3},{3,2},{4,5},{5,4},{6,7},{7,6},{8,9},{9,8},{10,11... | collective-permute-start | bytes 1769480 | tf_op jit(solution)/shard_map/ppermute | solution.py:235
  162.7 19.6 %collective-permute-start.3 = (bf16[2,1,384,384]{2,3,0,1:T(8,128)(2,1)}, bf16[2,1,384,384]{2,3,0,1:T(8,128)(2,1)}, u32[]{:S(2)}, u32[]{:S(2)}) collective-permute-start(bf16[2,1,384,384]{2,3,0,1:T(8,128)(2,1)} %add_convert_fusion), channel_id=1, source_target_pairs={{0,2},{1,3},{2,0},{3,1},{4,6},{5,7},{6,4},{7,5},{8,10},{9,11},{10,... | collective-permute-start | bytes 1769480 | tf_op jit(solution)/shard_map/ppermute | solution.py:235
  170.6 18.9 %all-to-all-start.5 = ((f32[32,1,4096]{2,1,0:T(1,128)}), f32[32,1,4096]{2,1,0:T(1,128)}, u32[]{:S(2)}, u32[]{:S(2)}) async-start(f32[32,1,4096]{2,1,0:T(1,128)} %broadcast_in_dim.5), calls=%async_computation.5 | async-start | bytes 1048576 | tf_op jit(solution)/shard_map/all_to_all | solution.py:223

commit v5 on v4

--- a/solution.py
+++ b/solution.py
@@ -48,36 +48,37 @@
     return left, right
 
 
-def entry_kernel(valid_ref, patch_ref, amp_ref, probe_ref, left_ref, right_ref, update_ref, grad_ref):
+def entry_kernel(order_ref, patch_ref, amp_ref, probe_ref, left_ref, right_ref, update_ref, grad_ref):
+    slots = order_ref.shape[0] - 1
+    count = order_ref[slots]
+    group = 2 if slots % 2 == 0 else 1
     grad_ref[...] = jnp.zeros(grad_ref.shape, grad_ref.dtype)
-
-    def one_slot(slot, carry):
-        @pl.when(valid_ref[slot] == 0)
-        def _():
-            update_ref[:, slot] = jnp.zeros((2,) + update_ref.shape[2:], update_ref.dtype)
-
-        @pl.when(valid_ref[slot] != 0)
-        def _():
-            entry_body(slot, patch_ref, amp_ref, probe_ref, left_ref, right_ref, update_ref, grad_ref)
-
+    update_ref[...] = jnp.zeros(update_ref.shape, update_ref.dtype)
+
+    def one_group(index, carry):
+        chosen = [order_ref[index * group + g] for g in range(group)]
+        entry_body(chosen, patch_ref, amp_ref, probe_ref, left_ref, right_ref, update_ref, grad_ref)
         return carry
 
-    lax.fori_loop(0, valid_ref.shape[0], one_slot, 0)
-
-
-def entry_body(slot, patch_ref, amp_ref, probe_ref, left_ref, right_ref, update_ref, grad_ref):
+    lax.fori_loop(0, (count + group - 1) // group, one_group, 0)
+
+
+def entry_body(chosen, patch_ref, amp_ref, probe_ref, left_ref, right_ref, update_ref, grad_ref):
     modes, length = probe_ref.shape[0], probe_ref.shape[-1]
-
-    patch_re = patch_ref[0, slot].astype(jnp.float32)
-    patch_im = patch_ref[1, slot].astype(jnp.float32)
+    blocks = len(chosen) * modes
+    patches = [
+        (patch_ref[0, slot].astype(jnp.float32), patch_ref[1, slot].astype(jnp.float32))
+        for slot in chosen
+    ]
     left = left_ref[...]
     right = right_ref[...]
     exits_re, exits_im = [], []
-    for m in range(modes):
-        probe_re = probe_ref[m, 0]
-        probe_im = probe_ref[m, 1]
-        exits_re.append((probe_re * patch_re - probe_im * patch_im).astype(jnp.bfloat16))
-        exits_im.append((probe_re * patch_im + probe_im * patch_re).astype(jnp.bfloat16))
+    for patch_re, patch_im in patches:
+        for m in range(modes):
+            probe_re = probe_ref[m, 0]
+            probe_im = probe_ref[m, 1]
+            exits_re.append((probe_re * patch_re - probe_im * patch_im).astype(jnp.bfloat16))
+            exits_im.append((probe_re * patch_im + probe_im * patch_re).astype(jnp.bfloat16))
     stacked = jnp.concatenate(
         [jnp.concatenate(exits_re, 1), jnp.concatenate(exits_im, 1)], 0
     )
@@ -88,12 +89,12 @@
             [
                 jnp.concatenate(
                     [
-                        wide[:length, m * length : (m + 1) * length],
-                        wide[length:, m * length : (m + 1) * length],
+                        wide[:length, j * length : (j + 1) * length],
+                        wide[length:, j * length : (j + 1) * length],
                     ],
                     1,
                 )
-                for m in range(modes)
+                for j in range(blocks)
             ],
             0,
         )
@@ -102,46 +103,59 @@
         return jnp.concatenate(
             [
                 jnp.concatenate(
-                    [tall[m * length : (m + 1) * length, :length] for m in range(modes)], 1
+                    [tall[j * length : (j + 1) * length, :length] for j in range(blocks)], 1
                 ),
                 jnp.concatenate(
-                    [tall[m * length : (m + 1) * length, length:] for m in range(modes)], 1
+                    [tall[j * length : (j + 1) * length, length:] for j in range(blocks)], 1
                 ),
             ],
             0,
         )
 
     far = jnp.dot(by_mode(half), right, preferred_element_type=jnp.float32)
-    intensity = jnp.zeros((length, length), jnp.float32)
-    for m in range(modes):
-        far_re = far[m * length : (m + 1) * length, :length]
-        far_im = far[m * length : (m + 1) * length, length:]
-        intensity = intensity + (far_re * far_re + far_im * far_im)
-    measured = amp_ref[slot, :length, :].astype(jnp.float32)
-    factor = measured / jnp.sqrt(jnp.maximum(intensity, 1.0)) - 1.0
-    factor = jnp.concatenate([factor, factor], 1)
-    factor = jnp.concatenate([factor] * modes, 0)
-    scaled = (factor * far).astype(jnp.bfloat16)
+    factors = []
+    for g, slot in enumerate(chosen):
+        intensity = jnp.zeros((length, length), jnp.float32)
+        for m in range(modes):
+            j = g * modes + m
+            far_re = far[j * length : (j + 1) * length, :length]
+            far_im = far[j * length : (j + 1) * length, length:]
+            intensity = intensity + (far_re * far_re + far_im * far_im)
+        measured = amp_ref[slot, :length, :].astype(jnp.float32)
+        factor = measured / jnp.sqrt(jnp.maximum(intensity, 1.0)) - 1.0
+        factors.extend([jnp.concatenate([factor, factor], 1)] * modes)
+    scaled = (jnp.concatenate(factors, 0) * far).astype(jnp.bfloat16)
     back = jnp.dot(right, by_part(scaled), preferred_element_type=jnp.float32).astype(
         jnp.bfloat16
     )
     change = jnp.dot(by_mode(back), left, preferred_element_type=jnp.float32)
-    update_re = jnp.zeros((length, length), jnp.float32)
-    update_im = jnp.zeros((length, length), jnp.float32)
+    grads = [[None, None] for _ in range(modes)]
+    for g, slot in enumerate(chosen):
+        patch_re, patch_im = patches[g]
+        update_re = jnp.zeros((length, length), jnp.float32)
+        update_im = jnp.zeros((length, length), jnp.float32)
+        for m in range(modes):
+            j = g * modes + m
+            change_re = change[j * length : (j + 1) * length, :length]
+            change_im = change[j * length : (j + 1) * length, length:]
+            probe_re = probe_ref[m, 0]
+            probe_im = probe_ref[m, 1]
+            update_re = update_re + (probe_re * change_re + probe_im * change_im)
+            update_im = update_im + (probe_re * change_im - probe_im * change_re)
+            grad_re = patch_re * change_re + patch_im * change_im
+            grad_im = patch_re * change_im - patch_im * change_re
+            if g == 0:
+                grads[m] = [grad_re, grad_im]
+            else:
+                grads[m] = [grads[m][0] + grad_re, grads[m][1] + grad_im]
+        update_ref[0, slot] = update_re.astype(update_ref.dtype)
+        update_ref[1, slot] = update_im.astype(update_ref.dtype)
     for m in range(modes):
-        change_re = change[m * length : (m + 1) * length, :length]
-        change_im = change[m * length : (m + 1) * length, length:]
-        probe_re = probe_ref[m, 0]
-        probe_im = probe_ref[m, 1]
-        update_re = update_re + (probe_re * change_re + probe_im * change_im)
-        update_im = update_im + (probe_re * change_im - probe_im * change_re)
-        grad_ref[m, 0] += patch_re * change_re + patch_im * change_im
-        grad_ref[m, 1] += patch_re * change_im - patch_im * change_re
-    update_ref[0, slot] = update_re.astype(update_ref.dtype)
-    update_ref[1, slot] = update_im.astype(update_ref.dtype)
-
-
-def entries_kernel(valid, patch, amp_in, probe_now, left, right):
+        grad_ref[m, 0] += grads[m][0]
+        grad_ref[m, 1] += grads[m][1]
+
+
+def entries_kernel(order, patch, amp_in, probe_now, left, right):
     slots, length = amp_in.shape[0], amp_in.shape[-1]
     modes = probe_now.shape[0]
     flops = slots * 4 * 2 * (2 * length) * (2 * length) * (modes * length)
@@ -165,7 +179,7 @@
             transcendentals=slots * length * length,
             bytes_accessed=slots * length * length * 10 + probe_now.size * 8,
         ),
-    )(valid, patch, amp_in, probe_now, left, right)
+    )(order, patch, amp_in, probe_now, left, right)
 
 
 def route(amplitudes, batch_ids, scan_tile, scan_offset, tiles_here):
@@ -258,8 +272,18 @@
     ).astype(jnp.bfloat16)
     patch = jnp.einsum("xskc,scl->xskl", rows, pick_cols, preferred_element_type=jnp.float32)
     left, right = block_tables(tables[0], tables[1])
+    held = (valid > 0).astype(jnp.int32)
+    count = jnp.sum(held)
+    place = jnp.where(held > 0, jnp.cumsum(held) - 1, count + jnp.cumsum(1 - held) - 1)
+    slots = valid.shape[0]
+    order = jnp.sum(
+        (place[:, None] == jnp.arange(slots, dtype=jnp.int32)[None, :])
+        * jnp.arange(slots, dtype=jnp.int32)[:, None],
+        axis=0,
+    )
+    order = jnp.concatenate([order, count[None]]).astype(jnp.int32)
     update, probe_grad = entries_kernel(
-        valid, patch.astype(jnp.bfloat16), amp_in, probe_now, left, right
+        order, patch.astype(jnp.bfloat16), amp_in, probe_now, left, right
     )
     spread = jnp.einsum(
         "xskl,scl->xskc", update, pick_cols, preferred_element_type=jnp.float32

time: 195 us -> 198 us (1.015)
  blocking collectives: 0 us -> 29.1 us
  starting transfers between devices: 41.7 us -> 28.8 us
  Pallas kernels: 38 us -> 26 us
  waiting for transfers between devices: 51.5 us -> 45.7 us
  other arithmetic: 23.8 us -> 28.6 us
    all_to_all x0 -> x1, blocking collectives: none -> 29.1 us  [exchange(): lax.all_to_all(payload, 'tile', 0, 0, tiled=True)]
    pallas_call x2, Pallas kernels: 38 us -> 26 us  [entries_kernel(): pl.pallas_call(entry_kernel, grid_spec=grid_spec, out_shape=[jax.ShapeDty...]
    all_to_all x2 -> x1, starting transfers between devices: 11.6 us -> 4.22 us  [exchange(): lax.all_to_all(payload, 'tile', 0, 0, tiled=True)]
    all_to_all x2, starting transfers between devices: 19.6 us -> 14 us  [sum_over(): lax.all_to_all(value.astype(send_type).reshape(count, -1), axes, 0, 0, ti...]
    all_to_all x2 -> x1, waiting for transfers between devices: 20 us -> 15.9 us  [exchange(): lax.all_to_all(payload, 'tile', 0, 0, tiled=True)]
    concatenate x0 -> x2, other arithmetic: none -> 2.51 us  [entries_pass(): order = jnp.concatenate([order, count[None]]).astype(jnp.int32)]
  transfers between devices with their start and end apart: 10 -> 9, of which waited for: 8 -> 8; matrix products, arithmetic and copies ran while one was open for 25% -> 19% of each run, Pallas kernels for 10% -> 0%
where the time goes in v5:
time: 198 us; the launch traced here: 196 us
  waiting for transfers between devices  45.7 us (23%)
  blocking collectives  29.1 us (15%)
  starting transfers between devices  28.8 us (15%)
  other arithmetic  28.6 us (14%)
  matrix products  26.8 us (14%)
  Pallas kernels  26 us (13%)
  local copies, waits for them, and re-layouts  10.4 us (5%)
    all_to_all x1, blocking collectives, exchange(): lax.all_to_all(payload, 'tile', 0, 0, tiled=True)  29.1 us
    pallas_call x2, Pallas kernels, entries_kernel(): pl.pallas_call(entry_kernel, grid_spec=grid_spec, out_shape=[jax.ShapeDty...  26 us
    all_to_all x1, waiting for transfers between devices, exchange(): lax.all_to_all(payload, 'tile', 0, 0, tiled=True)  15.9 us
    all_to_all x2, waiting for transfers between devices, sum_over(): lax.all_to_all(value.astype(send_type).reshape(count, -1), axes, 0, 0, ti...  14.1 us
    all_to_all x2, starting transfers between devices, sum_over(): lax.all_to_all(value.astype(send_type).reshape(count, -1), axes, 0, 0, ti...  14 us
    dot_general x2, matrix products, entries_pass(): jnp.einsum('skq,xskc->xqc', pick_rows, spread, preferred_element_type=jnp...  11.4 us
    ppermute x4, waiting for transfers between devices, all_sum_pairs(): other = lax.ppermute(total.astype(send_type), axis, pairs)  9.79 us
    dot_general x2, matrix products, entries_pass(): jnp.einsum('skq,xqc->xskc', pick_rows, stacked, preferred_element_type=jn...  9.49 us
  transfers between devices with their start and end apart: 9, of which 8 were waited for; matrix products, arithmetic and copies ran while one was open for 19% of the time, Pallas kernels for 0%

profile of v5, /device:TPU:0, one launch (start us, length us, event | category | flops | bytes accessed | tf_op | source)
XLA Modules:
  0.0 196.3 jit_solution(7006367911874314944)
XLA Ops:
  7.5 29.1 %all_to_all.40 = bf16[8,3,136,128]{3,2,1,0:T(8,128)(2,1)} all-to-all(bf16[8,3,136,128]{3,2,1,0:T(8,128)(2,1)S(1)} %bitcast.155), channel_id=1, replica_groups=mesh['tile'=8,'pat'=4] {'tile'}, dimensions={0} | all-to-all | bytes 1671168 | tf_op jit(solution)/shard_map/all_to_all | solution.py:213
  36.5 4.2 %all-to-all-start = ((bf16[8,3,136,128]{3,2,1,0:T(8,128)(2,1)}), bf16[8,3,136,128]{3,2,1,0:T(8,128)(2,1)}, u32[]{:S(2)}, u32[]{:S(2)}) async-start(bf16[8,3,136,128]{3,2,1,0:T(8,128)(2,1)} %bitcast.4), calls=%async_computation | async-start | bytes 1671168 | tf_op jit(solution)/shard_map/all_to_all | solution.py:213
  45.5 15.9 %all-to-all-done = bf16[8,3,136,128]{3,2,1,0:T(8,128)(2,1)} async-done(((bf16[8,3,136,128]{3,2,1,0:T(8,128)(2,1)}), bf16[8,3,136,128]{3,2,1,0:T(8,128)(2,1)}, u32[]{:S(2)}, u32[]{:S(2)}) %all-to-all-start) | async-done | bytes 835616 | tf_op jit(solution)/shard_map/all_to_all | solution.py:213
  64.1 4.4 %convert_bitcast_fusion.1 = bf16[2,24,128,384]{3,2,0,1:T(8,128)(2,1)S(1)} fusion(s32[24,128]{1,0:T(8,128)S(1)} %get-tuple-element.34, pred[24]{0:T(512)(128)(4,1)S(1)} %reduce.4, f32[2,1,384,384]{3,2,1,0:T(8,128)} %param.10), kind=kOutput, calls=%fused_computation.14 | convolution fusion | flops 1816952832 | bytes 5910552 | tf_op jit(solution)/shard_map/skq,xqc->xskc/dot_general | solution.py:270
  69.7 2.6 %fusion.73.patch_ref = bf16[2,24,128,128]{3,2,1,0:T(8,128)(2,1)} fusion(bf16[2,24,128,384]{3,2,0,1:T(8,128)(2,1)S(1)} %convert_bitcast_fusion.1, s32[24,128]{1,0:T(8,128)S(1)} %get-tuple-element.35), kind=kOutput, calls=%fused_computation.47 | convolution fusion | flops 605945856 | bytes 6303744 | tf_op jit(solution)/shard_map/xskc,scl->xskl/dot_general | solution.py:273
  72.4 13.0 %shard_map.77 = (bf16[2,24,128,128]{3,2,1,0:T(8,128)(2,1)}, f32[4,2,128,128]{3,2,1,0:T(8,128)}) custom-call(s32[25]{0:T(128)} %pad_add_fusion.order_ref, bf16[2,24,128,128]{3,2,1,0:T(8,128)(2,1)} %fusion.73.patch_ref, bf16[24,136,128]{2,1,0:T(8,128)(2,1)} %bitcast.5.amp_ref, f32[4,2,128,128]{3,2,1,0:T(8,128)} %probe_ref.1, ...), custom_call_target="tpu_custom_call" | custom-call | flops 6442450944 | bytes 4980736 | tf_op jit(solution)/shard_map/pallas_call | solution.py:169
  85.4 5.3 %fusion.106 = bf16[2,1,384,384]{2,3,0,1:T(8,128)(2,1)S(1)} fusion(s32[24,128]{1,0:T(8,128)S(1)} %get-tuple-element.34, pred[24]{0:T(512)(128)(4,1)S(1)} %reduce.4, bf16[2,24,128,128]{3,2,1,0:T(8,128)(2,1)} %get-tuple-element.6, s32[24,128]{1,0:T(8,128)S(1)} %get-tuple-element.35), kind=kOutput, calls=%fused_computation.52 | convolution fusion | flops 2422112256 | bytes 2187288 | tf_op jit(solution)/shard_map/skq,xskc->xqc/dot_general | solution.py:291
  91.0 7.1 %all-to-all-start.2 = ((f32[32,1,4096]{2,1,0:T(1,128)}), f32[32,1,4096]{2,1,0:T(1,128)S(1)}, u32[]{:S(2)}, u32[]{:S(2)}) async-start(f32[32,1,4096]{2,1,0:T(1,128)} %bitcast.160), calls=%async_computation.2 | async-start | bytes 1048576 | tf_op jit(solution)/shard_map/all_to_all | solution.py:230
  101.1 1.8 collective-permute-start.1
  103.1 10.6 %all-to-all-done.2 = f32[32,1,4096]{2,1,0:T(1,128)S(1)} async-done(((f32[32,1,4096]{2,1,0:T(1,128)}), f32[32,1,4096]{2,1,0:T(1,128)S(1)}, u32[]{:S(2)}, u32[]{:S(2)}) %all-to-all-start.2) | async-done | bytes 524320 | tf_op jit(solution)/shard_map/all_to_all | solution.py:230
  115.3 3.5 %all-to-all-start.3 = ((f32[32,1,4096]{2,1,0:T(1,128)}), f32[32,1,4096]{2,1,0:T(1,128)}, u32[]{:S(2)}, u32[]{:S(2)}) async-start(f32[32,1,4096]{2,1,0:T(1,128)} %broadcast_in_dim.10), calls=%async_computation.3 | async-start | bytes 1048576 | tf_op jit(solution)/shard_map/all_to_all | solution.py:237
  120.2 5.1 %convert_bitcast_fusion = bf16[2,24,128,384]{2,3,0,1:T(8,128)(2,1)S(1)} fusion(s32[24,128]{1,0:T(8,128)S(1)} %iota_add_fusion, pred[24]{0:T(512)(128)(4,1)S(1)} %reduce.6, f32[2,1,384,384]{2,3,0,1:T(8,128)S(1)} %copy.69, bf16[2,1,384,384]{2,3,0,1:T(8,128)(2,1)} %collective-permute-done.1, bf16[2,1,384,384]{2,3,0,1:T(8,128)(2,1)S(1)} %add_convert_fusion.1, ...), kind=kOutput, calls=%fused_computation.10 | convolution fusion | flops 1818427392 | bytes 7090204 | tf_op jit(solution)/shard_map/skq,xqc->xskc/dot_general | solution.py:270
  125.3 3.3 %fusion.68.patch_ref = bf16[2,24,128,128]{3,2,1,0:T(8,128)(2,1)} fusion(bf16[2,24,128,384]{2,3,0,1:T(8,128)(2,1)S(1)} %convert_bitcast_fusion, s32[24,128]{1,0:T(8,128)S(1)} %iota_add_fusion.1), kind=kOutput, calls=%fused_computation.46 | convolution fusion | flops 605945856 | bytes 6303744 | tf_op jit(solution)/shard_map/xskc,scl->xskl/dot_general | solution.py:273
  128.6 5.6 %all-to-all-done.3 = f32[32,1,4096]{2,1,0:T(1,128)} async-done(((f32[32,1,4096]{2,1,0:T(1,128)}), f32[32,1,4096]{2,1,0:T(1,128)}, u32[]{:S(2)}, u32[]{:S(2)}) %all-to-all-start.3) | async-done | bytes 524320 | tf_op jit(solution)/shard_map/all_to_all | solution.py:237
  136.8 13.0 %shard_map.78 = (bf16[2,24,128,128]{3,2,1,0:T(8,128)(2,1)}, f32[4,2,128,128]{3,2,1,0:T(8,128)}) custom-call(s32[25]{0:T(128)} %pad_add_fusion.1.order_ref, bf16[2,24,128,128]{3,2,1,0:T(8,128)(2,1)} %fusion.68.patch_ref, bf16[24,136,128]{2,1,0:T(8,128)(2,1)} %bitcast.159, f32[4,2,128,128]{3,2,1,0:T(8,128)} %add.263.probe_ref, ...), custom_call_target="tpu_custom_call" | custom-call | flops 6442450944 | bytes 4980736 | tf_op jit(solution)/shard_map/pallas_call | solution.py:169
  149.8 6.8 %all-to-all-start.4 = ((f32[32,1,4096]{2,1,0:T(1,128)}), f32[32,1,4096]{2,1,0:T(1,128)}, u32[]{:S(2)}, u32[]{:S(2)}) async-start(f32[32,1,4096]{2,1,0:T(1,128)} %bitcast.161), calls=%async_computation.4 | async-start | bytes 1048576 | tf_op jit(solution)/shard_map/all_to_all | solution.py:230
  156.6 6.1 %fusion.113 = bf16[2,1,384,384]{2,3,0,1:T(8,128)(2,1)} fusion(s32[24,128]{1,0:T(8,128)S(1)} %iota_add_fusion, pred[24]{0:T(512)(128)(4,1)S(1)} %reduce.6, bf16[2,24,128,128]{3,2,1,0:T(8,128)(2,1)} %get-tuple-element.8, s32[24,128]{1,0:T(8,128)S(1)} %iota_add_fusion.1), kind=kOutput, calls=%fused_computation.53 | convolution fusion | flops 2422112256 | bytes 2187288 | tf_op jit(solution)/shard_map/skq,xskc->xqc/dot_general | solution.py:291
  162.9 2.0 %collective-permute-done.2 = bf16[2,1,384,384]{2,3,0,1:T(8,128)(2,1)S(1)} collective-permute-done((bf16[2,1,384,384]{2,3,0,1:T(8,128)(2,1)}, bf16[2,1,384,384]{2,3,0,1:T(8,128)(2,1)S(1)}, u32[]{:S(2)}, u32[]{:S(2)}) %collective-permute-start.2) | collective-permute-done | bytes 589856 | tf_op jit(solution)/shard_map/ppermute | solution.py:249
  164.9 2.0 %add_convert_fusion = bf16[2,1,384,384]{2,3,0,1:T(8,128)(2,1)} fusion(bf16[2,1,384,384]{2,3,0,1:T(8,128)(2,1)S(1)} %collective-permute-done.2, bf16[2,1,384,384]{2,3,0,1:T(8,128)(2,1)} %fusion.113), kind=kLoop, calls=%fused_computation.55 | loop fusion | flops 1179648 | bytes 1769472 | tf_op jit(solution)/shard_map/convert_element_type | solution.py:250
  168.7 3.6 %all-to-all-done.4 = f32[32,1,4096]{2,1,0:T(1,128)} async-done(((f32[32,1,4096]{2,1,0:T(1,128)}), f32[32,1,4096]{2,1,0:T(1,128)}, u32[]{:S(2)}, u32[]{:S(2)}) %all-to-all-start.4) | async-done | bytes 524320 | tf_op jit(solution)/shard_map/all_to_all | solution.py:230
  174.9 3.3 %all-to-all-start.5 = ((f32[32,1,4096]{2,1,0:T(1,128)}), f32[32,1,4096]{2,1,0:T(1,128)}, u32[]{:S(2)}, u32[]{:S(2)}) async-start(f32[32,1,4096]{2,1,0:T(1,128)} %broadcast_in_dim.11), calls=%async_computation.5 | async-start | bytes 1048576 | tf_op jit(solution)/shard_map/all_to_all | solution.py:237
  178.9 7.7 %collective-permute-done.3 = bf16[2,1,384,384]{2,3,0,1:T(8,128)(2,1)} collective-permute-done((bf16[2,1,384,384]{2,3,0,1:T(8,128)(2,1)}, bf16[2,1,384,384]{2,3,0,1:T(8,128)(2,1)}, u32[]{:S(2)}, u32[]{:S(2)}) %collective-permute-start.3) | collective-permute-done | bytes 589856 | tf_op jit(solution)/shard_map/ppermute | solution.py:249
  186.6 4.1 %divide_add_fusion = f32[2,1,384,384]{2,3,0,1:T(8,128)} fusion(bf16[2,1,384,384]{2,3,0,1:T(8,128)(2,1)} %collective-permute-done.3, bf16[2,1,384,384]{2,3,0,1:T(8,128)(2,1)} %add_convert_fusion, f32[]{:T(128)} %reduce_max.19, f32[2,1,384,384]{2,3,0,1:T(8,128)S(1)} %copy.69, f32[]{:T(128)} %reduce_max.18, bf16[2,1,384,384]{2,3,0,1:T(8,128)(2,1)} %collective-permute-done.1, ...), kind=kLoop, calls=%fused_computation.54 | loop fusion | flops 2949120 | bytes 4718600 | tf_op jit(solution)/shard_map/add | solution.py:319
  190.7 2.7 %copy.77 = f32[2,1,384,384]{3,2,1,0:T(8,128)} copy(f32[2,1,384,384]{2,3,0,1:T(8,128)} %divide_add_fusion) | data formatting | bytes 2359296
  (84 shorter events, 32.5 us)
Async XLA Ops:
  0.6 4.8 %copy-start = (bf16[32,128,128]{2,1,0:T(8,128)(2,1)S(1)}, bf16[32,128,128]{2,1,0:T(8,128)(2,1)}, u32[]{:S(2)}) copy-start(bf16[32,128,128]{2,1,0:T(8,128)(2,1)} %param.6) | copy-start | bytes 3145732
  36.5 24.8 %all-to-all-start = ((bf16[8,3,136,128]{3,2,1,0:T(8,128)(2,1)}), bf16[8,3,136,128]{3,2,1,0:T(8,128)(2,1)}, u32[]{:S(2)}, u32[]{:S(2)}) async-start(bf16[8,3,136,128]{3,2,1,0:T(8,128)(2,1)} %bitcast.4), calls=%async_computation | async-start | bytes 1671168 | tf_op jit(solution)/shard_map/all_to_all | solution.py:213
  40.8 1.7 copy-start.2
  90.7 9.0 %copy-start.4 = (bf16[2,1,384,384]{2,3,0,1:T(8,128)(2,1)}, bf16[2,1,384,384]{2,3,0,1:T(8,128)(2,1)S(1)}, u32[]{:S(2)}) copy-start(bf16[2,1,384,384]{2,3,0,1:T(8,128)(2,1)S(1)} %fusion.106) | copy-start | bytes 1769476
  90.7 9.0 %collective-permute-start = (bf16[2,1,384,384]{2,3,0,1:T(8,128)(2,1)S(1)}, bf16[2,1,384,384]{2,3,0,1:T(8,128)(2,1)}, u32[]{:S(2)}, u32[]{:S(2)}) collective-permute-start(bf16[2,1,384,384]{2,3,0,1:T(8,128)(2,1)S(1)} %fusion.106), channel_id=1, source_target_pairs={{0,1},{1,0},{2,3},{3,2},{4,5},{5,4},{6,7},{7,6},{8,9},{9,8},{10,11... | collective-permute-start | bytes 1769480 | tf_op jit(solution)/shard_map/ppermute | solution.py:249
  91.0 22.7 %all-to-all-start.2 = ((f32[32,1,4096]{2,1,0:T(1,128)}), f32[32,1,4096]{2,1,0:T(1,128)S(1)}, u32[]{:S(2)}, u32[]{:S(2)}) async-start(f32[32,1,4096]{2,1,0:T(1,128)} %bitcast.160), calls=%async_computation.2 | async-start | bytes 1048576 | tf_op jit(solution)/shard_map/all_to_all | solution.py:230
  101.1 19.1 %collective-permute-start.1 = (bf16[2,1,384,384]{2,3,0,1:T(8,128)(2,1)S(1)}, bf16[2,1,384,384]{2,3,0,1:T(8,128)(2,1)}, u32[]{:S(2)}, u32[]{:S(2)}) collective-permute-start(bf16[2,1,384,384]{2,3,0,1:T(8,128)(2,1)S(1)} %add_convert_fusion.1), channel_id=1, source_target_pairs={{0,2},{1,3},{2,0},{3,1},{4,6},{5,7},{6,4},{7,5},{8,10},{9,11},{10,... | collective-permute-start | bytes 1769480 | tf_op jit(solution)/shard_map/ppermute | solution.py:249
  115.3 18.9 %all-to-all-start.3 = ((f32[32,1,4096]{2,1,0:T(1,128)}), f32[32,1,4096]{2,1,0:T(1,128)}, u32[]{:S(2)}, u32[]{:S(2)}) async-start(f32[32,1,4096]{2,1,0:T(1,128)} %broadcast_in_dim.10), calls=%async_computation.3 | async-start | bytes 1048576 | tf_op jit(solution)/shard_map/all_to_all | solution.py:237
  125.3 10.6 %copy-start.3 = (f32[4,2,128,128]{3,2,1,0:T(8,128)S(1)}, f32[4,2,128,128]{3,2,1,0:T(8,128)}, u32[]{:S(2)}) copy-start(f32[4,2,128,128]{3,2,1,0:T(8,128)} %probe_ref.1) | copy-start | bytes 1572868
  149.8 22.5 %all-to-all-start.4 = ((f32[32,1,4096]{2,1,0:T(1,128)}), f32[32,1,4096]{2,1,0:T(1,128)}, u32[]{:S(2)}, u32[]{:S(2)}) async-start(f32[32,1,4096]{2,1,0:T(1,128)} %bitcast.161), calls=%async_computation.4 | async-start | bytes 1048576 | tf_op jit(solution)/shard_map/all_to_all | solution.py:230
  162.7 15.5 %copy-start.1 = (f32[4,2,128,128]{3,2,1,0:T(8,128)S(1)}, f32[4,2,128,128]{3,2,1,0:T(8,128)}, u32[]{:S(2)}) copy-start(f32[4,2,128,128]{3,2,1,0:T(8,128)} %add.263.probe_ref) | copy-start | bytes 1572868
  162.7 2.2 %collective-permute-start.2 = (bf16[2,1,384,384]{2,3,0,1:T(8,128)(2,1)}, bf16[2,1,384,384]{2,3,0,1:T(8,128)(2,1)S(1)}, u32[]{:S(2)}, u32[]{:S(2)}) collective-permute-start(bf16[2,1,384,384]{2,3,0,1:T(8,128)(2,1)} %fusion.113), channel_id=1, source_target_pairs={{0,1},{1,0},{2,3},{3,2},{4,5},{5,4},{6,7},{7,6},{8,9},{9,8},{10,11... | collective-permute-start | bytes 1769480 | tf_op jit(solution)/shard_map/ppermute | solution.py:249
  167.0 19.6 %collective-permute-start.3 = (bf16[2,1,384,384]{2,3,0,1:T(8,128)(2,1)}, bf16[2,1,384,384]{2,3,0,1:T(8,128)(2,1)}, u32[]{:S(2)}, u32[]{:S(2)}) collective-permute-start(bf16[2,1,384,384]{2,3,0,1:T(8,128)(2,1)} %add_convert_fusion), channel_id=1, source_target_pairs={{0,2},{1,3},{2,0},{3,1},{4,6},{5,7},{6,4},{7,5},{8,10},{9,11},{10,... | collective-permute-start | bytes 1769480 | tf_op jit(solution)/shard_map/ppermute | solution.py:249
  174.9 18.9 %all-to-all-start.5 = ((f32[32,1,4096]{2,1,0:T(1,128)}), f32[32,1,4096]{2,1,0:T(1,128)}, u32[]{:S(2)}, u32[]{:S(2)}) async-start(f32[32,1,4096]{2,1,0:T(1,128)} %broadcast_in_dim.11), calls=%async_computation.5 | async-start | bytes 1048576 | tf_op jit(solution)/shard_map/all_to_all | solution.py:237

commit v6 on v5

--- a/solution.py
+++ b/solution.py
@@ -208,11 +208,9 @@
     return payload.reshape(steps, tile_count, capacity, length + 8, length)
 
 
-def exchange(payload, size):
-    tile_count, capacity, rows, length = payload.shape
-    arrived = lax.all_to_all(payload, "tile", 0, 0, tiled=True).reshape(
-        tile_count * capacity, rows, length
-    )
+def unpack(arrived, size):
+    tile_count, capacity, rows, length = arrived.shape
+    arrived = arrived.reshape(tile_count * capacity, rows, length)
     meta = arrived[:, length, :4].astype(jnp.int32)
     meta_in = jnp.stack([meta[:, 0] * size + meta[:, 1], meta[:, 2], meta[:, 3]], axis=1)
     return arrived, meta_in
@@ -329,8 +327,9 @@
     payload = route(amplitudes, batch_ids, scan_tile, scan_offset, tiles_here)
     tiles_now = object_tiles
     probe_now = probe
+    arrived = lax.all_to_all(jnp.swapaxes(payload, 0, 1), "tile", 0, 0, tiled=True)
     for step_no in range(batch_ids.shape[0]):
-        amp_in, meta_in = exchange(payload[step_no], size)
+        amp_in, meta_in = unpack(arrived[:, step_no], size)
         tiles_now, probe_now, _ = one_step(tiles_now, probe_now, amp_in, meta_in, tables, batch_total)
     return (tiles_now, probe_now)
 

time: 198 us -> 193 us (0.975)
  blocking collectives: 29.1 us -> 0 us
  waiting for transfers between devices: 45.7 us -> 64 us
  starting transfers between devices: 28.8 us -> 33.7 us
  local copies, waits for them, and re-layouts: 10.4 us -> 12.7 us
    all_to_all x1 -> x0, blocking collectives: 29.1 us -> none  [exchange(): lax.all_to_all(payload, 'tile', 0, 0, tiled=True)]
    all_to_all x1, waiting for transfers between devices: 15.9 us -> 34.4 us  [on_device(): lax.all_to_all(jnp.swapaxes(payload, 0, 1), 'tile', 0, 0, tiled=True)]
    all_to_all x1, starting transfers between devices: 4.22 us -> 7.28 us  [on_device(): lax.all_to_all(jnp.swapaxes(payload, 0, 1), 'tile', 0, 0, tiled=True)]
    unnamed x16 -> x26, local copies, waits for them, and re-layouts: 5.43 us -> 7.34 us
  transfers between devices with their start and end apart: 9 -> 9, of which waited for: 8 -> 8; matrix products, arithmetic and copies ran while one was open for 19% -> 20% of each run, Pallas kernels for 0% -> 0%
where the time goes in v6:
time: 193 us; the launch traced here: 192 us
  waiting for transfers between devices  64 us (33%)
  starting transfers between devices  33.7 us (17%)
  other arithmetic  27.7 us (14%)
  matrix products  26.8 us (14%)
  Pallas kernels  26 us (13%)
  local copies, waits for them, and re-layouts  12.7 us (7%)
    all_to_all x1, waiting for transfers between devices, on_device(): lax.all_to_all(jnp.swapaxes(payload, 0, 1), 'tile', 0, 0, tiled=True)  34.4 us
    pallas_call x2, Pallas kernels, entries_kernel(): pl.pallas_call(entry_kernel, grid_spec=grid_spec, out_shape=[jax.ShapeDty...  26 us
    all_to_all x2, starting transfers between devices, sum_over(): lax.all_to_all(value.astype(send_type).reshape(count, -1), axes, 0, 0, ti...  15.8 us
    all_to_all x2, waiting for transfers between devices, sum_over(): lax.all_to_all(value.astype(send_type).reshape(count, -1), axes, 0, 0, ti...  14 us
    dot_general x2, matrix products, entries_pass(): jnp.einsum('skq,xskc->xqc', pick_rows, spread, preferred_element_type=jnp...  11.4 us
    ppermute x4, waiting for transfers between devices, all_sum_pairs(): other = lax.ppermute(total.astype(send_type), axis, pairs)  9.94 us
    dot_general x2, matrix products, entries_pass(): jnp.einsum('skq,xqc->xskc', pick_rows, stacked, preferred_element_type=jn...  9.49 us
    unnamed x26, local copies, waits for them, and re-layouts  7.34 us
  transfers between devices with their start and end apart: 9, of which 8 were waited for; matrix products, arithmetic and copies ran while one was open for 20% of the time, Pallas kernels for 0%

profile of v6, /device:TPU:0, one launch (start us, length us, event | category | flops | bytes accessed | tf_op | source)
XLA Modules:
  0.0 192.0 jit_solution(8623193953306150934)
XLA Ops:
  7.8 7.3 %all-to-all-start = ((bf16[8,2,3,136,128]{4,3,2,1,0:T(8,128)(2,1)}), bf16[8,2,3,136,128]{4,3,2,1,0:T(8,128)(2,1)S(1)}, u32[]{:S(2)}, u32[]{:S(2)}) async-start(bf16[8,2,3,136,128]{4,3,2,1,0:T(8,128)(2,1)} %copy.96), calls=%async_computation | async-start | bytes 3342336 | tf_op jit(solution)/shard_map/all_to_all | solution.py:330
  15.1 2.7 %copy.101 = f32[2,1,384,384]{2,3,0,1:T(8,128)} copy(f32[2,1,384,384]{3,2,1,0:T(8,128)} %param.10) | data formatting | bytes 2359296 | tf_op args[4]
  19.8 34.4 %all-to-all-done = bf16[8,2,3,136,128]{4,3,2,1,0:T(8,128)(2,1)S(1)} async-done(((bf16[8,2,3,136,128]{4,3,2,1,0:T(8,128)(2,1)}), bf16[8,2,3,136,128]{4,3,2,1,0:T(8,128)(2,1)S(1)}, u32[]{:S(2)}, u32[]{:S(2)}) %all-to-all-start) | async-done | bytes 1671200 | tf_op jit(solution)/shard_map/all_to_all | solution.py:330
  57.9 4.4 %convert_bitcast_fusion.1 = bf16[2,24,128,384]{3,2,0,1:T(8,128)(2,1)S(1)} fusion(s32[24,128]{1,0:T(8,128)S(1)} %get-tuple-element.38, pred[24]{0:T(512)(128)(4,1)S(1)} %reduce.4, f32[2,1,384,384]{3,2,1,0:T(8,128)} %param.10), kind=kOutput, calls=%fused_computation.14 | convolution fusion | flops 1816952832 | bytes 5910552 | tf_op jit(solution)/shard_map/skq,xqc->xskc/dot_general | solution.py:268
  63.6 2.6 %fusion.71.patch_ref = bf16[2,24,128,128]{3,2,1,0:T(8,128)(2,1)} fusion(bf16[2,24,128,384]{3,2,0,1:T(8,128)(2,1)S(1)} %convert_bitcast_fusion.1, s32[24,128]{1,0:T(8,128)S(1)} %get-tuple-element.39), kind=kOutput, calls=%fused_computation.45 | convolution fusion | flops 605945856 | bytes 6303744 | tf_op jit(solution)/shard_map/xskc,scl->xskl/dot_general | solution.py:271
  66.3 13.0 %shard_map.77 = (bf16[2,24,128,128]{3,2,1,0:T(8,128)(2,1)}, f32[4,2,128,128]{3,2,1,0:T(8,128)}) custom-call(s32[25]{0:T(128)} %pad_add_fusion.order_ref, bf16[2,24,128,128]{3,2,1,0:T(8,128)(2,1)} %fusion.71.patch_ref, bf16[24,136,128]{2,1,0:T(8,128)(2,1)} %bitcast.161, f32[4,2,128,128]{3,2,1,0:T(8,128)} %probe_ref.1, ...), custom_call_target="tpu_custom_call" | custom-call | flops 6442450944 | bytes 4980736 | tf_op jit(solution)/shard_map/pallas_call | solution.py:169
  79.3 5.3 %fusion.104 = bf16[2,1,384,384]{2,3,0,1:T(8,128)(2,1)S(1)} fusion(s32[24,128]{1,0:T(8,128)S(1)} %get-tuple-element.38, pred[24]{0:T(512)(128)(4,1)S(1)} %reduce.4, bf16[2,24,128,128]{3,2,1,0:T(8,128)(2,1)} %get-tuple-element.6, s32[24,128]{1,0:T(8,128)S(1)} %get-tuple-element.39), kind=kOutput, calls=%fused_computation.50 | convolution fusion | flops 2422112256 | bytes 2187288 | tf_op jit(solution)/shard_map/skq,xskc->xqc/dot_general | solution.py:289
  84.9 8.2 %all-to-all-start.1 = ((f32[32,1,4096]{2,1,0:T(1,128)}), f32[32,1,4096]{2,1,0:T(1,128)S(1)}, u32[]{:S(2)}, u32[]{:S(2)}) async-start(f32[32,1,4096]{2,1,0:T(1,128)} %bitcast.38), calls=%async_computation.1 | async-start | bytes 1048576 | tf_op jit(solution)/shard_map/all_to_all | solution.py:228
  96.2 1.8 collective-permute-start.1
  98.2 10.5 %all-to-all-done.1 = f32[32,1,4096]{2,1,0:T(1,128)S(1)} async-done(((f32[32,1,4096]{2,1,0:T(1,128)}), f32[32,1,4096]{2,1,0:T(1,128)S(1)}, u32[]{:S(2)}, u32[]{:S(2)}) %all-to-all-start.1) | async-done | bytes 524320 | tf_op jit(solution)/shard_map/all_to_all | solution.py:228
  110.3 3.5 %all-to-all-start.2 = ((f32[32,1,4096]{2,1,0:T(1,128)}), f32[32,1,4096]{2,1,0:T(1,128)}, u32[]{:S(2)}, u32[]{:S(2)}) async-start(f32[32,1,4096]{2,1,0:T(1,128)} %broadcast_in_dim.10), calls=%async_computation.2 | async-start | bytes 1048576 | tf_op jit(solution)/shard_map/all_to_all | solution.py:235
  115.3 5.1 %convert_bitcast_fusion = bf16[2,24,128,384]{2,3,0,1:T(8,128)(2,1)S(1)} fusion(s32[24,128]{1,0:T(8,128)S(1)} %iota_add_fusion, pred[24]{0:T(512)(128)(4,1)S(1)} %reduce.6, f32[2,1,384,384]{2,3,0,1:T(8,128)S(1)} %copy-done.2, bf16[2,1,384,384]{2,3,0,1:T(8,128)(2,1)} %collective-permute-done.1, bf16[2,1,384,384]{2,3,0,1:T(8,128)(2,1)S(1)} %add_convert_fusion.1, ...), kind=kOutput, calls=%fused_computation.10 | convolution fusion | flops 1818427392 | bytes 7090204 | tf_op jit(solution)/shard_map/skq,xqc->xskc/dot_general | solution.py:268
  120.4 3.3 %fusion.66.patch_ref = bf16[2,24,128,128]{3,2,1,0:T(8,128)(2,1)} fusion(bf16[2,24,128,384]{2,3,0,1:T(8,128)(2,1)S(1)} %convert_bitcast_fusion, s32[24,128]{1,0:T(8,128)S(1)} %iota_add_fusion.1), kind=kOutput, calls=%fused_computation.44 | convolution fusion | flops 605945856 | bytes 6303744 | tf_op jit(solution)/shard_map/xskc,scl->xskl/dot_general | solution.py:271
  123.7 5.5 %all-to-all-done.2 = f32[32,1,4096]{2,1,0:T(1,128)} async-done(((f32[32,1,4096]{2,1,0:T(1,128)}), f32[32,1,4096]{2,1,0:T(1,128)}, u32[]{:S(2)}, u32[]{:S(2)}) %all-to-all-start.2) | async-done | bytes 524320 | tf_op jit(solution)/shard_map/all_to_all | solution.py:235
  131.7 13.0 %shard_map.78 = (bf16[2,24,128,128]{3,2,1,0:T(8,128)(2,1)}, f32[4,2,128,128]{3,2,1,0:T(8,128)}) custom-call(s32[25]{0:T(128)} %pad_add_fusion.1.order_ref, bf16[2,24,128,128]{3,2,1,0:T(8,128)(2,1)} %fusion.66.patch_ref, bf16[24,136,128]{2,1,0:T(8,128)(2,1)} %bitcast.159, f32[4,2,128,128]{3,2,1,0:T(8,128)} %add.263.probe_ref, ...), custom_call_target="tpu_custom_call" | custom-call | flops 6442450944 | bytes 4980736 | tf_op jit(solution)/shard_map/pallas_call | solution.py:169
  144.8 7.6 %all-to-all-start.3 = ((f32[32,1,4096]{2,1,0:T(1,128)}), f32[32,1,4096]{2,1,0:T(1,128)}, u32[]{:S(2)}, u32[]{:S(2)}) async-start(f32[32,1,4096]{2,1,0:T(1,128)} %bitcast.162), calls=%async_computation.3 | async-start | bytes 1048576 | tf_op jit(solution)/shard_map/all_to_all | solution.py:228
  152.4 6.1 %fusion.111 = bf16[2,1,384,384]{2,3,0,1:T(8,128)(2,1)} fusion(s32[24,128]{1,0:T(8,128)S(1)} %iota_add_fusion, pred[24]{0:T(512)(128)(4,1)S(1)} %reduce.6, bf16[2,24,128,128]{3,2,1,0:T(8,128)(2,1)} %get-tuple-element.8, s32[24,128]{1,0:T(8,128)S(1)} %iota_add_fusion.1), kind=kOutput, calls=%fused_computation.51 | convolution fusion | flops 2422112256 | bytes 2187288 | tf_op jit(solution)/shard_map/skq,xskc->xqc/dot_general | solution.py:289
  158.7 2.0 %collective-permute-done.2 = bf16[2,1,384,384]{2,3,0,1:T(8,128)(2,1)S(1)} collective-permute-done((bf16[2,1,384,384]{2,3,0,1:T(8,128)(2,1)}, bf16[2,1,384,384]{2,3,0,1:T(8,128)(2,1)S(1)}, u32[]{:S(2)}, u32[]{:S(2)}) %collective-permute-start.2) | collective-permute-done | bytes 589856 | tf_op jit(solution)/shard_map/ppermute | solution.py:247
  160.7 2.0 %add_convert_fusion = bf16[2,1,384,384]{2,3,0,1:T(8,128)(2,1)} fusion(bf16[2,1,384,384]{2,3,0,1:T(8,128)(2,1)S(1)} %collective-permute-done.2, bf16[2,1,384,384]{2,3,0,1:T(8,128)(2,1)} %fusion.111), kind=kLoop, calls=%fused_computation.53 | loop fusion | flops 1179648 | bytes 1769472 | tf_op jit(solution)/shard_map/convert_element_type | solution.py:248
  164.4 3.5 %all-to-all-done.3 = f32[32,1,4096]{2,1,0:T(1,128)} async-done(((f32[32,1,4096]{2,1,0:T(1,128)}), f32[32,1,4096]{2,1,0:T(1,128)}, u32[]{:S(2)}, u32[]{:S(2)}) %all-to-all-start.3) | async-done | bytes 524320 | tf_op jit(solution)/shard_map/all_to_all | solution.py:228
  170.6 3.3 %all-to-all-start.4 = ((f32[32,1,4096]{2,1,0:T(1,128)}), f32[32,1,4096]{2,1,0:T(1,128)}, u32[]{:S(2)}, u32[]{:S(2)}) async-start(f32[32,1,4096]{2,1,0:T(1,128)} %broadcast_in_dim.11), calls=%async_computation.4 | async-start | bytes 1048576 | tf_op jit(solution)/shard_map/all_to_all | solution.py:235
  174.6 7.8 %collective-permute-done.3 = bf16[2,1,384,384]{2,3,0,1:T(8,128)(2,1)} collective-permute-done((bf16[2,1,384,384]{2,3,0,1:T(8,128)(2,1)}, bf16[2,1,384,384]{2,3,0,1:T(8,128)(2,1)}, u32[]{:S(2)}, u32[]{:S(2)}) %collective-permute-start.3) | collective-permute-done | bytes 589856 | tf_op jit(solution)/shard_map/ppermute | solution.py:247
  182.3 4.1 %divide_add_fusion = f32[2,1,384,384]{2,3,0,1:T(8,128)} fusion(bf16[2,1,384,384]{2,3,0,1:T(8,128)(2,1)} %collective-permute-done.3, bf16[2,1,384,384]{2,3,0,1:T(8,128)(2,1)} %add_convert_fusion, f32[]{:T(128)} %reduce_max.19, f32[2,1,384,384]{2,3,0,1:T(8,128)S(1)} %copy-done.2, f32[]{:T(128)} %reduce_max.18, ...), kind=kLoop, calls=%fused_computation.52 | loop fusion | flops 2949120 | bytes 4718600 | tf_op jit(solution)/shard_map/add | solution.py:317
  186.5 2.7 %copy.109 = f32[2,1,384,384]{3,2,1,0:T(8,128)} copy(f32[2,1,384,384]{2,3,0,1:T(8,128)} %divide_add_fusion) | data formatting | bytes 2359296
  (95 shorter events, 31.3 us)
Async XLA Ops:
  0.6 4.8 %copy-start = (bf16[32,128,128]{2,1,0:T(8,128)(2,1)S(1)}, bf16[32,128,128]{2,1,0:T(8,128)(2,1)}, u32[]{:S(2)}) copy-start(bf16[32,128,128]{2,1,0:T(8,128)(2,1)} %param.6) | copy-start | bytes 3145732
  7.8 46.4 %all-to-all-start = ((bf16[8,2,3,136,128]{4,3,2,1,0:T(8,128)(2,1)}), bf16[8,2,3,136,128]{4,3,2,1,0:T(8,128)(2,1)S(1)}, u32[]{:S(2)}, u32[]{:S(2)}) async-start(bf16[8,2,3,136,128]{4,3,2,1,0:T(8,128)(2,1)} %copy.96), calls=%async_computation | async-start | bytes 3342336 | tf_op jit(solution)/shard_map/all_to_all | solution.py:330
  15.1 2.7 %copy-start.3 = (f32[4,2,128,128]{3,2,1,0:T(8,128)S(1)}, f32[4,2,128,128]{3,2,1,0:T(8,128)}, u32[]{:S(2)}) copy-start(f32[4,2,128,128]{3,2,1,0:T(8,128)} %probe_ref.1) | copy-start | bytes 1572868
  54.3 0.9 copy-start.5
  54.3 8.0 %copy-start.6 = (bf16[8,1,3,136,128]{4,3,2,1,0:T(8,128)(2,1)}, bf16[8,1,3,136,128]{4,3,2,1,0:T(8,128)(2,1)S(1)}, u32[]{:S(2)}) copy-start(bf16[8,1,3,136,128]{4,3,2,1,0:T(8,128)(2,1)S(1)} %get-tuple-element.28) | copy-start | bytes 2506756
  84.6 10.1 %copy-start.7 = (bf16[2,1,384,384]{2,3,0,1:T(8,128)(2,1)}, bf16[2,1,384,384]{2,3,0,1:T(8,128)(2,1)S(1)}, u32[]{:S(2)}) copy-start(bf16[2,1,384,384]{2,3,0,1:T(8,128)(2,1)S(1)} %fusion.104) | copy-start | bytes 1769476
  84.6 13.5 %copy-start.9 = (s32[24]{0:T(128)S(1)}, s32[24]{0:T(128)}, u32[]{:S(2)}) copy-start(s32[24]{0:T(128)} %get-tuple-element.33) | copy-start | bytes 292
  84.6 13.6 %copy-start.8 = (s32[24]{0:T(128)S(1)}, s32[24]{0:T(128)}, u32[]{:S(2)}) copy-start(s32[24]{0:T(128)} %get-tuple-element.32) | copy-start | bytes 292
  84.6 10.1 %collective-permute-start = (bf16[2,1,384,384]{2,3,0,1:T(8,128)(2,1)S(1)}, bf16[2,1,384,384]{2,3,0,1:T(8,128)(2,1)}, u32[]{:S(2)}, u32[]{:S(2)}) collective-permute-start(bf16[2,1,384,384]{2,3,0,1:T(8,128)(2,1)S(1)} %fusion.104), channel_id=1, source_target_pairs={{0,1},{1,0},{2,3},{3,2},{4,5},{5,4},{6,7},{7,6},{8,9},{9,8},{10,11... | collective-permute-start | bytes 1769480 | tf_op jit(solution)/shard_map/ppermute | solution.py:247
  84.9 23.8 %all-to-all-start.1 = ((f32[32,1,4096]{2,1,0:T(1,128)}), f32[32,1,4096]{2,1,0:T(1,128)S(1)}, u32[]{:S(2)}, u32[]{:S(2)}) async-start(f32[32,1,4096]{2,1,0:T(1,128)} %bitcast.38), calls=%async_computation.1 | async-start | bytes 1048576 | tf_op jit(solution)/shard_map/all_to_all | solution.py:228
  94.7 20.6 %copy-start.2 = (f32[2,1,384,384]{2,3,0,1:T(8,128)S(1)}, f32[2,1,384,384]{2,3,0,1:T(8,128)}, u32[]{:S(2)}) copy-start(f32[2,1,384,384]{2,3,0,1:T(8,128)} %copy.101) | copy-start | bytes 3538948
  96.2 19.1 %collective-permute-start.1 = (bf16[2,1,384,384]{2,3,0,1:T(8,128)(2,1)S(1)}, bf16[2,1,384,384]{2,3,0,1:T(8,128)(2,1)}, u32[]{:S(2)}, u32[]{:S(2)}) collective-permute-start(bf16[2,1,384,384]{2,3,0,1:T(8,128)(2,1)S(1)} %add_convert_fusion.1), channel_id=1, source_target_pairs={{0,2},{1,3},{2,0},{3,1},{4,6},{5,7},{6,4},{7,5},{8,10},{9,11},{10,... | collective-permute-start | bytes 1769480 | tf_op jit(solution)/shard_map/ppermute | solution.py:247
  110.3 18.9 %all-to-all-start.2 = ((f32[32,1,4096]{2,1,0:T(1,128)}), f32[32,1,4096]{2,1,0:T(1,128)}, u32[]{:S(2)}, u32[]{:S(2)}) async-start(f32[32,1,4096]{2,1,0:T(1,128)} %broadcast_in_dim.10), calls=%async_computation.2 | async-start | bytes 1048576 | tf_op jit(solution)/shard_map/all_to_all | solution.py:235
  120.4 10.5 %copy-start.4 = (f32[4,2,128,128]{3,2,1,0:T(8,128)S(1)}, f32[4,2,128,128]{3,2,1,0:T(8,128)}, u32[]{:S(2)}) copy-start(f32[4,2,128,128]{3,2,1,0:T(8,128)} %probe_ref.1) | copy-start | bytes 1572868
  144.8 23.1 %all-to-all-start.3 = ((f32[32,1,4096]{2,1,0:T(1,128)}), f32[32,1,4096]{2,1,0:T(1,128)}, u32[]{:S(2)}, u32[]{:S(2)}) async-start(f32[32,1,4096]{2,1,0:T(1,128)} %bitcast.162), calls=%async_computation.3 | async-start | bytes 1048576 | tf_op jit(solution)/shard_map/all_to_all | solution.py:228
  158.5 15.4 %copy-start.1 = (f32[4,2,128,128]{3,2,1,0:T(8,128)S(1)}, f32[4,2,128,128]{3,2,1,0:T(8,128)}, u32[]{:S(2)}) copy-start(f32[4,2,128,128]{3,2,1,0:T(8,128)} %add.263.probe_ref) | copy-start | bytes 1572868
  158.5 2.2 %collective-permute-start.2 = (bf16[2,1,384,384]{2,3,0,1:T(8,128)(2,1)}, bf16[2,1,384,384]{2,3,0,1:T(8,128)(2,1)S(1)}, u32[]{:S(2)}, u32[]{:S(2)}) collective-permute-start(bf16[2,1,384,384]{2,3,0,1:T(8,128)(2,1)} %fusion.111), channel_id=1, source_target_pairs={{0,1},{1,0},{2,3},{3,2},{4,5},{5,4},{6,7},{7,6},{8,9},{9,8},{10,11... | collective-permute-start | bytes 1769480 | tf_op jit(solution)/shard_map/ppermute | solution.py:247
  162.7 19.6 %collective-permute-start.3 = (bf16[2,1,384,384]{2,3,0,1:T(8,128)(2,1)}, bf16[2,1,384,384]{2,3,0,1:T(8,128)(2,1)}, u32[]{:S(2)}, u32[]{:S(2)}) collective-permute-start(bf16[2,1,384,384]{2,3,0,1:T(8,128)(2,1)} %add_convert_fusion), channel_id=1, source_target_pairs={{0,2},{1,3},{2,0},{3,1},{4,6},{5,7},{6,4},{7,5},{8,10},{9,11},{10,... | collective-permute-start | bytes 1769480 | tf_op jit(solution)/shard_map/ppermute | solution.py:247
  170.6 18.9 %all-to-all-start.4 = ((f32[32,1,4096]{2,1,0:T(1,128)}), f32[32,1,4096]{2,1,0:T(1,128)}, u32[]{:S(2)}, u32[]{:S(2)}) async-start(f32[32,1,4096]{2,1,0:T(1,128)} %broadcast_in_dim.11), calls=%async_computation.4 | async-start | bytes 1048576 | tf_op jit(solution)/shard_map/all_to_all | solution.py:235

commit v7 on v6

--- a/solution.py
+++ b/solution.py
@@ -48,28 +48,55 @@
     return left, right
 
 
-def entry_kernel(order_ref, patch_ref, amp_ref, probe_ref, left_ref, right_ref, update_ref, grad_ref):
-    slots = order_ref.shape[0] - 1
-    count = order_ref[slots]
+def entry_kernel(table_ref, tile_ref, amp_ref, probe_ref, left_ref, right_ref, sum_ref, grad_ref):
+    slots = amp_ref.shape[0]
+    count = table_ref[slots]
     group = 2 if slots % 2 == 0 else 1
     grad_ref[...] = jnp.zeros(grad_ref.shape, grad_ref.dtype)
-    update_ref[...] = jnp.zeros(update_ref.shape, update_ref.dtype)
+    sum_ref[...] = jnp.zeros(sum_ref.shape, sum_ref.dtype)
 
     def one_group(index, carry):
-        chosen = [order_ref[index * group + g] for g in range(group)]
-        entry_body(chosen, patch_ref, amp_ref, probe_ref, left_ref, right_ref, update_ref, grad_ref)
+        chosen = [table_ref[index * group + g] for g in range(group)]
+        entry_body(chosen, table_ref, tile_ref, amp_ref, probe_ref, left_ref, right_ref, sum_ref, grad_ref)
         return carry
 
     lax.fori_loop(0, (count + group - 1) // group, one_group, 0)
 
 
-def entry_body(chosen, patch_ref, amp_ref, probe_ref, left_ref, right_ref, update_ref, grad_ref):
+def one_hot(shape, offset, keep=None):
+    rows = lax.broadcasted_iota(jnp.int32, shape, 0)
+    cols = lax.broadcasted_iota(jnp.int32, shape, 1)
+    hit = cols - rows == offset
+    if keep is not None:
+        hit = hit & keep
+    return jnp.where(hit, 1.0, 0.0).astype(jnp.bfloat16)
+
+
+def entry_body(chosen, table_ref, tile_ref, amp_ref, probe_ref, left_ref, right_ref, sum_ref, grad_ref):
     modes, length = probe_ref.shape[0], probe_ref.shape[-1]
+    slots = amp_ref.shape[0]
+    rows_all, size = tile_ref.shape[1], tile_ref.shape[2]
+    window = length + 16
     blocks = len(chosen) * modes
-    patches = [
-        (patch_ref[0, slot].astype(jnp.float32), patch_ref[1, slot].astype(jnp.float32))
-        for slot in chosen
-    ]
+    places, patches = [], []
+    for slot in chosen:
+        row = table_ref[slots + 1 + slot]
+        col = table_ref[2 * slots + 1 + slot]
+        keep = table_ref[3 * slots + 1 + slot] != 0
+        base = jnp.minimum((row // 8) * 8, rows_all - window)
+        shift = row - base
+        pick_rows = one_hot((length, window), shift, keep)
+        pick_cols = one_hot((size, length), -col)
+        spread_cols = one_hot((length, size), col)
+        spread_rows = one_hot((window, length), -shift, keep)
+        start = pl.multiple_of(base, 8)
+        parts = []
+        for x in range(2):
+            near = tile_ref[x, pl.ds(start, window), :].astype(jnp.bfloat16)
+            rows = jnp.dot(pick_rows, near, preferred_element_type=jnp.float32).astype(jnp.bfloat16)
+            parts.append(jnp.dot(rows, pick_cols, preferred_element_type=jnp.float32))
+        places.append((start, spread_cols, spread_rows))
+        patches.append(tuple(parts))
     left = left_ref[...]
     right = right_ref[...]
     exits_re, exits_im = [], []
@@ -148,17 +175,25 @@
                 grads[m] = [grad_re, grad_im]
             else:
                 grads[m] = [grads[m][0] + grad_re, grads[m][1] + grad_im]
-        update_ref[0, slot] = update_re.astype(update_ref.dtype)
-        update_ref[1, slot] = update_im.astype(update_ref.dtype)
+        start, spread_cols, spread_rows = places[g]
+        for x, update in enumerate((update_re, update_im)):
+            wide = jnp.dot(
+                update.astype(jnp.bfloat16), spread_cols, preferred_element_type=jnp.float32
+            ).astype(jnp.bfloat16)
+            sum_ref[x, pl.ds(start, window), :] += jnp.dot(
+                spread_rows, wide, preferred_element_type=jnp.float32
+            )
     for m in range(modes):
         grad_ref[m, 0] += grads[m][0]
         grad_ref[m, 1] += grads[m][1]
 
 
-def entries_kernel(order, patch, amp_in, probe_now, left, right):
+def entries_kernel(table, tile, amp_in, probe_now, left, right):
     slots, length = amp_in.shape[0], amp_in.shape[-1]
     modes = probe_now.shape[0]
+    rows_all, size = tile.shape[1], tile.shape[2]
     flops = slots * 4 * 2 * (2 * length) * (2 * length) * (modes * length)
+    flops += slots * 8 * 2 * length * (length + 16) * size
     whole = pl.BlockSpec(memory_space=pltpu.VMEM)
     grid_spec = pltpu.PrefetchScalarGridSpec(
         num_scalar_prefetch=1,
@@ -170,16 +205,16 @@
         entry_kernel,
         grid_spec=grid_spec,
         out_shape=[
-            jax.ShapeDtypeStruct((2, slots, length, length), jnp.bfloat16),
+            jax.ShapeDtypeStruct(tile.shape, jnp.float32),
             jax.ShapeDtypeStruct(probe_now.shape, jnp.float32),
         ],
         compiler_params=pltpu.CompilerParams(dimension_semantics=("arbitrary",)),
         cost_estimate=pl.CostEstimate(
             flops=flops,
             transcendentals=slots * length * length,
-            bytes_accessed=slots * length * length * 10 + probe_now.size * 8,
+            bytes_accessed=slots * length * length * 2 + tile.size * 8 + probe_now.size * 8,
         ),
-    )(order, patch, amp_in, probe_now, left, right)
+    )(table, tile, amp_in, probe_now, left, right)
 
 
 def route(amplitudes, batch_ids, scan_tile, scan_offset, tiles_here):
@@ -251,24 +286,7 @@
 
 
 def entries_pass(stacked, probe_now, amp_in, meta_in, tables):
-    table_re, table_im, table_neg = tables
-    length = probe_now.shape[-1]
-    rows_all, size = stacked.shape[1], stacked.shape[2]
-    within = jnp.arange(length, dtype=jnp.int32)
     row_at, col_at, valid = meta_in[:, 0], meta_in[:, 1], meta_in[:, 2]
-    pick_rows = (
-        (row_at[:, None, None] + within[None, :, None])
-        == jnp.arange(rows_all, dtype=jnp.int32)[None, None, :]
-    ) & (valid[:, None, None] > 0)
-    pick_rows = pick_rows.astype(jnp.bfloat16)
-    pick_cols = (
-        (col_at[:, None, None] + within[None, None, :])
-        == jnp.arange(size, dtype=jnp.int32)[None, :, None]
-    ).astype(jnp.bfloat16)
-    rows = jnp.einsum(
-        "skq,xqc->xskc", pick_rows, stacked, preferred_element_type=jnp.float32
-    ).astype(jnp.bfloat16)
-    patch = jnp.einsum("xskc,scl->xskl", rows, pick_cols, preferred_element_type=jnp.float32)
     left, right = block_tables(tables[0], tables[1])
     held = (valid > 0).astype(jnp.int32)
     count = jnp.sum(held)
@@ -279,21 +297,14 @@
         * jnp.arange(slots, dtype=jnp.int32)[:, None],
         axis=0,
     )
-    order = jnp.concatenate([order, count[None]]).astype(jnp.int32)
-    update, probe_grad = entries_kernel(
-        order, patch.astype(jnp.bfloat16), amp_in, probe_now, left, right
-    )
-    spread = jnp.einsum(
-        "xskl,scl->xskc", update, pick_cols, preferred_element_type=jnp.float32
-    ).astype(jnp.bfloat16)
-    local_sum = jnp.einsum("skq,xskc->xqc", pick_rows, spread, preferred_element_type=jnp.float32)
-    return local_sum, probe_grad
+    table = jnp.concatenate([order, count[None], row_at, col_at, held]).astype(jnp.int32)
+    return entries_kernel(table, stacked, amp_in, probe_now, left, right)
 
 
 def one_step(tiles_now, probe_now, amp_in, meta_in, tables, batch_total):
     tiles_here, size = tiles_now.shape[1], tiles_now.shape[2]
     slots, length = amp_in.shape[0], amp_in.shape[-1]
-    stacked = tiles_now.astype(jnp.bfloat16).reshape(2, tiles_here * size, size)
+    stacked = tiles_now.reshape(2, tiles_here * size, size)
     chunk = max(d for d in range(1, min(slots, 24) + 1) if slots % d == 0)
     if chunk == slots:
         local_sum, probe_grad = entries_pass(stacked, probe_now, amp_in, meta_in, tables)

time: 193 us -> 221 us (1.15)
  starting transfers between devices: 33.7 us -> 66 us
  matrix products: 26.8 us -> 0 us
  waiting for transfers between devices: 64 us -> 86.9 us
  local copies, waits for them, and re-layouts: 12.7 us -> 9.93 us
  Pallas kernels: 26 us -> 28.6 us
    all_to_all x2, starting transfers between devices: 15.8 us -> 48.2 us  [sum_over(): lax.all_to_all(value.astype(send_type).reshape(count, -1), axes, 0, 0, ti...]
    dot_general x6 -> x0, matrix products: 26.8 us -> none  [the longest x2 11.4 us: entries_pass(): jnp.einsum('skq,xskc->xqc', pick_rows, spread, preferred_element_type=jnp...]
    all_to_all x2, waiting for transfers between devices: 14 us -> 21.7 us  [sum_over(): lax.all_to_all(value.astype(send_type).reshape(count, -1), axes, 0, 0, ti...]
    ppermute x4, waiting for transfers between devices: 9.94 us -> 16.6 us  [all_sum_pairs(): other = lax.ppermute(total.astype(send_type), axis, pairs)]
    unnamed x26 -> x22, local copies, waits for them, and re-layouts: 7.34 us -> 1.98 us
    all_to_all x2, waiting for transfers between devices: 5.77 us -> 10.8 us  [all_sum_a2a(): lax.all_to_all(jnp.broadcast_to(total, (count, total.shape[1])), axes, 0,...]
    add x6 -> x0, other arithmetic: 4.95 us -> none  [the longest x1 4.14 us: one_step(): tiles_next = tiles_now + summed / peak_power]
    unnamed x0 -> x1, other arithmetic: none -> 4.08 us
  transfers between devices with their start and end apart: 9 -> 9, of which waited for: 8 -> 6; matrix products, arithmetic and copies ran while one was open for 20% -> 10% of each run, Pallas kernels for 0% -> 0%
where the time goes in v7:
time: 221 us
  waiting for transfers between devices  86.9 us (39%)
  starting transfers between devices  66 us (30%)
  Pallas kernels  28.6 us (13%)
  other arithmetic  28.4 us (13%)
  local copies, waits for them, and re-layouts  9.93 us (4%)
    all_to_all x2, starting transfers between devices, sum_over(): lax.all_to_all(value.astype(send_type).reshape(count, -1), axes, 0, 0, ti...  48.2 us
    all_to_all x1, waiting for transfers between devices, on_device(): lax.all_to_all(jnp.swapaxes(payload, 0, 1), 'tile', 0, 0, tiled=True)  37.8 us
    pallas_call x2, Pallas kernels, entries_kernel(): pl.pallas_call(entry_kernel, grid_spec=grid_spec, out_shape=[jax.ShapeDty...  28.6 us
    all_to_all x2, waiting for transfers between devices, sum_over(): lax.all_to_all(value.astype(send_type).reshape(count, -1), axes, 0, 0, ti...  21.7 us
    ppermute x4, waiting for transfers between devices, all_sum_pairs(): other = lax.ppermute(total.astype(send_type), axis, pairs)  16.6 us
    all_to_all x2, waiting for transfers between devices, all_sum_a2a(): lax.all_to_all(jnp.broadcast_to(total, (count, total.shape[1])), axes, 0,...  10.8 us
    all_to_all x1, starting transfers between devices, on_device(): lax.all_to_all(jnp.swapaxes(payload, 0, 1), 'tile', 0, 0, tiled=True)  7.28 us
    all_to_all x2, starting transfers between devices, all_sum_a2a(): lax.all_to_all(jnp.broadcast_to(total, (count, total.shape[1])), axes, 0,...  6.66 us
  transfers between devices with their start and end apart: 9, of which 6 were waited for; matrix products, arithmetic and copies ran while one was open for 10% of the time, Pallas kernels for 0%

profile of v7, /device:TPU:0, one launch (start us, length us, event | category | flops | bytes accessed | tf_op | source)
XLA Modules:
  0.0 220.7 jit_solution(1891339701283746085)
XLA Ops:
  7.8 7.3 %all-to-all-start = ((bf16[8,2,3,136,128]{4,3,2,1,0:T(8,128)(2,1)}), bf16[8,2,3,136,128]{4,3,2,1,0:T(8,128)(2,1)S(1)}, u32[]{:S(2)}, u32[]{:S(2)}) async-start(bf16[8,2,3,136,128]{4,3,2,1,0:T(8,128)(2,1)} %copy.72), calls=%async_computation | async-start | bytes 3342336 | tf_op jit(solution)/shard_map/all_to_all | solution.py:341
  16.4 37.8 %all-to-all-done = bf16[8,2,3,136,128]{4,3,2,1,0:T(8,128)(2,1)S(1)} async-done(((bf16[8,2,3,136,128]{4,3,2,1,0:T(8,128)(2,1)}), bf16[8,2,3,136,128]{4,3,2,1,0:T(8,128)(2,1)S(1)}, u32[]{:S(2)}, u32[]{:S(2)}) %all-to-all-start) | async-done | bytes 1671200 | tf_op jit(solution)/shard_map/all_to_all | solution.py:341
  57.0 1.3 concatenate.41.table_ref
  58.3 14.3 %shard_map.77 = (f32[2,384,384]{2,1,0:T(8,128)}, f32[4,2,128,128]{3,2,1,0:T(8,128)}) custom-call(s32[97]{0:T(128)} %concatenate.41.table_ref, f32[2,384,384]{2,1,0:T(8,128)} %bitcast.49, bf16[24,136,128]{2,1,0:T(8,128)(2,1)} %bitcast.55, f32[4,2,128,128]{3,2,1,0:T(8,128)} %probe_ref.1, bf16[256,256]{1,0:T(8,128)(2,1)} %get-tuple-element.35.left_ref, ...), custom_call_target="tpu_custom_call" | custom-call | flops 9160359936 | bytes 4194304 | tf_op jit(solution)/shard_map/pallas_call | solution.py:204
  72.6 23.1 %all-to-all-start.1 = ((f32[32,1,4096]{2,1,0:T(1,128)}), f32[32,1,4096]{2,1,0:T(1,128)S(1)}, u32[]{:S(2)}, u32[]{:S(2)}) async-start(f32[32,1,4096]{2,1,0:T(1,128)} %bitcast.56), calls=%async_computation.1 | async-start | bytes 1048576 | tf_op jit(solution)/shard_map/all_to_all | solution.py:263
  95.7 2.1 convert_bitcast_fusion.1
  99.0 12.2 %all-to-all-done.1 = f32[32,1,4096]{2,1,0:T(1,128)S(1)} async-done(((f32[32,1,4096]{2,1,0:T(1,128)}), f32[32,1,4096]{2,1,0:T(1,128)S(1)}, u32[]{:S(2)}, u32[]{:S(2)}) %all-to-all-start.1) | async-done | bytes 524320 | tf_op jit(solution)/shard_map/all_to_all | solution.py:263
  112.9 3.3 %all-to-all-start.2 = ((f32[32,1,4096]{2,1,0:T(1,128)}), f32[32,1,4096]{2,1,0:T(1,128)}, u32[]{:S(2)}, u32[]{:S(2)}) async-start(f32[32,1,4096]{2,1,0:T(1,128)} %broadcast_in_dim.10), calls=%async_computation.2 | async-start | bytes 1048576 | tf_op jit(solution)/shard_map/all_to_all | solution.py:270
  116.3 1.7 add_convert_fusion.1
  117.9 1.6 collective-permute-start.1
  122.4 14.8 %collective-permute-done.1 = bf16[2,1,384,384]{3,2,0,1:T(8,128)(2,1)S(1)} collective-permute-done((bf16[2,1,384,384]{3,2,0,1:T(8,128)(2,1)S(1)}, bf16[2,1,384,384]{3,2,0,1:T(8,128)(2,1)S(1)}, u32[]{:S(2)}, u32[]{:S(2)}) %collective-permute-start.1) | collective-permute-done | bytes 589856 | tf_op jit(solution)/shard_map/ppermute | solution.py:282
  137.2 1.8 fusion.14.tile_ref
  139.0 1.7 broadcast_multiply_fusion.1
  141.7 14.3 %shard_map.78 = (f32[2,384,384]{2,1,0:T(8,128)}, f32[4,2,128,128]{3,2,1,0:T(8,128)}) custom-call(s32[97]{0:T(128)} %concatenate.48.table_ref, f32[2,384,384]{2,1,0:T(8,128)} %fusion.14.tile_ref, bf16[24,136,128]{2,1,0:T(8,128)(2,1)} %bitcast.53, f32[4,2,128,128]{3,2,1,0:T(8,128)} %add.165.probe_ref, bf16[256,256]{1,0:T(8,128)(2,1)} %get-tuple-element.35.left_ref, ...), custom_call_target="tpu_custom_call" | custom-call | flops 9160359936 | bytes 4194304 | tf_op jit(solution)/shard_map/pallas_call | solution.py:204
  156.0 25.1 %all-to-all-start.3 = ((f32[32,1,4096]{2,1,0:T(1,128)}), f32[32,1,4096]{2,1,0:T(1,128)}, u32[]{:S(2)}, u32[]{:S(2)}) async-start(f32[32,1,4096]{2,1,0:T(1,128)} %bitcast.57), calls=%async_computation.3 | async-start | bytes 1048576 | tf_op jit(solution)/shard_map/all_to_all | solution.py:263
  181.1 1.4 convert_bitcast_fusion
  182.8 1.8 collective-permute-done.2
  185.5 1.7 collective-permute-start.3
  187.2 9.4 %all-to-all-done.3 = f32[32,1,4096]{2,1,0:T(1,128)} async-done(((f32[32,1,4096]{2,1,0:T(1,128)}), f32[32,1,4096]{2,1,0:T(1,128)}, u32[]{:S(2)}, u32[]{:S(2)}) %all-to-all-start.3) | async-done | bytes 524320 | tf_op jit(solution)/shard_map/all_to_all | solution.py:263
  196.6 1.4 reduce_sum.109
  199.3 3.3 %all-to-all-start.4 = ((f32[32,1,4096]{2,1,0:T(1,128)}), f32[32,1,4096]{2,1,0:T(1,128)}, u32[]{:S(2)}, u32[]{:S(2)}) async-start(f32[32,1,4096]{2,1,0:T(1,128)} %broadcast_in_dim.11), calls=%async_computation.4 | async-start | bytes 1048576 | tf_op jit(solution)/shard_map/all_to_all | solution.py:270
  203.3 4.1 %add_bitcast_fusion = f32[2,1,384,384]{3,2,1,0:T(8,128)} fusion(bf16[2,1,384,384]{3,2,0,1:T(8,128)(2,1)} %collective-permute-done.3, bf16[2,1,384,384]{3,2,0,1:T(8,128)(2,1)} %add_convert_fusion, f32[]{:T(128)} %reduce_max.19, f32[]{:T(128)} %reduce_max.18, bf16[2,1,384,384]{3,2,0,1:T(8,128)(2,1)} %copy-done.4, ...), kind=kLoop, calls=%fused_computation.3 | loop fusion | flops 2949120 | bytes 4718600
  207.4 10.8 %all-to-all-done.4 = f32[32,1,4096]{2,1,0:T(1,128)} async-done(((f32[32,1,4096]{2,1,0:T(1,128)}), f32[32,1,4096]{2,1,0:T(1,128)}, u32[]{:S(2)}, u32[]{:S(2)}) %all-to-all-start.4) | async-done | bytes 524320 | tf_op jit(solution)/shard_map/all_to_all | solution.py:270
  218.2 1.7 broadcast_multiply_fusion
  (81 shorter events, 21.6 us)
Async XLA Ops:
  0.6 4.8 %copy-start = (bf16[32,128,128]{2,1,0:T(8,128)(2,1)S(1)}, bf16[32,128,128]{2,1,0:T(8,128)(2,1)}, u32[]{:S(2)}) copy-start(bf16[32,128,128]{2,1,0:T(8,128)(2,1)} %param.6) | copy-start | bytes 3145732
  7.8 46.4 %all-to-all-start = ((bf16[8,2,3,136,128]{4,3,2,1,0:T(8,128)(2,1)}), bf16[8,2,3,136,128]{4,3,2,1,0:T(8,128)(2,1)S(1)}, u32[]{:S(2)}, u32[]{:S(2)}) async-start(bf16[8,2,3,136,128]{4,3,2,1,0:T(8,128)(2,1)} %copy.72), calls=%async_computation | async-start | bytes 3342336 | tf_op jit(solution)/shard_map/all_to_all | solution.py:341
  54.3 0.9 copy-start.8
  54.3 44.5 %copy-start.7 = (bf16[8,1,3,136,128]{4,3,2,1,0:T(8,128)(2,1)}, bf16[8,1,3,136,128]{4,3,2,1,0:T(8,128)(2,1)S(1)}, u32[]{:S(2)}) copy-start(bf16[8,1,3,136,128]{4,3,2,1,0:T(8,128)(2,1)S(1)} %get-tuple-element.33) | copy-start | bytes 2506756
  72.6 25.5 %copy-start.5 = (f32[4,2,128,128]{3,2,1,0:T(8,128)S(1)}, f32[4,2,128,128]{3,2,1,0:T(8,128)}, u32[]{:S(2)}) copy-start(f32[4,2,128,128]{3,2,1,0:T(8,128)} %probe_ref.1) | copy-start | bytes 1572868
  72.6 38.6 %all-to-all-start.1 = ((f32[32,1,4096]{2,1,0:T(1,128)}), f32[32,1,4096]{2,1,0:T(1,128)S(1)}, u32[]{:S(2)}, u32[]{:S(2)}) async-start(f32[32,1,4096]{2,1,0:T(1,128)} %bitcast.56), calls=%async_computation.1 | async-start | bytes 1048576 | tf_op jit(solution)/shard_map/all_to_all | solution.py:263
  97.9 18.4 %collective-permute-start = (bf16[2,1,384,384]{3,2,0,1:T(8,128)(2,1)}, bf16[2,1,384,384]{3,2,0,1:T(8,128)(2,1)}, u32[]{:S(2)}, u32[]{:S(2)}) collective-permute-start(bf16[2,1,384,384]{3,2,0,1:T(8,128)(2,1)} %convert_bitcast_fusion.1), channel_id=1, source_target_pairs={{0,1},{1,0},{2,3},{3,2},{4,5},{5,4},{6,7},{7,6},{8,9},{9,8},{10,11... | collective-permute-start | bytes 1769480 | tf_op jit(solution)/shard_map/ppermute | solution.py:282
  112.9 26.1 %all-to-all-start.2 = ((f32[32,1,4096]{2,1,0:T(1,128)}), f32[32,1,4096]{2,1,0:T(1,128)}, u32[]{:S(2)}, u32[]{:S(2)}) async-start(f32[32,1,4096]{2,1,0:T(1,128)} %broadcast_in_dim.10), calls=%async_computation.2 | async-start | bytes 1048576 | tf_op jit(solution)/shard_map/all_to_all | solution.py:270
  116.3 20.9 %copy-start.2 = (f32[2,1,384,384]{3,2,1,0:T(8,128)S(1)}, f32[2,1,384,384]{3,2,1,0:T(8,128)}, u32[]{:S(2)}) copy-start(f32[2,1,384,384]{3,2,1,0:T(8,128)} %param.10) | copy-start | bytes 3538948
  117.9 19.3 %collective-permute-start.1 = (bf16[2,1,384,384]{3,2,0,1:T(8,128)(2,1)S(1)}, bf16[2,1,384,384]{3,2,0,1:T(8,128)(2,1)S(1)}, u32[]{:S(2)}, u32[]{:S(2)}) collective-permute-start(bf16[2,1,384,384]{3,2,0,1:T(8,128)(2,1)S(1)} %add_convert_fusion.1), channel_id=1, source_target_pairs={{0,2},{1,3},{2,0},{3,1},{4,6},{5,7},{6,4},{7,5},{8,10},{9,11},{10,... | collective-permute-start | bytes 1769480 | tf_op jit(solution)/shard_map/ppermute | solution.py:282
  137.2 1.8 copy-start.4
  139.0 1.8 copy-start.6
  156.0 40.7 %all-to-all-start.3 = ((f32[32,1,4096]{2,1,0:T(1,128)}), f32[32,1,4096]{2,1,0:T(1,128)}, u32[]{:S(2)}, u32[]{:S(2)}) async-start(f32[32,1,4096]{2,1,0:T(1,128)} %bitcast.57), calls=%async_computation.3 | async-start | bytes 1048576 | tf_op jit(solution)/shard_map/all_to_all | solution.py:263
  181.1 3.5 %copy-start.3 = (f32[2,384,384]{2,1,0:T(8,128)S(1)}, f32[2,384,384]{2,1,0:T(8,128)}, u32[]{:S(2)}) copy-start(f32[2,384,384]{2,1,0:T(8,128)} %get-tuple-element.8) | copy-start | bytes 3538948
  182.5 2.1 collective-permute-start.2
  185.5 17.1 %copy-start.1 = (f32[4,2,128,128]{3,2,1,0:T(8,128)S(1)}, f32[4,2,128,128]{3,2,1,0:T(8,128)}, u32[]{:S(2)}) copy-start(f32[4,2,128,128]{3,2,1,0:T(8,128)} %add.165.probe_ref) | copy-start | bytes 1572868
  185.5 17.8 %collective-permute-start.3 = (bf16[2,1,384,384]{3,2,0,1:T(8,128)(2,1)}, bf16[2,1,384,384]{3,2,0,1:T(8,128)(2,1)}, u32[]{:S(2)}, u32[]{:S(2)}) collective-permute-start(bf16[2,1,384,384]{3,2,0,1:T(8,128)(2,1)} %add_convert_fusion), channel_id=1, source_target_pairs={{0,2},{1,3},{2,0},{3,1},{4,6},{5,7},{6,4},{7,5},{8,10},{9,11},{10,... | collective-permute-start | bytes 1769480 | tf_op jit(solution)/shard_map/ppermute | solution.py:282
  199.3 18.9 %all-to-all-start.4 = ((f32[32,1,4096]{2,1,0:T(1,128)}), f32[32,1,4096]{2,1,0:T(1,128)}, u32[]{:S(2)}, u32[]{:S(2)}) async-start(f32[32,1,4096]{2,1,0:T(1,128)} %broadcast_in_dim.11), calls=%async_computation.4 | async-start | bytes 1048576 | tf_op jit(solution)/shard_map/all_to_all | solution.py:270

commit v8 on v6

--- a/solution.py
+++ b/solution.py
@@ -51,7 +51,7 @@
 def entry_kernel(order_ref, patch_ref, amp_ref, probe_ref, left_ref, right_ref, update_ref, grad_ref):
     slots = order_ref.shape[0] - 1
     count = order_ref[slots]
-    group = 2 if slots % 2 == 0 else 1
+    group = next(size for size in (4, 2, 1) if slots % size == 0)
     grad_ref[...] = jnp.zeros(grad_ref.shape, grad_ref.dtype)
     update_ref[...] = jnp.zeros(update_ref.shape, update_ref.dtype)
 

time: 193 us -> 185 us (0.959)
  Pallas kernels: 26 us -> 15 us
    pallas_call x2, Pallas kernels: 26 us -> 15 us  [entries_kernel(): pl.pallas_call(entry_kernel, grid_spec=grid_spec, out_shape=[jax.ShapeDty...]
  transfers between devices with their start and end apart: 9 -> 9, of which waited for: 8 -> 8; matrix products, arithmetic and copies ran while one was open for 20% -> 21% of each run, Pallas kernels for 0% -> 0%
where the time goes in v8:
time: 185 us; the launch traced here: 182 us
  waiting for transfers between devices  64.4 us (35%)
  starting transfers between devices  34.5 us (19%)
  other arithmetic  27.7 us (15%)
  matrix products  26.8 us (14%)
  Pallas kernels  15 us (8%)
  local copies, waits for them, and re-layouts  12.7 us (7%)
    all_to_all x1, waiting for transfers between devices, on_device(): lax.all_to_all(jnp.swapaxes(payload, 0, 1), 'tile', 0, 0, tiled=True)  34.4 us
    all_to_all x2, starting transfers between devices, sum_over(): lax.all_to_all(value.astype(send_type).reshape(count, -1), axes, 0, 0, ti...  17.3 us
    pallas_call x2, Pallas kernels, entries_kernel(): pl.pallas_call(entry_kernel, grid_spec=grid_spec, out_shape=[jax.ShapeDty...  15 us
    all_to_all x2, waiting for transfers between devices, sum_over(): lax.all_to_all(value.astype(send_type).reshape(count, -1), axes, 0, 0, ti...  13.9 us
    dot_general x2, matrix products, entries_pass(): jnp.einsum('skq,xskc->xqc', pick_rows, spread, preferred_element_type=jnp...  11.4 us
    ppermute x4, waiting for transfers between devices, all_sum_pairs(): other = lax.ppermute(total.astype(send_type), axis, pairs)  10.4 us
    dot_general x2, matrix products, entries_pass(): jnp.einsum('skq,xqc->xskc', pick_rows, stacked, preferred_element_type=jn...  9.47 us
    unnamed x26, local copies, waits for them, and re-layouts  7.34 us
  transfers between devices with their start and end apart: 9, of which 8 were waited for; matrix products, arithmetic and copies ran while one was open for 21% of the time, Pallas kernels for 0%

profile of v8, /device:TPU:0, one launch (start us, length us, event | category | flops | bytes accessed | tf_op | source)
XLA Modules:
  0.0 182.1 jit_solution(8125972482037585290)
XLA Ops:
  7.8 7.3 %all-to-all-start = ((bf16[8,2,3,136,128]{4,3,2,1,0:T(8,128)(2,1)}), bf16[8,2,3,136,128]{4,3,2,1,0:T(8,128)(2,1)S(1)}, u32[]{:S(2)}, u32[]{:S(2)}) async-start(bf16[8,2,3,136,128]{4,3,2,1,0:T(8,128)(2,1)} %copy.96), calls=%async_computation | async-start | bytes 3342336 | tf_op jit(solution)/shard_map/all_to_all | solution.py:330
  15.1 2.7 %copy.101 = f32[2,1,384,384]{2,3,0,1:T(8,128)} copy(f32[2,1,384,384]{3,2,1,0:T(8,128)} %param.10) | data formatting | bytes 2359296 | tf_op args[4]
  19.8 34.4 %all-to-all-done = bf16[8,2,3,136,128]{4,3,2,1,0:T(8,128)(2,1)S(1)} async-done(((bf16[8,2,3,136,128]{4,3,2,1,0:T(8,128)(2,1)}), bf16[8,2,3,136,128]{4,3,2,1,0:T(8,128)(2,1)S(1)}, u32[]{:S(2)}, u32[]{:S(2)}) %all-to-all-start) | async-done | bytes 1671200 | tf_op jit(solution)/shard_map/all_to_all | solution.py:330
  57.9 4.4 %convert_bitcast_fusion.1 = bf16[2,24,128,384]{3,2,0,1:T(8,128)(2,1)S(1)} fusion(s32[24,128]{1,0:T(8,128)S(1)} %get-tuple-element.38, pred[24]{0:T(512)(128)(4,1)S(1)} %reduce.4, f32[2,1,384,384]{3,2,1,0:T(8,128)} %param.10), kind=kOutput, calls=%fused_computation.14 | convolution fusion | flops 1816952832 | bytes 5910552 | tf_op jit(solution)/shard_map/skq,xqc->xskc/dot_general | solution.py:268
  63.6 2.6 %fusion.71.patch_ref = bf16[2,24,128,128]{3,2,1,0:T(8,128)(2,1)} fusion(bf16[2,24,128,384]{3,2,0,1:T(8,128)(2,1)S(1)} %convert_bitcast_fusion.1, s32[24,128]{1,0:T(8,128)S(1)} %get-tuple-element.39), kind=kOutput, calls=%fused_computation.45 | convolution fusion | flops 605945856 | bytes 6303744 | tf_op jit(solution)/shard_map/xskc,scl->xskl/dot_general | solution.py:271
  66.3 7.5 %shard_map.77 = (bf16[2,24,128,128]{3,2,1,0:T(8,128)(2,1)}, f32[4,2,128,128]{3,2,1,0:T(8,128)}) custom-call(s32[25]{0:T(128)} %pad_add_fusion.order_ref, bf16[2,24,128,128]{3,2,1,0:T(8,128)(2,1)} %fusion.71.patch_ref, bf16[24,136,128]{2,1,0:T(8,128)(2,1)} %bitcast.161, f32[4,2,128,128]{3,2,1,0:T(8,128)} %probe_ref.1, ...), custom_call_target="tpu_custom_call" | custom-call | flops 6442450944 | bytes 4980736 | tf_op jit(solution)/shard_map/pallas_call | solution.py:169
  73.8 5.3 %fusion.104 = bf16[2,1,384,384]{2,3,0,1:T(8,128)(2,1)S(1)} fusion(s32[24,128]{1,0:T(8,128)S(1)} %get-tuple-element.38, pred[24]{0:T(512)(128)(4,1)S(1)} %reduce.4, bf16[2,24,128,128]{3,2,1,0:T(8,128)(2,1)} %get-tuple-element.6, s32[24,128]{1,0:T(8,128)S(1)} %get-tuple-element.39), kind=kOutput, calls=%fused_computation.50 | convolution fusion | flops 2422112256 | bytes 2187288 | tf_op jit(solution)/shard_map/skq,xskc->xqc/dot_general | solution.py:289
  79.4 8.2 %all-to-all-start.1 = ((f32[32,1,4096]{2,1,0:T(1,128)}), f32[32,1,4096]{2,1,0:T(1,128)S(1)}, u32[]{:S(2)}, u32[]{:S(2)}) async-start(f32[32,1,4096]{2,1,0:T(1,128)} %bitcast.38), calls=%async_computation.1 | async-start | bytes 1048576 | tf_op jit(solution)/shard_map/all_to_all | solution.py:228
  92.5 10.5 %all-to-all-done.1 = f32[32,1,4096]{2,1,0:T(1,128)S(1)} async-done(((f32[32,1,4096]{2,1,0:T(1,128)}), f32[32,1,4096]{2,1,0:T(1,128)S(1)}, u32[]{:S(2)}, u32[]{:S(2)}) %all-to-all-start.1) | async-done | bytes 524320 | tf_op jit(solution)/shard_map/all_to_all | solution.py:228
  104.6 3.3 %all-to-all-start.2 = ((f32[32,1,4096]{2,1,0:T(1,128)}), f32[32,1,4096]{2,1,0:T(1,128)}, u32[]{:S(2)}, u32[]{:S(2)}) async-start(f32[32,1,4096]{2,1,0:T(1,128)} %broadcast_in_dim.10), calls=%async_computation.2 | async-start | bytes 1048576 | tf_op jit(solution)/shard_map/all_to_all | solution.py:235
  109.5 5.1 %convert_bitcast_fusion = bf16[2,24,128,384]{2,3,0,1:T(8,128)(2,1)S(1)} fusion(s32[24,128]{1,0:T(8,128)S(1)} %iota_add_fusion, pred[24]{0:T(512)(128)(4,1)S(1)} %reduce.6, f32[2,1,384,384]{2,3,0,1:T(8,128)S(1)} %copy-done.2, bf16[2,1,384,384]{2,3,0,1:T(8,128)(2,1)} %collective-permute-done.1, bf16[2,1,384,384]{2,3,0,1:T(8,128)(2,1)S(1)} %add_convert_fusion.1, ...), kind=kOutput, calls=%fused_computation.10 | convolution fusion | flops 1818427392 | bytes 7090204 | tf_op jit(solution)/shard_map/skq,xqc->xskc/dot_general | solution.py:268
  114.7 3.3 %fusion.66.patch_ref = bf16[2,24,128,128]{3,2,1,0:T(8,128)(2,1)} fusion(bf16[2,24,128,384]{2,3,0,1:T(8,128)(2,1)S(1)} %convert_bitcast_fusion, s32[24,128]{1,0:T(8,128)S(1)} %iota_add_fusion.1), kind=kOutput, calls=%fused_computation.44 | convolution fusion | flops 605945856 | bytes 6303744 | tf_op jit(solution)/shard_map/xskc,scl->xskl/dot_general | solution.py:271
  118.0 5.5 %all-to-all-done.2 = f32[32,1,4096]{2,1,0:T(1,128)} async-done(((f32[32,1,4096]{2,1,0:T(1,128)}), f32[32,1,4096]{2,1,0:T(1,128)}, u32[]{:S(2)}, u32[]{:S(2)}) %all-to-all-start.2) | async-done | bytes 524320 | tf_op jit(solution)/shard_map/all_to_all | solution.py:235
  123.5 1.7 broadcast_multiply_fusion.1
  126.0 7.5 %shard_map.78 = (bf16[2,24,128,128]{3,2,1,0:T(8,128)(2,1)}, f32[4,2,128,128]{3,2,1,0:T(8,128)}) custom-call(s32[25]{0:T(128)} %pad_add_fusion.1.order_ref, bf16[2,24,128,128]{3,2,1,0:T(8,128)(2,1)} %fusion.66.patch_ref, bf16[24,136,128]{2,1,0:T(8,128)(2,1)} %bitcast.159, f32[4,2,128,128]{3,2,1,0:T(8,128)} %add.263.probe_ref, ...), custom_call_target="tpu_custom_call" | custom-call | flops 6442450944 | bytes 4980736 | tf_op jit(solution)/shard_map/pallas_call | solution.py:169
  133.5 9.1 %all-to-all-start.3 = ((f32[32,1,4096]{2,1,0:T(1,128)}), f32[32,1,4096]{2,1,0:T(1,128)}, u32[]{:S(2)}, u32[]{:S(2)}) async-start(f32[32,1,4096]{2,1,0:T(1,128)} %bitcast.162), calls=%async_computation.3 | async-start | bytes 1048576 | tf_op jit(solution)/shard_map/all_to_all | solution.py:228
  142.7 6.1 %fusion.111 = bf16[2,1,384,384]{2,3,0,1:T(8,128)(2,1)} fusion(s32[24,128]{1,0:T(8,128)S(1)} %iota_add_fusion, pred[24]{0:T(512)(128)(4,1)S(1)} %reduce.6, bf16[2,24,128,128]{3,2,1,0:T(8,128)(2,1)} %get-tuple-element.8, s32[24,128]{1,0:T(8,128)S(1)} %iota_add_fusion.1), kind=kOutput, calls=%fused_computation.51 | convolution fusion | flops 2422112256 | bytes 2187288 | tf_op jit(solution)/shard_map/skq,xskc->xqc/dot_general | solution.py:289
  148.8 2.2 %collective-permute-done.2 = bf16[2,1,384,384]{2,3,0,1:T(8,128)(2,1)S(1)} collective-permute-done((bf16[2,1,384,384]{2,3,0,1:T(8,128)(2,1)}, bf16[2,1,384,384]{2,3,0,1:T(8,128)(2,1)S(1)}, u32[]{:S(2)}, u32[]{:S(2)}) %collective-permute-start.2) | collective-permute-done | bytes 589856 | tf_op jit(solution)/shard_map/ppermute | solution.py:247
  151.0 2.0 %add_convert_fusion = bf16[2,1,384,384]{2,3,0,1:T(8,128)(2,1)} fusion(bf16[2,1,384,384]{2,3,0,1:T(8,128)(2,1)S(1)} %collective-permute-done.2, bf16[2,1,384,384]{2,3,0,1:T(8,128)(2,1)} %fusion.111), kind=kLoop, calls=%fused_computation.53 | loop fusion | flops 1179648 | bytes 1769472 | tf_op jit(solution)/shard_map/convert_element_type | solution.py:248
  154.5 3.5 %all-to-all-done.3 = f32[32,1,4096]{2,1,0:T(1,128)} async-done(((f32[32,1,4096]{2,1,0:T(1,128)}), f32[32,1,4096]{2,1,0:T(1,128)}, u32[]{:S(2)}, u32[]{:S(2)}) %all-to-all-start.3) | async-done | bytes 524320 | tf_op jit(solution)/shard_map/all_to_all | solution.py:228
  160.7 3.3 %all-to-all-start.4 = ((f32[32,1,4096]{2,1,0:T(1,128)}), f32[32,1,4096]{2,1,0:T(1,128)}, u32[]{:S(2)}, u32[]{:S(2)}) async-start(f32[32,1,4096]{2,1,0:T(1,128)} %broadcast_in_dim.11), calls=%async_computation.4 | async-start | bytes 1048576 | tf_op jit(solution)/shard_map/all_to_all | solution.py:235
  164.7 7.8 %collective-permute-done.3 = bf16[2,1,384,384]{2,3,0,1:T(8,128)(2,1)} collective-permute-done((bf16[2,1,384,384]{2,3,0,1:T(8,128)(2,1)}, bf16[2,1,384,384]{2,3,0,1:T(8,128)(2,1)}, u32[]{:S(2)}, u32[]{:S(2)}) %collective-permute-start.3) | collective-permute-done | bytes 589856 | tf_op jit(solution)/shard_map/ppermute | solution.py:247
  172.5 4.1 %divide_add_fusion = f32[2,1,384,384]{2,3,0,1:T(8,128)} fusion(bf16[2,1,384,384]{2,3,0,1:T(8,128)(2,1)} %collective-permute-done.3, bf16[2,1,384,384]{2,3,0,1:T(8,128)(2,1)} %add_convert_fusion, f32[]{:T(128)} %reduce_max.19, f32[2,1,384,384]{2,3,0,1:T(8,128)S(1)} %copy-done.2, f32[]{:T(128)} %reduce_max.18, ...), kind=kLoop, calls=%fused_computation.52 | loop fusion | flops 2949120 | bytes 4718600 | tf_op jit(solution)/shard_map/add | solution.py:317
  176.7 2.7 %copy.109 = f32[2,1,384,384]{3,2,1,0:T(8,128)} copy(f32[2,1,384,384]{2,3,0,1:T(8,128)} %divide_add_fusion) | data formatting | bytes 2359296
  (95 shorter events, 31.0 us)
Async XLA Ops:
  0.6 4.8 %copy-start = (bf16[32,128,128]{2,1,0:T(8,128)(2,1)S(1)}, bf16[32,128,128]{2,1,0:T(8,128)(2,1)}, u32[]{:S(2)}) copy-start(bf16[32,128,128]{2,1,0:T(8,128)(2,1)} %param.6) | copy-start | bytes 3145732
  7.8 46.4 %all-to-all-start = ((bf16[8,2,3,136,128]{4,3,2,1,0:T(8,128)(2,1)}), bf16[8,2,3,136,128]{4,3,2,1,0:T(8,128)(2,1)S(1)}, u32[]{:S(2)}, u32[]{:S(2)}) async-start(bf16[8,2,3,136,128]{4,3,2,1,0:T(8,128)(2,1)} %copy.96), calls=%async_computation | async-start | bytes 3342336 | tf_op jit(solution)/shard_map/all_to_all | solution.py:330
  15.1 2.7 %copy-start.3 = (f32[4,2,128,128]{3,2,1,0:T(8,128)S(1)}, f32[4,2,128,128]{3,2,1,0:T(8,128)}, u32[]{:S(2)}) copy-start(f32[4,2,128,128]{3,2,1,0:T(8,128)} %probe_ref.1) | copy-start | bytes 1572868
  54.3 0.9 copy-start.5
  54.3 8.0 %copy-start.6 = (bf16[8,1,3,136,128]{4,3,2,1,0:T(8,128)(2,1)}, bf16[8,1,3,136,128]{4,3,2,1,0:T(8,128)(2,1)S(1)}, u32[]{:S(2)}) copy-start(bf16[8,1,3,136,128]{4,3,2,1,0:T(8,128)(2,1)S(1)} %get-tuple-element.28) | copy-start | bytes 2506756
  79.1 10.0 %copy-start.7 = (bf16[2,1,384,384]{2,3,0,1:T(8,128)(2,1)}, bf16[2,1,384,384]{2,3,0,1:T(8,128)(2,1)S(1)}, u32[]{:S(2)}) copy-start(bf16[2,1,384,384]{2,3,0,1:T(8,128)(2,1)S(1)} %fusion.104) | copy-start | bytes 1769476
  79.1 13.3 %copy-start.9 = (s32[24]{0:T(128)S(1)}, s32[24]{0:T(128)}, u32[]{:S(2)}) copy-start(s32[24]{0:T(128)} %get-tuple-element.33) | copy-start | bytes 292
  79.1 13.4 %copy-start.8 = (s32[24]{0:T(128)S(1)}, s32[24]{0:T(128)}, u32[]{:S(2)}) copy-start(s32[24]{0:T(128)} %get-tuple-element.32) | copy-start | bytes 292
  79.1 10.0 %collective-permute-start = (bf16[2,1,384,384]{2,3,0,1:T(8,128)(2,1)S(1)}, bf16[2,1,384,384]{2,3,0,1:T(8,128)(2,1)}, u32[]{:S(2)}, u32[]{:S(2)}) collective-permute-start(bf16[2,1,384,384]{2,3,0,1:T(8,128)(2,1)S(1)} %fusion.104), channel_id=1, source_target_pairs={{0,1},{1,0},{2,3},{3,2},{4,5},{5,4},{6,7},{7,6},{8,9},{9,8},{10,11... | collective-permute-start | bytes 1769480 | tf_op jit(solution)/shard_map/ppermute | solution.py:247
  79.4 23.6 %all-to-all-start.1 = ((f32[32,1,4096]{2,1,0:T(1,128)}), f32[32,1,4096]{2,1,0:T(1,128)S(1)}, u32[]{:S(2)}, u32[]{:S(2)}) async-start(f32[32,1,4096]{2,1,0:T(1,128)} %bitcast.38), calls=%async_computation.1 | async-start | bytes 1048576 | tf_op jit(solution)/shard_map/all_to_all | solution.py:228
  89.1 20.4 %copy-start.2 = (f32[2,1,384,384]{2,3,0,1:T(8,128)S(1)}, f32[2,1,384,384]{2,3,0,1:T(8,128)}, u32[]{:S(2)}) copy-start(f32[2,1,384,384]{2,3,0,1:T(8,128)} %copy.101) | copy-start | bytes 3538948
  90.6 18.9 %collective-permute-start.1 = (bf16[2,1,384,384]{2,3,0,1:T(8,128)(2,1)S(1)}, bf16[2,1,384,384]{2,3,0,1:T(8,128)(2,1)}, u32[]{:S(2)}, u32[]{:S(2)}) collective-permute-start(bf16[2,1,384,384]{2,3,0,1:T(8,128)(2,1)S(1)} %add_convert_fusion.1), channel_id=1, source_target_pairs={{0,2},{1,3},{2,0},{3,1},{4,6},{5,7},{6,4},{7,5},{8,10},{9,11},{10,... | collective-permute-start | bytes 1769480 | tf_op jit(solution)/shard_map/ppermute | solution.py:247
  104.6 18.9 %all-to-all-start.2 = ((f32[32,1,4096]{2,1,0:T(1,128)}), f32[32,1,4096]{2,1,0:T(1,128)}, u32[]{:S(2)}, u32[]{:S(2)}) async-start(f32[32,1,4096]{2,1,0:T(1,128)} %broadcast_in_dim.10), calls=%async_computation.2 | async-start | bytes 1048576 | tf_op jit(solution)/shard_map/all_to_all | solution.py:235
  114.6 10.5 %copy-start.4 = (f32[4,2,128,128]{3,2,1,0:T(8,128)S(1)}, f32[4,2,128,128]{3,2,1,0:T(8,128)}, u32[]{:S(2)}) copy-start(f32[4,2,128,128]{3,2,1,0:T(8,128)} %probe_ref.1) | copy-start | bytes 1572868
  133.5 24.5 %all-to-all-start.3 = ((f32[32,1,4096]{2,1,0:T(1,128)}), f32[32,1,4096]{2,1,0:T(1,128)}, u32[]{:S(2)}, u32[]{:S(2)}) async-start(f32[32,1,4096]{2,1,0:T(1,128)} %bitcast.162), calls=%async_computation.3 | async-start | bytes 1048576 | tf_op jit(solution)/shard_map/all_to_all | solution.py:228
  148.8 15.2 %copy-start.1 = (f32[4,2,128,128]{3,2,1,0:T(8,128)S(1)}, f32[4,2,128,128]{3,2,1,0:T(8,128)}, u32[]{:S(2)}) copy-start(f32[4,2,128,128]{3,2,1,0:T(8,128)} %add.263.probe_ref) | copy-start | bytes 1572868
  148.8 2.2 %collective-permute-start.2 = (bf16[2,1,384,384]{2,3,0,1:T(8,128)(2,1)}, bf16[2,1,384,384]{2,3,0,1:T(8,128)(2,1)S(1)}, u32[]{:S(2)}, u32[]{:S(2)}) collective-permute-start(bf16[2,1,384,384]{2,3,0,1:T(8,128)(2,1)} %fusion.111), channel_id=1, source_target_pairs={{0,1},{1,0},{2,3},{3,2},{4,5},{5,4},{6,7},{7,6},{8,9},{9,8},{10,11... | collective-permute-start | bytes 1769480 | tf_op jit(solution)/shard_map/ppermute | solution.py:247
  153.0 19.5 %collective-permute-start.3 = (bf16[2,1,384,384]{2,3,0,1:T(8,128)(2,1)}, bf16[2,1,384,384]{2,3,0,1:T(8,128)(2,1)}, u32[]{:S(2)}, u32[]{:S(2)}) collective-permute-start(bf16[2,1,384,384]{2,3,0,1:T(8,128)(2,1)} %add_convert_fusion), channel_id=1, source_target_pairs={{0,2},{1,3},{2,0},{3,1},{4,6},{5,7},{6,4},{7,5},{8,10},{9,11},{10,... | collective-permute-start | bytes 1769480 | tf_op jit(solution)/shard_map/ppermute | solution.py:247
  160.7 18.9 %all-to-all-start.4 = ((f32[32,1,4096]{2,1,0:T(1,128)}), f32[32,1,4096]{2,1,0:T(1,128)}, u32[]{:S(2)}, u32[]{:S(2)}) async-start(f32[32,1,4096]{2,1,0:T(1,128)} %broadcast_in_dim.11), calls=%async_computation.4 | async-start | bytes 1048576 | tf_op jit(solution)/shard_map/all_to_all | solution.py:235

commit v9 on v8

--- a/solution.py
+++ b/solution.py
@@ -51,7 +51,7 @@
 def entry_kernel(order_ref, patch_ref, amp_ref, probe_ref, left_ref, right_ref, update_ref, grad_ref):
     slots = order_ref.shape[0] - 1
     count = order_ref[slots]
-    group = next(size for size in (4, 2, 1) if slots % size == 0)
+    group = next(size for size in (8, 4, 2, 1) if slots % size == 0)
     grad_ref[...] = jnp.zeros(grad_ref.shape, grad_ref.dtype)
     update_ref[...] = jnp.zeros(update_ref.shape, update_ref.dtype)
 

time: 185 us -> 184 us (level); the launches traced: 182 us -> 184 us
  Pallas kernels: 15 us -> 21.9 us
  starting transfers between devices: 34.5 us -> 29.6 us
    pallas_call x2, Pallas kernels: 15 us -> 21.9 us  [entries_kernel(): pl.pallas_call(entry_kernel, grid_spec=grid_spec, out_shape=[jax.ShapeDty...]
    all_to_all x2, starting transfers between devices: 17.3 us -> 11.9 us  [sum_over(): lax.all_to_all(value.astype(send_type).reshape(count, -1), axes, 0, 0, ti...]
where the time goes in v9:
time: 184 us
  waiting for transfers between devices  64.3 us (35%)
  starting transfers between devices  29.6 us (16%)
  other arithmetic  27.7 us (15%)
  matrix products  26.8 us (15%)
  Pallas kernels  21.9 us (12%)
  local copies, waits for them, and re-layouts  12.7 us (7%)
    all_to_all x1, waiting for transfers between devices, on_device(): lax.all_to_all(jnp.swapaxes(payload, 0, 1), 'tile', 0, 0, tiled=True)  34.4 us
    pallas_call x2, Pallas kernels, entries_kernel(): pl.pallas_call(entry_kernel, grid_spec=grid_spec, out_shape=[jax.ShapeDty...  21.9 us
    all_to_all x2, waiting for transfers between devices, sum_over(): lax.all_to_all(value.astype(send_type).reshape(count, -1), axes, 0, 0, ti...  14 us
    all_to_all x2, starting transfers between devices, sum_over(): lax.all_to_all(value.astype(send_type).reshape(count, -1), axes, 0, 0, ti...  11.9 us
    dot_general x2, matrix products, entries_pass(): jnp.einsum('skq,xskc->xqc', pick_rows, spread, preferred_element_type=jnp...  11.4 us
    ppermute x4, waiting for transfers between devices, all_sum_pairs(): other = lax.ppermute(total.astype(send_type), axis, pairs)  10 us
    dot_general x2, matrix products, entries_pass(): jnp.einsum('skq,xqc->xskc', pick_rows, stacked, preferred_element_type=jn...  9.49 us
    unnamed x26, local copies, waits for them, and re-layouts  7.34 us
  transfers between devices with their start and end apart: 9, of which 8 were waited for; matrix products, arithmetic and copies ran while one was open for 21% of the time, Pallas kernels for 0%

profile of v9, /device:TPU:0, one launch (start us, length us, event | category | flops | bytes accessed | tf_op | source)
XLA Modules:
  0.0 184.0 jit_solution(5697358089165982002)
XLA Ops:
  7.8 7.3 %all-to-all-start = ((bf16[8,2,3,136,128]{4,3,2,1,0:T(8,128)(2,1)}), bf16[8,2,3,136,128]{4,3,2,1,0:T(8,128)(2,1)S(1)}, u32[]{:S(2)}, u32[]{:S(2)}) async-start(bf16[8,2,3,136,128]{4,3,2,1,0:T(8,128)(2,1)} %copy.96), calls=%async_computation | async-start | bytes 3342336 | tf_op jit(solution)/shard_map/all_to_all | solution.py:330
  15.1 2.7 %copy.101 = f32[2,1,384,384]{2,3,0,1:T(8,128)} copy(f32[2,1,384,384]{3,2,1,0:T(8,128)} %param.10) | data formatting | bytes 2359296 | tf_op args[4]
  19.8 34.4 %all-to-all-done = bf16[8,2,3,136,128]{4,3,2,1,0:T(8,128)(2,1)S(1)} async-done(((bf16[8,2,3,136,128]{4,3,2,1,0:T(8,128)(2,1)}), bf16[8,2,3,136,128]{4,3,2,1,0:T(8,128)(2,1)S(1)}, u32[]{:S(2)}, u32[]{:S(2)}) %all-to-all-start) | async-done | bytes 1671200 | tf_op jit(solution)/shard_map/all_to_all | solution.py:330
  57.9 4.4 %convert_bitcast_fusion.1 = bf16[2,24,128,384]{3,2,0,1:T(8,128)(2,1)S(1)} fusion(s32[24,128]{1,0:T(8,128)S(1)} %get-tuple-element.38, pred[24]{0:T(512)(128)(4,1)S(1)} %reduce.4, f32[2,1,384,384]{3,2,1,0:T(8,128)} %param.10), kind=kOutput, calls=%fused_computation.14 | convolution fusion | flops 1816952832 | bytes 5910552 | tf_op jit(solution)/shard_map/skq,xqc->xskc/dot_general | solution.py:268
  63.6 2.6 %fusion.71.patch_ref = bf16[2,24,128,128]{3,2,1,0:T(8,128)(2,1)} fusion(bf16[2,24,128,384]{3,2,0,1:T(8,128)(2,1)S(1)} %convert_bitcast_fusion.1, s32[24,128]{1,0:T(8,128)S(1)} %get-tuple-element.39), kind=kOutput, calls=%fused_computation.45 | convolution fusion | flops 605945856 | bytes 6303744 | tf_op jit(solution)/shard_map/xskc,scl->xskl/dot_general | solution.py:271
  66.3 10.9 %shard_map.77 = (bf16[2,24,128,128]{3,2,1,0:T(8,128)(2,1)}, f32[4,2,128,128]{3,2,1,0:T(8,128)}) custom-call(s32[25]{0:T(128)} %pad_add_fusion.order_ref, bf16[2,24,128,128]{3,2,1,0:T(8,128)(2,1)} %fusion.71.patch_ref, bf16[24,136,128]{2,1,0:T(8,128)(2,1)} %bitcast.161, f32[4,2,128,128]{3,2,1,0:T(8,128)} %probe_ref.1, ...), custom_call_target="tpu_custom_call" | custom-call | flops 6442450944 | bytes 4980736 | tf_op jit(solution)/shard_map/pallas_call | solution.py:169
  77.2 5.3 %fusion.104 = bf16[2,1,384,384]{2,3,0,1:T(8,128)(2,1)S(1)} fusion(s32[24,128]{1,0:T(8,128)S(1)} %get-tuple-element.38, pred[24]{0:T(512)(128)(4,1)S(1)} %reduce.4, bf16[2,24,128,128]{3,2,1,0:T(8,128)(2,1)} %get-tuple-element.6, s32[24,128]{1,0:T(8,128)S(1)} %get-tuple-element.39), kind=kOutput, calls=%fused_computation.50 | convolution fusion | flops 2422112256 | bytes 2187288 | tf_op jit(solution)/shard_map/skq,xskc->xqc/dot_general | solution.py:289
  82.8 6.2 %all-to-all-start.1 = ((f32[32,1,4096]{2,1,0:T(1,128)}), f32[32,1,4096]{2,1,0:T(1,128)S(1)}, u32[]{:S(2)}, u32[]{:S(2)}) async-start(f32[32,1,4096]{2,1,0:T(1,128)} %bitcast.38), calls=%async_computation.1 | async-start | bytes 1048576 | tf_op jit(solution)/shard_map/all_to_all | solution.py:228
  92.1 1.8 collective-permute-start.1
  94.1 10.5 %all-to-all-done.1 = f32[32,1,4096]{2,1,0:T(1,128)S(1)} async-done(((f32[32,1,4096]{2,1,0:T(1,128)}), f32[32,1,4096]{2,1,0:T(1,128)S(1)}, u32[]{:S(2)}, u32[]{:S(2)}) %all-to-all-start.1) | async-done | bytes 524320 | tf_op jit(solution)/shard_map/all_to_all | solution.py:228
  106.2 3.3 %all-to-all-start.2 = ((f32[32,1,4096]{2,1,0:T(1,128)}), f32[32,1,4096]{2,1,0:T(1,128)}, u32[]{:S(2)}, u32[]{:S(2)}) async-start(f32[32,1,4096]{2,1,0:T(1,128)} %broadcast_in_dim.10), calls=%async_computation.2 | async-start | bytes 1048576 | tf_op jit(solution)/shard_map/all_to_all | solution.py:235
  111.2 5.1 %convert_bitcast_fusion = bf16[2,24,128,384]{2,3,0,1:T(8,128)(2,1)S(1)} fusion(s32[24,128]{1,0:T(8,128)S(1)} %iota_add_fusion, pred[24]{0:T(512)(128)(4,1)S(1)} %reduce.6, f32[2,1,384,384]{2,3,0,1:T(8,128)S(1)} %copy-done.2, bf16[2,1,384,384]{2,3,0,1:T(8,128)(2,1)} %collective-permute-done.1, bf16[2,1,384,384]{2,3,0,1:T(8,128)(2,1)S(1)} %add_convert_fusion.1, ...), kind=kOutput, calls=%fused_computation.10 | convolution fusion | flops 1818427392 | bytes 7090204 | tf_op jit(solution)/shard_map/skq,xqc->xskc/dot_general | solution.py:268
  116.3 3.3 %fusion.66.patch_ref = bf16[2,24,128,128]{3,2,1,0:T(8,128)(2,1)} fusion(bf16[2,24,128,384]{2,3,0,1:T(8,128)(2,1)S(1)} %convert_bitcast_fusion, s32[24,128]{1,0:T(8,128)S(1)} %iota_add_fusion.1), kind=kOutput, calls=%fused_computation.44 | convolution fusion | flops 605945856 | bytes 6303744 | tf_op jit(solution)/shard_map/xskc,scl->xskl/dot_general | solution.py:271
  119.6 5.5 %all-to-all-done.2 = f32[32,1,4096]{2,1,0:T(1,128)} async-done(((f32[32,1,4096]{2,1,0:T(1,128)}), f32[32,1,4096]{2,1,0:T(1,128)}, u32[]{:S(2)}, u32[]{:S(2)}) %all-to-all-start.2) | async-done | bytes 524320 | tf_op jit(solution)/shard_map/all_to_all | solution.py:235
  127.6 11.0 %shard_map.78 = (bf16[2,24,128,128]{3,2,1,0:T(8,128)(2,1)}, f32[4,2,128,128]{3,2,1,0:T(8,128)}) custom-call(s32[25]{0:T(128)} %pad_add_fusion.1.order_ref, bf16[2,24,128,128]{3,2,1,0:T(8,128)(2,1)} %fusion.66.patch_ref, bf16[24,136,128]{2,1,0:T(8,128)(2,1)} %bitcast.159, f32[4,2,128,128]{3,2,1,0:T(8,128)} %add.263.probe_ref, ...), custom_call_target="tpu_custom_call" | custom-call | flops 6442450944 | bytes 4980736 | tf_op jit(solution)/shard_map/pallas_call | solution.py:169
  138.6 5.7 %all-to-all-start.3 = ((f32[32,1,4096]{2,1,0:T(1,128)}), f32[32,1,4096]{2,1,0:T(1,128)}, u32[]{:S(2)}, u32[]{:S(2)}) async-start(f32[32,1,4096]{2,1,0:T(1,128)} %bitcast.162), calls=%async_computation.3 | async-start | bytes 1048576 | tf_op jit(solution)/shard_map/all_to_all | solution.py:228
  144.3 6.1 %fusion.111 = bf16[2,1,384,384]{2,3,0,1:T(8,128)(2,1)} fusion(s32[24,128]{1,0:T(8,128)S(1)} %iota_add_fusion, pred[24]{0:T(512)(128)(4,1)S(1)} %reduce.6, bf16[2,24,128,128]{3,2,1,0:T(8,128)(2,1)} %get-tuple-element.8, s32[24,128]{1,0:T(8,128)S(1)} %iota_add_fusion.1), kind=kOutput, calls=%fused_computation.51 | convolution fusion | flops 2422112256 | bytes 2187288 | tf_op jit(solution)/shard_map/skq,xskc->xqc/dot_general | solution.py:289
  150.6 2.0 %collective-permute-done.2 = bf16[2,1,384,384]{2,3,0,1:T(8,128)(2,1)S(1)} collective-permute-done((bf16[2,1,384,384]{2,3,0,1:T(8,128)(2,1)}, bf16[2,1,384,384]{2,3,0,1:T(8,128)(2,1)S(1)}, u32[]{:S(2)}, u32[]{:S(2)}) %collective-permute-start.2) | collective-permute-done | bytes 589856 | tf_op jit(solution)/shard_map/ppermute | solution.py:247
  152.7 2.0 %add_convert_fusion = bf16[2,1,384,384]{2,3,0,1:T(8,128)(2,1)} fusion(bf16[2,1,384,384]{2,3,0,1:T(8,128)(2,1)S(1)} %collective-permute-done.2, bf16[2,1,384,384]{2,3,0,1:T(8,128)(2,1)} %fusion.111), kind=kLoop, calls=%fused_computation.53 | loop fusion | flops 1179648 | bytes 1769472 | tf_op jit(solution)/shard_map/convert_element_type | solution.py:248
  156.4 3.6 %all-to-all-done.3 = f32[32,1,4096]{2,1,0:T(1,128)} async-done(((f32[32,1,4096]{2,1,0:T(1,128)}), f32[32,1,4096]{2,1,0:T(1,128)}, u32[]{:S(2)}, u32[]{:S(2)}) %all-to-all-start.3) | async-done | bytes 524320 | tf_op jit(solution)/shard_map/all_to_all | solution.py:228
  162.6 3.3 %all-to-all-start.4 = ((f32[32,1,4096]{2,1,0:T(1,128)}), f32[32,1,4096]{2,1,0:T(1,128)}, u32[]{:S(2)}, u32[]{:S(2)}) async-start(f32[32,1,4096]{2,1,0:T(1,128)} %broadcast_in_dim.11), calls=%async_computation.4 | async-start | bytes 1048576 | tf_op jit(solution)/shard_map/all_to_all | solution.py:235
  166.6 7.7 %collective-permute-done.3 = bf16[2,1,384,384]{2,3,0,1:T(8,128)(2,1)} collective-permute-done((bf16[2,1,384,384]{2,3,0,1:T(8,128)(2,1)}, bf16[2,1,384,384]{2,3,0,1:T(8,128)(2,1)}, u32[]{:S(2)}, u32[]{:S(2)}) %collective-permute-start.3) | collective-permute-done | bytes 589856 | tf_op jit(solution)/shard_map/ppermute | solution.py:247
  174.3 4.1 %divide_add_fusion = f32[2,1,384,384]{2,3,0,1:T(8,128)} fusion(bf16[2,1,384,384]{2,3,0,1:T(8,128)(2,1)} %collective-permute-done.3, bf16[2,1,384,384]{2,3,0,1:T(8,128)(2,1)} %add_convert_fusion, f32[]{:T(128)} %reduce_max.19, f32[2,1,384,384]{2,3,0,1:T(8,128)S(1)} %copy-done.2, f32[]{:T(128)} %reduce_max.18, ...), kind=kLoop, calls=%fused_computation.52 | loop fusion | flops 2949120 | bytes 4718600 | tf_op jit(solution)/shard_map/add | solution.py:317
  178.4 2.7 %copy.109 = f32[2,1,384,384]{3,2,1,0:T(8,128)} copy(f32[2,1,384,384]{2,3,0,1:T(8,128)} %divide_add_fusion) | data formatting | bytes 2359296
  (95 shorter events, 31.5 us)
Async XLA Ops:
  0.6 4.8 %copy-start = (bf16[32,128,128]{2,1,0:T(8,128)(2,1)S(1)}, bf16[32,128,128]{2,1,0:T(8,128)(2,1)}, u32[]{:S(2)}) copy-start(bf16[32,128,128]{2,1,0:T(8,128)(2,1)} %param.6) | copy-start | bytes 3145732
  7.8 46.4 %all-to-all-start = ((bf16[8,2,3,136,128]{4,3,2,1,0:T(8,128)(2,1)}), bf16[8,2,3,136,128]{4,3,2,1,0:T(8,128)(2,1)S(1)}, u32[]{:S(2)}, u32[]{:S(2)}) async-start(bf16[8,2,3,136,128]{4,3,2,1,0:T(8,128)(2,1)} %copy.96), calls=%async_computation | async-start | bytes 3342336 | tf_op jit(solution)/shard_map/all_to_all | solution.py:330
  15.1 2.7 %copy-start.3 = (f32[4,2,128,128]{3,2,1,0:T(8,128)S(1)}, f32[4,2,128,128]{3,2,1,0:T(8,128)}, u32[]{:S(2)}) copy-start(f32[4,2,128,128]{3,2,1,0:T(8,128)} %probe_ref.1) | copy-start | bytes 1572868
  54.3 0.9 copy-start.5
  54.3 8.0 %copy-start.6 = (bf16[8,1,3,136,128]{4,3,2,1,0:T(8,128)(2,1)}, bf16[8,1,3,136,128]{4,3,2,1,0:T(8,128)(2,1)S(1)}, u32[]{:S(2)}) copy-start(bf16[8,1,3,136,128]{4,3,2,1,0:T(8,128)(2,1)S(1)} %get-tuple-element.28) | copy-start | bytes 2506756
  82.5 8.1 %copy-start.7 = (bf16[2,1,384,384]{2,3,0,1:T(8,128)(2,1)}, bf16[2,1,384,384]{2,3,0,1:T(8,128)(2,1)S(1)}, u32[]{:S(2)}) copy-start(bf16[2,1,384,384]{2,3,0,1:T(8,128)(2,1)S(1)} %fusion.104) | copy-start | bytes 1769476
  82.5 11.5 %copy-start.9 = (s32[24]{0:T(128)S(1)}, s32[24]{0:T(128)}, u32[]{:S(2)}) copy-start(s32[24]{0:T(128)} %get-tuple-element.33) | copy-start | bytes 292
  82.5 11.6 %copy-start.8 = (s32[24]{0:T(128)S(1)}, s32[24]{0:T(128)}, u32[]{:S(2)}) copy-start(s32[24]{0:T(128)} %get-tuple-element.32) | copy-start | bytes 292
  82.5 8.1 %collective-permute-start = (bf16[2,1,384,384]{2,3,0,1:T(8,128)(2,1)S(1)}, bf16[2,1,384,384]{2,3,0,1:T(8,128)(2,1)}, u32[]{:S(2)}, u32[]{:S(2)}) collective-permute-start(bf16[2,1,384,384]{2,3,0,1:T(8,128)(2,1)S(1)} %fusion.104), channel_id=1, source_target_pairs={{0,1},{1,0},{2,3},{3,2},{4,5},{5,4},{6,7},{7,6},{8,9},{9,8},{10,11... | collective-permute-start | bytes 1769480 | tf_op jit(solution)/shard_map/ppermute | solution.py:247
  82.8 21.8 %all-to-all-start.1 = ((f32[32,1,4096]{2,1,0:T(1,128)}), f32[32,1,4096]{2,1,0:T(1,128)S(1)}, u32[]{:S(2)}, u32[]{:S(2)}) async-start(f32[32,1,4096]{2,1,0:T(1,128)} %bitcast.38), calls=%async_computation.1 | async-start | bytes 1048576 | tf_op jit(solution)/shard_map/all_to_all | solution.py:228
  90.6 20.6 %copy-start.2 = (f32[2,1,384,384]{2,3,0,1:T(8,128)S(1)}, f32[2,1,384,384]{2,3,0,1:T(8,128)}, u32[]{:S(2)}) copy-start(f32[2,1,384,384]{2,3,0,1:T(8,128)} %copy.101) | copy-start | bytes 3538948
  92.1 19.1 %collective-permute-start.1 = (bf16[2,1,384,384]{2,3,0,1:T(8,128)(2,1)S(1)}, bf16[2,1,384,384]{2,3,0,1:T(8,128)(2,1)}, u32[]{:S(2)}, u32[]{:S(2)}) collective-permute-start(bf16[2,1,384,384]{2,3,0,1:T(8,128)(2,1)S(1)} %add_convert_fusion.1), channel_id=1, source_target_pairs={{0,2},{1,3},{2,0},{3,1},{4,6},{5,7},{6,4},{7,5},{8,10},{9,11},{10,... | collective-permute-start | bytes 1769480 | tf_op jit(solution)/shard_map/ppermute | solution.py:247
  106.2 18.9 %all-to-all-start.2 = ((f32[32,1,4096]{2,1,0:T(1,128)}), f32[32,1,4096]{2,1,0:T(1,128)}, u32[]{:S(2)}, u32[]{:S(2)}) async-start(f32[32,1,4096]{2,1,0:T(1,128)} %broadcast_in_dim.10), calls=%async_computation.2 | async-start | bytes 1048576 | tf_op jit(solution)/shard_map/all_to_all | solution.py:235
  116.3 10.5 %copy-start.4 = (f32[4,2,128,128]{3,2,1,0:T(8,128)S(1)}, f32[4,2,128,128]{3,2,1,0:T(8,128)}, u32[]{:S(2)}) copy-start(f32[4,2,128,128]{3,2,1,0:T(8,128)} %probe_ref.1) | copy-start | bytes 1572868
  138.6 21.3 %all-to-all-start.3 = ((f32[32,1,4096]{2,1,0:T(1,128)}), f32[32,1,4096]{2,1,0:T(1,128)}, u32[]{:S(2)}, u32[]{:S(2)}) async-start(f32[32,1,4096]{2,1,0:T(1,128)} %bitcast.162), calls=%async_computation.3 | async-start | bytes 1048576 | tf_op jit(solution)/shard_map/all_to_all | solution.py:228
  150.4 15.5 %copy-start.1 = (f32[4,2,128,128]{3,2,1,0:T(8,128)S(1)}, f32[4,2,128,128]{3,2,1,0:T(8,128)}, u32[]{:S(2)}) copy-start(f32[4,2,128,128]{3,2,1,0:T(8,128)} %add.263.probe_ref) | copy-start | bytes 1572868
  150.4 2.2 %collective-permute-start.2 = (bf16[2,1,384,384]{2,3,0,1:T(8,128)(2,1)}, bf16[2,1,384,384]{2,3,0,1:T(8,128)(2,1)S(1)}, u32[]{:S(2)}, u32[]{:S(2)}) collective-permute-start(bf16[2,1,384,384]{2,3,0,1:T(8,128)(2,1)} %fusion.111), channel_id=1, source_target_pairs={{0,1},{1,0},{2,3},{3,2},{4,5},{5,4},{6,7},{7,6},{8,9},{9,8},{10,11... | collective-permute-start | bytes 1769480 | tf_op jit(solution)/shard_map/ppermute | solution.py:247
  154.7 19.6 %collective-permute-start.3 = (bf16[2,1,384,384]{2,3,0,1:T(8,128)(2,1)}, bf16[2,1,384,384]{2,3,0,1:T(8,128)(2,1)}, u32[]{:S(2)}, u32[]{:S(2)}) collective-permute-start(bf16[2,1,384,384]{2,3,0,1:T(8,128)(2,1)} %add_convert_fusion), channel_id=1, source_target_pairs={{0,2},{1,3},{2,0},{3,1},{4,6},{5,7},{6,4},{7,5},{8,10},{9,11},{10,... | collective-permute-start | bytes 1769480 | tf_op jit(solution)/shard_map/ppermute | solution.py:247
  162.6 18.9 %all-to-all-start.4 = ((f32[32,1,4096]{2,1,0:T(1,128)}), f32[32,1,4096]{2,1,0:T(1,128)}, u32[]{:S(2)}, u32[]{:S(2)}) async-start(f32[32,1,4096]{2,1,0:T(1,128)} %broadcast_in_dim.11), calls=%async_computation.4 | async-start | bytes 1048576 | tf_op jit(solution)/shard_map/all_to_all | solution.py:235

commit v10 on v8

--- a/solution.py
+++ b/solution.py
@@ -286,7 +286,16 @@
     spread = jnp.einsum(
         "xskl,scl->xskc", update, pick_cols, preferred_element_type=jnp.float32
     ).astype(jnp.bfloat16)
-    local_sum = jnp.einsum("skq,xskc->xqc", pick_rows, spread, preferred_element_type=jnp.float32)
+    local_sum = jnp.stack(
+        [
+            jnp.dot(
+                pick_rows.reshape(-1, pick_rows.shape[-1]).T,
+                spread[x].reshape(-1, spread.shape[-1]),
+                preferred_element_type=jnp.float32,
+            )
+            for x in range(2)
+        ]
+    )
     return local_sum, probe_grad
 
 

time: 185 us -> 190 us (1.027)
  matrix products: 26.8 us -> 31.7 us
  starting transfers between devices: 34.5 us -> 36.9 us
    dot_general x2 -> x6, matrix products: 11.4 us -> 15.7 us  [the longest x4 10 us: entries_pass(): jnp.dot(pick_rows.reshape(-1, pick_rows.shape[-1]).T, spread[x].reshape(-...]
    unnamed x26 -> x30, local copies, waits for them, and re-layouts: 7.34 us -> 3.68 us
    all_to_all x1, waiting for transfers between devices: 34.4 us -> 37.1 us  [on_device(): lax.all_to_all(jnp.swapaxes(payload, 0, 1), 'tile', 0, 0, tiled=True)]
    all_to_all x2, waiting for transfers between devices: 13.9 us -> 11.6 us  [sum_over(): lax.all_to_all(value.astype(send_type).reshape(count, -1), axes, 0, 0, ti...]
    all_to_all x2, starting transfers between devices: 17.3 us -> 19.3 us  [sum_over(): lax.all_to_all(value.astype(send_type).reshape(count, -1), axes, 0, 0, ti...]
  transfers between devices with their start and end apart: 9 -> 9, of which waited for: 8 -> 8; matrix products, arithmetic and copies ran while one was open for 21% -> 19% of each run, Pallas kernels for 0% -> 0%
where the time goes in v10:
time: 190 us; the launch traced here: 188 us
  waiting for transfers between devices  65.2 us (34%)
  starting transfers between devices  36.9 us (19%)
  matrix products  31.7 us (17%)
  other arithmetic  27.4 us (14%)
  Pallas kernels  15.2 us (8%)
  local copies, waits for them, and re-layouts  10.8 us (6%)
    all_to_all x1, waiting for transfers between devices, on_device(): lax.all_to_all(jnp.swapaxes(payload, 0, 1), 'tile', 0, 0, tiled=True)  37.1 us
    all_to_all x2, starting transfers between devices, sum_over(): lax.all_to_all(value.astype(send_type).reshape(count, -1), axes, 0, 0, ti...  19.3 us
    pallas_call x2, Pallas kernels, entries_kernel(): pl.pallas_call(entry_kernel, grid_spec=grid_spec, out_shape=[jax.ShapeDty...  15.2 us
    ppermute x4, waiting for transfers between devices, all_sum_pairs(): other = lax.ppermute(total.astype(send_type), axis, pairs)  12 us
    all_to_all x2, waiting for transfers between devices, sum_over(): lax.all_to_all(value.astype(send_type).reshape(count, -1), axes, 0, 0, ti...  11.6 us
    dot_general x2, matrix products, entries_pass(): jnp.einsum('skq,xqc->xskc', pick_rows, stacked, preferred_element_type=jn...  10.1 us
    dot_general x4, matrix products, entries_pass(): jnp.dot(pick_rows.reshape(-1, pick_rows.shape[-1]).T, spread[x].reshape(-...  10 us
    all_to_all x1, starting transfers between devices, on_device(): lax.all_to_all(jnp.swapaxes(payload, 0, 1), 'tile', 0, 0, tiled=True)  7.41 us
  transfers between devices with their start and end apart: 9, of which 8 were waited for; matrix products, arithmetic and copies ran while one was open for 19% of the time, Pallas kernels for 0%

profile of v10, /device:TPU:0, one launch (start us, length us, event | category | flops | bytes accessed | tf_op | source)
XLA Modules:
  0.0 188.2 jit_solution(7521572633378781349)
XLA Ops:
  7.8 7.4 %all-to-all-start = ((bf16[8,2,3,136,128]{4,3,2,1,0:T(8,128)(2,1)}), bf16[8,2,3,136,128]{4,3,2,1,0:T(8,128)(2,1)S(1)}, u32[]{:S(2)}, u32[]{:S(2)}) async-start(bf16[8,2,3,136,128]{4,3,2,1,0:T(8,128)(2,1)} %copy.104), calls=%async_computation | async-start | bytes 3342336 | tf_op jit(solution)/shard_map/all_to_all | solution.py:339
  17.3 37.1 %all-to-all-done = bf16[8,2,3,136,128]{4,3,2,1,0:T(8,128)(2,1)S(1)} async-done(((bf16[8,2,3,136,128]{4,3,2,1,0:T(8,128)(2,1)}), bf16[8,2,3,136,128]{4,3,2,1,0:T(8,128)(2,1)S(1)}, u32[]{:S(2)}, u32[]{:S(2)}) %all-to-all-start) | async-done | bytes 1671200 | tf_op jit(solution)/shard_map/all_to_all | solution.py:339
  60.8 4.4 %convert_bitcast_fusion.3 = bf16[2,24,128,384]{3,2,0,1:T(8,128)(2,1)S(1)} fusion(s32[24,128]{1,0:T(8,128)S(1)} %get-tuple-element.31, pred[24]{0:T(512)(128)(4,1)S(1)} %reduce.4, f32[2,1,384,384]{3,2,1,0:T(8,128)} %param.10), kind=kOutput, calls=%fused_computation.13 | convolution fusion | flops 1816952832 | bytes 5910552 | tf_op jit(solution)/shard_map/skq,xqc->xskc/dot_general | solution.py:268
  65.2 2.6 %fusion.73.patch_ref = bf16[2,24,128,128]{3,2,1,0:T(8,128)(2,1)} fusion(bf16[2,24,128,384]{3,2,0,1:T(8,128)(2,1)S(1)} %convert_bitcast_fusion.3, s32[24,128]{1,0:T(8,128)S(1)} %get-tuple-element.32), kind=kOutput, calls=%fused_computation.55 | convolution fusion | flops 605945856 | bytes 6303744 | tf_op jit(solution)/shard_map/xskc,scl->xskl/dot_general | solution.py:271
  67.8 7.7 %shard_map.77 = (bf16[2,24,128,128]{3,2,1,0:T(8,128)(2,1)}, f32[4,2,128,128]{3,2,1,0:T(8,128)}) custom-call(s32[25]{0:T(128)} %pad_add_fusion.order_ref, bf16[2,24,128,128]{3,2,1,0:T(8,128)(2,1)} %fusion.73.patch_ref, bf16[24,136,128]{2,1,0:T(8,128)(2,1)} %bitcast.126, f32[4,2,128,128]{3,2,1,0:T(8,128)} %probe_ref.1, ...), custom_call_target="tpu_custom_call" | custom-call | flops 6442450944 | bytes 4980736 | tf_op jit(solution)/shard_map/pallas_call | solution.py:169
  75.5 2.8 %convert_bitcast_fusion.2 = bf16[2,24,128,384]{3,2,0,1:T(8,128)(2,1)S(1)} fusion(s32[24,128]{1,0:T(8,128)S(1)} %get-tuple-element.32, bf16[2,24,128,128]{3,2,1,0:T(8,128)(2,1)} %get-tuple-element.6), kind=kOutput, calls=%fused_computation.12 | convolution fusion | flops 607518720 | bytes 6303744 | tf_op jit(solution)/shard_map/xskl,scl->xskc/dot_general | solution.py:286
  79.1 2.5 %fusion.93 = bf16[1,1,384,384]{3,2,1,0:T(8,128)(2,1)S(1)} fusion(bf16[3072,384]{1,0:T(8,128)(2,1)S(1)} %bitcast.119, s32[3072]{0:T(1024)S(1)} %get-tuple-element.30, pred[3072]{0:T(1024)(128)(4,1)S(1)} %broadcast_bitcast_fusion.1), kind=kOutput, calls=%fused_computation.65 | convolution fusion | flops 908476416 | bytes 2669568 | tf_op jit(solution)/shard_map/dot_general | solution.py:291
  81.7 2.5 %fusion.90 = bf16[1,1,384,384]{3,2,1,0:T(8,128)(2,1)S(1)} fusion(bf16[3072,384]{1,0:T(8,128)(2,1)S(1)} %bitcast.117, s32[3072]{0:T(1024)S(1)} %get-tuple-element.30, pred[3072]{0:T(1024)(128)(4,1)S(1)} %broadcast_bitcast_fusion.1), kind=kOutput, calls=%fused_computation.64 | convolution fusion | flops 908476416 | bytes 2669568 | tf_op jit(solution)/shard_map/dot_general | solution.py:291
  84.4 9.8 %all-to-all-start.1 = ((f32[32,1,4096]{2,1,0:T(1,128)}), f32[32,1,4096]{2,1,0:T(1,128)S(1)}, u32[]{:S(2)}, u32[]{:S(2)}) async-start(f32[32,1,4096]{2,1,0:T(1,128)} %bitcast.127), calls=%async_computation.1 | async-start | bytes 1048576 | tf_op jit(solution)/shard_map/all_to_all | solution.py:228
  97.4 1.8 collective-permute-start.1
  99.4 10.4 %all-to-all-done.1 = f32[32,1,4096]{2,1,0:T(1,128)S(1)} async-done(((f32[32,1,4096]{2,1,0:T(1,128)}), f32[32,1,4096]{2,1,0:T(1,128)S(1)}, u32[]{:S(2)}, u32[]{:S(2)}) %all-to-all-start.1) | async-done | bytes 524320 | tf_op jit(solution)/shard_map/all_to_all | solution.py:228
  111.4 3.3 %all-to-all-start.2 = ((f32[32,1,4096]{2,1,0:T(1,128)}), f32[32,1,4096]{2,1,0:T(1,128)S(1)}, u32[]{:S(2)}, u32[]{:S(2)}) async-start(f32[32,1,4096]{2,1,0:T(1,128)} %broadcast_in_dim.10), calls=%async_computation.2 | async-start | bytes 1048576 | tf_op jit(solution)/shard_map/all_to_all | solution.py:235
  117.1 5.7 %convert_bitcast_fusion.1 = bf16[2,24,128,384]{2,3,0,1:T(8,128)(2,1)S(1)} fusion(s32[24,128]{1,0:T(8,128)S(1)} %get-tuple-element.29, pred[24]{0:T(512)(128)(4,1)S(1)} %copy-done.12, f32[2,1,384,384]{3,2,1,0:T(8,128)} %param.10, bf16[2,1,384,384]{3,2,1,0:T(8,128)(2,1)S(1)} %collective-permute-done.1, bf16[2,1,384,384]{3,2,1,0:T(8,128)(2,1)} %add_convert_fusion.1, ...), kind=kOutput, calls=%fused_computation.6 | convolution fusion | flops 1818427392 | bytes 7090204 | tf_op jit(solution)/shard_map/skq,xqc->xskc/dot_general | solution.py:268
  122.8 3.3 %fusion.68.patch_ref = bf16[2,24,128,128]{3,2,1,0:T(8,128)(2,1)} fusion(bf16[2,24,128,384]{2,3,0,1:T(8,128)(2,1)S(1)} %convert_bitcast_fusion.1, s32[24,128]{1,0:T(8,128)S(1)} %iota_add_fusion), kind=kOutput, calls=%fused_computation.54 | convolution fusion | flops 605945856 | bytes 6303744 | tf_op jit(solution)/shard_map/xskc,scl->xskl/dot_general | solution.py:271
  126.1 4.0 %all-to-all-done.2 = f32[32,1,4096]{2,1,0:T(1,128)S(1)} async-done(((f32[32,1,4096]{2,1,0:T(1,128)}), f32[32,1,4096]{2,1,0:T(1,128)S(1)}, u32[]{:S(2)}, u32[]{:S(2)}) %all-to-all-start.2) | async-done | bytes 524320 | tf_op jit(solution)/shard_map/all_to_all | solution.py:235
  131.6 7.5 %shard_map.78 = (bf16[2,24,128,128]{3,2,1,0:T(8,128)(2,1)}, f32[4,2,128,128]{3,2,1,0:T(8,128)}) custom-call(s32[25]{0:T(128)} %pad_add_fusion.1.order_ref, bf16[2,24,128,128]{3,2,1,0:T(8,128)(2,1)} %fusion.68.patch_ref, bf16[24,136,128]{2,1,0:T(8,128)(2,1)} %bitcast.124, f32[4,2,128,128]{3,2,1,0:T(8,128)} %add.273.probe_ref, ...), custom_call_target="tpu_custom_call" | custom-call | flops 6442450944 | bytes 4980736 | tf_op jit(solution)/shard_map/pallas_call | solution.py:169
  139.1 9.5 %all-to-all-start.3 = ((f32[32,1,4096]{2,1,0:T(1,128)}), f32[32,1,4096]{2,1,0:T(1,128)}, u32[]{:S(2)}, u32[]{:S(2)}) async-start(f32[32,1,4096]{2,1,0:T(1,128)} %bitcast.128), calls=%async_computation.3 | async-start | bytes 1048576 | tf_op jit(solution)/shard_map/all_to_all | solution.py:228
  148.6 2.8 %convert_bitcast_fusion = bf16[2,24,128,384]{3,2,0,1:T(8,128)(2,1)S(1)} fusion(s32[24,128]{1,0:T(8,128)S(1)} %iota_add_fusion, bf16[2,24,128,128]{3,2,1,0:T(8,128)(2,1)} %get-tuple-element.8), kind=kOutput, calls=%fused_computation.5 | convolution fusion | flops 607518720 | bytes 6303744 | tf_op jit(solution)/shard_map/xskl,scl->xskc/dot_general | solution.py:286
  152.3 2.5 %fusion.99 = bf16[1,1,384,384]{3,2,1,0:T(8,128)(2,1)S(1)} fusion(bf16[3072,384]{1,0:T(8,128)(2,1)S(1)} %bitcast.120, s32[3072]{0:T(1024)S(1)} %get-tuple-element.28, pred[3072]{0:T(1024)(128)(4,1)S(1)} %broadcast_bitcast_fusion), kind=kOutput, calls=%fused_computation.67 | convolution fusion | flops 908476416 | bytes 2669568 | tf_op jit(solution)/shard_map/dot_general | solution.py:291
  154.8 2.5 %fusion.96 = bf16[1,1,384,384]{3,2,1,0:T(8,128)(2,1)S(1)} fusion(bf16[3072,384]{1,0:T(8,128)(2,1)S(1)} %bitcast.118, s32[3072]{0:T(1024)S(1)} %get-tuple-element.28, pred[3072]{0:T(1024)(128)(4,1)S(1)} %broadcast_bitcast_fusion), kind=kOutput, calls=%fused_computation.66 | convolution fusion | flops 908476416 | bytes 2669568 | tf_op jit(solution)/shard_map/dot_general | solution.py:291
  157.5 2.0 %collective-permute-done.2 = bf16[2,1,384,384]{3,2,1,0:T(8,128)(2,1)S(1)} collective-permute-done((bf16[2,1,384,384]{3,2,1,0:T(8,128)(2,1)S(1)}, bf16[2,1,384,384]{3,2,1,0:T(8,128)(2,1)S(1)}, u32[]{:S(2)}, u32[]{:S(2)}) %collective-permute-start.2) | collective-permute-done | bytes 589856 | tf_op jit(solution)/shard_map/ppermute | solution.py:247
  166.6 3.6 %all-to-all-start.4 = ((f32[32,1,4096]{2,1,0:T(1,128)}), f32[32,1,4096]{2,1,0:T(1,128)}, u32[]{:S(2)}, u32[]{:S(2)}) async-start(f32[32,1,4096]{2,1,0:T(1,128)} %broadcast_in_dim.11), calls=%async_computation.4 | async-start | bytes 1048576 | tf_op jit(solution)/shard_map/all_to_all | solution.py:235
  170.8 9.7 %collective-permute-done.3 = bf16[2,1,384,384]{3,2,1,0:T(8,128)(2,1)} collective-permute-done((bf16[2,1,384,384]{3,2,1,0:T(8,128)(2,1)}, bf16[2,1,384,384]{3,2,1,0:T(8,128)(2,1)}, u32[]{:S(2)}, u32[]{:S(2)}) %collective-permute-start.3) | collective-permute-done | bytes 589856 | tf_op jit(solution)/shard_map/ppermute | solution.py:247
  180.5 4.7 %divide_add_fusion = f32[2,1,384,384]{3,2,1,0:T(8,128)} fusion(bf16[2,1,384,384]{3,2,1,0:T(8,128)(2,1)} %collective-permute-done.3, f32[]{:T(128)} %reduce_max.19, f32[2,1,384,384]{3,2,1,0:T(8,128)} %param.10, f32[]{:T(128)} %reduce_max.18, bf16[2,1,384,384]{3,2,1,0:T(8,128)(2,1)} %copy-done.7, bf16[2,1,384,384]{3,2,1,0:T(8,128)(2,1)} %copy-done.2, ...), kind=kLoop, calls=%fused_computation.60 | loop fusion | flops 5898240 | bytes 5898248 | tf_op jit(solution)/shard_map/add | solution.py:326
  (109 shorter events, 37.2 us)
Async XLA Ops:
  0.6 4.9 %copy-start = (bf16[32,128,128]{2,1,0:T(8,128)(2,1)S(1)}, bf16[32,128,128]{2,1,0:T(8,128)(2,1)}, u32[]{:S(2)}) copy-start(bf16[32,128,128]{2,1,0:T(8,128)(2,1)} %param.6) | copy-start | bytes 3145732
  7.8 7.4 %copy-start.3 = (f32[4,2,128,128]{3,2,1,0:T(8,128)S(1)}, f32[4,2,128,128]{3,2,1,0:T(8,128)}, u32[]{:S(2)}) copy-start(f32[4,2,128,128]{3,2,1,0:T(8,128)} %probe_ref.1) | copy-start | bytes 1572868
  7.8 46.5 %all-to-all-start = ((bf16[8,2,3,136,128]{4,3,2,1,0:T(8,128)(2,1)}), bf16[8,2,3,136,128]{4,3,2,1,0:T(8,128)(2,1)S(1)}, u32[]{:S(2)}, u32[]{:S(2)}) async-start(bf16[8,2,3,136,128]{4,3,2,1,0:T(8,128)(2,1)} %copy.104), calls=%async_computation | async-start | bytes 3342336 | tf_op jit(solution)/shard_map/all_to_all | solution.py:339
  54.4 0.9 copy-start.6
  54.5 10.7 %copy-start.5 = (bf16[8,1,3,136,128]{4,3,2,1,0:T(8,128)(2,1)}, bf16[8,1,3,136,128]{4,3,2,1,0:T(8,128)(2,1)S(1)}, u32[]{:S(2)}) copy-start(bf16[8,1,3,136,128]{4,3,2,1,0:T(8,128)(2,1)S(1)} %get-tuple-element.19) | copy-start | bytes 2506756
  57.2 27.2 %copy-start.9 = (pred[24,1]{1,0:T(8,128)(4,1)}, pred[24,1]{1,0:T(8,128)(4,1)S(1)}, u32[]{:S(2)}) copy-start(pred[24,1]{1,0:T(8,128)(4,1)S(1)} %get-tuple-element.13) | copy-start | bytes 76
  84.2 10.1 %copy-start.12 = (pred[24]{0:T(512)(128)(4,1)S(1)}, pred[24]{0:T(512)(128)(4,1)}, u32[]{:S(2)}) copy-start(pred[24]{0:T(512)(128)(4,1)} %reduce.6) | copy-start | bytes 76
  84.2 10.7 %copy-start.8 = (s32[24,1]{1,0:T(8,128)S(1)}, s32[24,1]{1,0:T(8,128)}, u32[]{:S(2)}) copy-start(s32[24,1]{1,0:T(8,128)} %reduce-window.16) | copy-start | bytes 292
  84.3 15.0 %copy-start.11 = (s32[24]{0:T(128)S(1)}, s32[24]{0:T(128)}, u32[]{:S(2)}) copy-start(s32[24]{0:T(128)} %get-tuple-element.27) | copy-start | bytes 292
  84.3 15.0 %copy-start.10 = (s32[24]{0:T(128)S(1)}, s32[24]{0:T(128)}, u32[]{:S(2)}) copy-start(s32[24]{0:T(128)} %get-tuple-element.25) | copy-start | bytes 292
  84.3 12.1 %collective-permute-start = (bf16[2,1,384,384]{3,2,1,0:T(8,128)(2,1)S(1)}, bf16[2,1,384,384]{3,2,1,0:T(8,128)(2,1)S(1)}, u32[]{:S(2)}, u32[]{:S(2)}) collective-permute-start(bf16[2,1,384,384]{3,2,1,0:T(8,128)(2,1)S(1)} %pad_maximum_fusion), channel_id=1, source_target_pairs={{0,1},{1,0},{2,3},{3,2},{4,5},{5,4},{6,7},{7,6},{8,9},{9,8},{10,11... | collective-permute-start | bytes 1769480 | tf_op jit(solution)/shard_map/ppermute | solution.py:247
  84.4 25.4 %all-to-all-start.1 = ((f32[32,1,4096]{2,1,0:T(1,128)}), f32[32,1,4096]{2,1,0:T(1,128)S(1)}, u32[]{:S(2)}, u32[]{:S(2)}) async-start(f32[32,1,4096]{2,1,0:T(1,128)} %bitcast.127), calls=%async_computation.1 | async-start | bytes 1048576 | tf_op jit(solution)/shard_map/all_to_all | solution.py:228
  97.4 18.9 %collective-permute-start.1 = (bf16[2,1,384,384]{3,2,1,0:T(8,128)(2,1)}, bf16[2,1,384,384]{3,2,1,0:T(8,128)(2,1)S(1)}, u32[]{:S(2)}, u32[]{:S(2)}) collective-permute-start(bf16[2,1,384,384]{3,2,1,0:T(8,128)(2,1)} %add_convert_fusion.1), channel_id=1, source_target_pairs={{0,2},{1,3},{2,0},{3,1},{4,6},{5,7},{6,4},{7,5},{8,10},{9,11},{10,... | collective-permute-start | bytes 1769480 | tf_op jit(solution)/shard_map/ppermute | solution.py:247
  111.4 18.6 %all-to-all-start.2 = ((f32[32,1,4096]{2,1,0:T(1,128)}), f32[32,1,4096]{2,1,0:T(1,128)S(1)}, u32[]{:S(2)}, u32[]{:S(2)}) async-start(f32[32,1,4096]{2,1,0:T(1,128)} %broadcast_in_dim.10), calls=%async_computation.2 | async-start | bytes 1048576 | tf_op jit(solution)/shard_map/all_to_all | solution.py:235
  116.3 0.8 copy-start.7
  122.8 7.9 %copy-start.4 = (f32[4,2,128,128]{3,2,1,0:T(8,128)S(1)}, f32[4,2,128,128]{3,2,1,0:T(8,128)}, u32[]{:S(2)}) copy-start(f32[4,2,128,128]{3,2,1,0:T(8,128)} %probe_ref.1) | copy-start | bytes 1572868
  139.1 24.8 %all-to-all-start.3 = ((f32[32,1,4096]{2,1,0:T(1,128)}), f32[32,1,4096]{2,1,0:T(1,128)}, u32[]{:S(2)}, u32[]{:S(2)}) async-start(f32[32,1,4096]{2,1,0:T(1,128)} %bitcast.128), calls=%async_computation.3 | async-start | bytes 1048576 | tf_op jit(solution)/shard_map/all_to_all | solution.py:228
  157.4 12.7 %copy-start.1 = (f32[4,2,128,128]{3,2,1,0:T(8,128)S(1)}, f32[4,2,128,128]{3,2,1,0:T(8,128)}, u32[]{:S(2)}) copy-start(f32[4,2,128,128]{3,2,1,0:T(8,128)} %add.273.probe_ref) | copy-start | bytes 1572868
  157.4 2.1 %collective-permute-start.2 = (bf16[2,1,384,384]{3,2,1,0:T(8,128)(2,1)S(1)}, bf16[2,1,384,384]{3,2,1,0:T(8,128)(2,1)S(1)}, u32[]{:S(2)}, u32[]{:S(2)}) collective-permute-start(bf16[2,1,384,384]{3,2,1,0:T(8,128)(2,1)S(1)} %pad_maximum_fusion.1), channel_id=1, source_target_pairs={{0,1},{1,0},{2,3},{3,2},{4,5},{5,4},{6,7},{7,6},{8,9},{9,8},{10,11... | collective-permute-start | bytes 1769480 | tf_op jit(solution)/shard_map/ppermute | solution.py:247
  159.5 0.8 copy-start.2
  161.3 19.2 %collective-permute-start.3 = (bf16[2,1,384,384]{3,2,1,0:T(8,128)(2,1)}, bf16[2,1,384,384]{3,2,1,0:T(8,128)(2,1)}, u32[]{:S(2)}, u32[]{:S(2)}) collective-permute-start(bf16[2,1,384,384]{3,2,1,0:T(8,128)(2,1)} %add_convert_fusion), channel_id=1, source_target_pairs={{0,2},{1,3},{2,0},{3,1},{4,6},{5,7},{6,4},{7,5},{8,10},{9,11},{10,... | collective-permute-start | bytes 1769480 | tf_op jit(solution)/shard_map/ppermute | solution.py:247
  166.6 19.1 %all-to-all-start.4 = ((f32[32,1,4096]{2,1,0:T(1,128)}), f32[32,1,4096]{2,1,0:T(1,128)}, u32[]{:S(2)}, u32[]{:S(2)}) async-start(f32[32,1,4096]{2,1,0:T(1,128)} %broadcast_in_dim.11), calls=%async_computation.4 | async-start | bytes 1048576 | tf_op jit(solution)/shard_map/all_to_all | solution.py:235

commit v11 on v8

--- a/solution.py
+++ b/solution.py
@@ -200,18 +200,16 @@
     fields = jnp.stack(
         [local_tile, scan_offset[:, :, 0], scan_offset[:, :, 1], jnp.ones_like(local_tile)], axis=2
     )
-    meta = jnp.sum(chosen[:, :, :, None] * fields[:, None, :, :], axis=2).astype(jnp.bfloat16)
-    meta = jnp.pad(meta[:, :, None, :], ((0, 0), (0, 0), (0, 7), (0, length - 4)))
+    meta = jnp.sum(chosen[:, :, :, None] * fields[:, None, :, :], axis=2)
     ids = jnp.sum(chosen * batch_ids[:, None, :], axis=2)
-    amp_send = amplitudes[ids.reshape(-1)].reshape(steps, slots, length, length)
-    payload = jnp.concatenate([amp_send, meta], axis=2)
-    return payload.reshape(steps, tile_count, capacity, length + 8, length)
-
-
-def unpack(arrived, size):
+    amp_send = amplitudes[ids.reshape(-1)].reshape(steps, tile_count, capacity, length, length)
+    return amp_send, meta.reshape(steps, tile_count, capacity, 4)
+
+
+def unpack(arrived, meta, size):
     tile_count, capacity, rows, length = arrived.shape
     arrived = arrived.reshape(tile_count * capacity, rows, length)
-    meta = arrived[:, length, :4].astype(jnp.int32)
+    meta = meta.reshape(tile_count * capacity, 4)
     meta_in = jnp.stack([meta[:, 0] * size + meta[:, 1], meta[:, 2], meta[:, 3]], axis=1)
     return arrived, meta_in
 
@@ -305,7 +303,7 @@
 
         start = (jnp.zeros(stacked.shape, jnp.float32), jnp.zeros(probe_now.shape, jnp.float32))
         pieces = (
-            amp_in.reshape(slots // chunk, chunk, length + 8, length),
+            amp_in.reshape(slots // chunk, chunk, length, length),
             meta_in.reshape(slots // chunk, chunk, 3),
         )
         (local_sum, probe_grad), _ = lax.scan(body, start, pieces)
@@ -324,12 +322,13 @@
     tables = dft_tables(probe.shape[-1])
     tiles_here, size = object_tiles.shape[1], object_tiles.shape[2]
     batch_total = batch_ids.shape[1] * lax.axis_size("tile") * lax.axis_size("pat")
-    payload = route(amplitudes, batch_ids, scan_tile, scan_offset, tiles_here)
+    payload, meta = route(amplitudes, batch_ids, scan_tile, scan_offset, tiles_here)
     tiles_now = object_tiles
     probe_now = probe
+    placed = lax.all_to_all(jnp.swapaxes(meta, 0, 1), "tile", 0, 0, tiled=True)
     arrived = lax.all_to_all(jnp.swapaxes(payload, 0, 1), "tile", 0, 0, tiled=True)
     for step_no in range(batch_ids.shape[0]):
-        amp_in, meta_in = unpack(arrived[:, step_no], size)
+        amp_in, meta_in = unpack(arrived[:, step_no], placed[:, step_no], size)
         tiles_now, probe_now, _ = one_step(tiles_now, probe_now, amp_in, meta_in, tables, batch_total)
     return (tiles_now, probe_now)
 

time: 185 us -> 181 us (0.978)
  waiting for transfers between devices: 64.4 us -> 57.1 us
  starting transfers between devices: 34.5 us -> 39.6 us
    all_to_all x1, waiting for transfers between devices: 34.4 us -> 25.6 us  [on_device(): lax.all_to_all(jnp.swapaxes(payload, 0, 1), 'tile', 0, 0, tiled=True)]
    all_to_all x0 -> x1, starting transfers between devices: none -> 7.28 us  [on_device(): placed = lax.all_to_all(jnp.swapaxes(meta, 0, 1), 'tile', 0, 0, tiled=True)]
    unnamed x26 -> x21, local copies, waits for them, and re-layouts: 7.34 us -> 5.31 us
  transfers between devices with their start and end apart: 9 -> 10, of which waited for: 8 -> 7; matrix products, arithmetic and copies ran while one was open for 21% -> 28% of each run, Pallas kernels for 0% -> 0%
where the time goes in v11:
time: 181 us; the launch traced here: 180 us
  waiting for transfers between devices  57.1 us (32%)
  starting transfers between devices  39.6 us (22%)
  other arithmetic  27.8 us (15%)
  matrix products  26.7 us (15%)
  Pallas kernels  15 us (8%)
  local copies, waits for them, and re-layouts  12.6 us (7%)
    all_to_all x1, waiting for transfers between devices, on_device(): lax.all_to_all(jnp.swapaxes(payload, 0, 1), 'tile', 0, 0, tiled=True)  25.6 us
    all_to_all x2, starting transfers between devices, sum_over(): lax.all_to_all(value.astype(send_type).reshape(count, -1), axes, 0, 0, ti...  16.1 us
    all_to_all x2, waiting for transfers between devices, sum_over(): lax.all_to_all(value.astype(send_type).reshape(count, -1), axes, 0, 0, ti...  15.4 us
    pallas_call x2, Pallas kernels, entries_kernel(): pl.pallas_call(entry_kernel, grid_spec=grid_spec, out_shape=[jax.ShapeDty...  15 us
    dot_general x2, matrix products, entries_pass(): jnp.einsum('skq,xskc->xqc', pick_rows, spread, preferred_element_type=jnp...  11.4 us
    ppermute x4, waiting for transfers between devices, all_sum_pairs(): other = lax.ppermute(total.astype(send_type), axis, pairs)  9.81 us
    dot_general x2, matrix products, entries_pass(): jnp.einsum('skq,xqc->xskc', pick_rows, stacked, preferred_element_type=jn...  9.39 us
    all_to_all x1, starting transfers between devices, on_device(): placed = lax.all_to_all(jnp.swapaxes(meta, 0, 1), 'tile', 0, 0, tiled=True)  7.28 us
  transfers between devices with their start and end apart: 10, of which 7 were waited for; matrix products, arithmetic and copies ran while one was open for 28% of the time, Pallas kernels for 0%

profile of v11, /device:TPU:0, one launch (start us, length us, event | category | flops | bytes accessed | tf_op | source)
XLA Modules:
  0.0 179.8 jit_solution(17450395127008541112)
XLA Ops:
  5.3 7.3 %all-to-all-start = ((s32[8,2,3,4]{3,1,2,0:T(2,128)}), s32[8,2,3,4]{3,1,2,0:T(2,128)S(1)}, u32[]{:S(2)}, u32[]{:S(2)}) async-start(s32[8,2,3,4]{3,1,2,0:T(2,128)} %copy.56), calls=%async_computation | async-start | bytes 49152 | tf_op jit(solution)/shard_map/all_to_all | solution.py:328
  20.1 6.0 %all-to-all-start.1 = ((bf16[8,2,3,128,128]{4,3,2,1,0:T(8,128)(2,1)}), bf16[8,2,3,128,128]{4,3,2,1,0:T(8,128)(2,1)S(1)}, u32[]{:S(2)}, u32[]{:S(2)}) async-start(bf16[8,2,3,128,128]{4,3,2,1,0:T(8,128)(2,1)} %copy.62), calls=%async_computation.1 | async-start | bytes 3145728 | tf_op jit(solution)/shard_map/all_to_all | solution.py:329
  29.9 4.4 %convert_bitcast_fusion.1 = bf16[2,24,128,384]{3,2,0,1:T(8,128)(2,1)S(1)} fusion(s32[24,128]{1,0:T(8,128)S(1)} %get-tuple-element.38, pred[24]{0:T(512)(128)(4,1)S(1)} %reduce.4, f32[2,1,384,384]{3,2,1,0:T(8,128)} %param.10), kind=kOutput, calls=%fused_computation.14 | convolution fusion | flops 1816952832 | bytes 5910552 | tf_op jit(solution)/shard_map/skq,xqc->xskc/dot_general | solution.py:266
  34.3 2.6 %fusion.71.patch_ref = bf16[2,24,128,128]{3,2,1,0:T(8,128)(2,1)} fusion(bf16[2,24,128,384]{3,2,0,1:T(8,128)(2,1)S(1)} %convert_bitcast_fusion.1, s32[24,128]{1,0:T(8,128)S(1)} %get-tuple-element.39), kind=kOutput, calls=%fused_computation.44 | convolution fusion | flops 605945856 | bytes 6303744 | tf_op jit(solution)/shard_map/xskc,scl->xskl/dot_general | solution.py:269
  36.9 25.6 %all-to-all-done.1 = bf16[8,2,3,128,128]{4,3,2,1,0:T(8,128)(2,1)S(1)} async-done(((bf16[8,2,3,128,128]{4,3,2,1,0:T(8,128)(2,1)}), bf16[8,2,3,128,128]{4,3,2,1,0:T(8,128)(2,1)S(1)}, u32[]{:S(2)}, u32[]{:S(2)}) %all-to-all-start.1) | async-done | bytes 1572896 | tf_op jit(solution)/shard_map/all_to_all | solution.py:329
  63.8 7.5 %shard_map.77 = (bf16[2,24,128,128]{3,2,1,0:T(8,128)(2,1)}, f32[4,2,128,128]{3,2,1,0:T(8,128)}) custom-call(s32[25]{0:T(128)} %pad_add_fusion.order_ref, bf16[2,24,128,128]{3,2,1,0:T(8,128)(2,1)} %fusion.71.patch_ref, bf16[24,128,128]{2,1,0:T(8,128)(2,1)} %bitcast.157, f32[4,2,128,128]{3,2,1,0:T(8,128)} %probe_ref.1, ...), custom_call_target="tpu_custom_call" | custom-call | flops 6442450944 | bytes 4980736 | tf_op jit(solution)/shard_map/pallas_call | solution.py:169
  71.2 5.3 %fusion.104 = bf16[2,1,384,384]{2,3,0,1:T(8,128)(2,1)S(1)} fusion(s32[24,128]{1,0:T(8,128)S(1)} %get-tuple-element.38, pred[24]{0:T(512)(128)(4,1)S(1)} %reduce.4, bf16[2,24,128,128]{3,2,1,0:T(8,128)(2,1)} %get-tuple-element.6, s32[24,128]{1,0:T(8,128)S(1)} %get-tuple-element.39), kind=kOutput, calls=%fused_computation.49 | convolution fusion | flops 2422112256 | bytes 2187288 | tf_op jit(solution)/shard_map/skq,xskc->xqc/dot_general | solution.py:287
  78.1 7.4 %all-to-all-start.2 = ((f32[32,1,4096]{2,1,0:T(1,128)}), f32[32,1,4096]{2,1,0:T(1,128)S(1)}, u32[]{:S(2)}, u32[]{:S(2)}) async-start(f32[32,1,4096]{2,1,0:T(1,128)} %bitcast.37), calls=%async_computation.2 | async-start | bytes 1048576 | tf_op jit(solution)/shard_map/all_to_all | solution.py:226
  89.1 11.9 %all-to-all-done.2 = f32[32,1,4096]{2,1,0:T(1,128)S(1)} async-done(((f32[32,1,4096]{2,1,0:T(1,128)}), f32[32,1,4096]{2,1,0:T(1,128)S(1)}, u32[]{:S(2)}, u32[]{:S(2)}) %all-to-all-start.2) | async-done | bytes 524320 | tf_op jit(solution)/shard_map/all_to_all | solution.py:226
  102.6 3.3 %all-to-all-start.3 = ((f32[32,1,4096]{2,1,0:T(1,128)}), f32[32,1,4096]{2,1,0:T(1,128)}, u32[]{:S(2)}, u32[]{:S(2)}) async-start(f32[32,1,4096]{2,1,0:T(1,128)} %broadcast_in_dim.10), calls=%async_computation.3 | async-start | bytes 1048576 | tf_op jit(solution)/shard_map/all_to_all | solution.py:233
  107.1 5.0 %convert_bitcast_fusion = bf16[2,24,128,384]{2,3,0,1:T(8,128)(2,1)S(1)} fusion(s32[24,128]{1,0:T(8,128)S(1)} %iota_add_fusion, pred[24]{0:T(512)(128)(4,1)S(1)} %reduce.6, f32[2,1,384,384]{2,3,0,1:T(8,128)S(1)} %copy-done.2, bf16[2,1,384,384]{2,3,0,1:T(8,128)(2,1)} %collective-permute-done.1, bf16[2,1,384,384]{2,3,0,1:T(8,128)(2,1)S(1)} %add_convert_fusion.1, ...), kind=kOutput, calls=%fused_computation.10 | convolution fusion | flops 1818427392 | bytes 7090204 | tf_op jit(solution)/shard_map/skq,xqc->xskc/dot_general | solution.py:266
  112.2 3.3 %fusion.66.patch_ref = bf16[2,24,128,128]{3,2,1,0:T(8,128)(2,1)} fusion(bf16[2,24,128,384]{2,3,0,1:T(8,128)(2,1)S(1)} %convert_bitcast_fusion, s32[24,128]{1,0:T(8,128)S(1)} %iota_add_fusion.1), kind=kOutput, calls=%fused_computation.43 | convolution fusion | flops 605945856 | bytes 6303744 | tf_op jit(solution)/shard_map/xskc,scl->xskl/dot_general | solution.py:269
  115.5 6.0 %all-to-all-done.3 = f32[32,1,4096]{2,1,0:T(1,128)} async-done(((f32[32,1,4096]{2,1,0:T(1,128)}), f32[32,1,4096]{2,1,0:T(1,128)}, u32[]{:S(2)}, u32[]{:S(2)}) %all-to-all-start.3) | async-done | bytes 524320 | tf_op jit(solution)/shard_map/all_to_all | solution.py:233
  124.0 7.5 %shard_map.78 = (bf16[2,24,128,128]{3,2,1,0:T(8,128)(2,1)}, f32[4,2,128,128]{3,2,1,0:T(8,128)}) custom-call(s32[25]{0:T(128)} %pad_add_fusion.1.order_ref, bf16[2,24,128,128]{3,2,1,0:T(8,128)(2,1)} %fusion.66.patch_ref, bf16[24,128,128]{2,1,0:T(8,128)(2,1)} %bitcast.156, f32[4,2,128,128]{3,2,1,0:T(8,128)} %add.261.probe_ref, ...), custom_call_target="tpu_custom_call" | custom-call | flops 6442450944 | bytes 4980736 | tf_op jit(solution)/shard_map/pallas_call | solution.py:169
  131.5 8.7 %all-to-all-start.4 = ((f32[32,1,4096]{2,1,0:T(1,128)}), f32[32,1,4096]{2,1,0:T(1,128)}, u32[]{:S(2)}, u32[]{:S(2)}) async-start(f32[32,1,4096]{2,1,0:T(1,128)} %bitcast.158), calls=%async_computation.4 | async-start | bytes 1048576 | tf_op jit(solution)/shard_map/all_to_all | solution.py:226
  140.2 6.1 %fusion.111 = bf16[2,1,384,384]{2,3,0,1:T(8,128)(2,1)} fusion(s32[24,128]{1,0:T(8,128)S(1)} %iota_add_fusion, pred[24]{0:T(512)(128)(4,1)S(1)} %reduce.6, bf16[2,24,128,128]{3,2,1,0:T(8,128)(2,1)} %get-tuple-element.8, s32[24,128]{1,0:T(8,128)S(1)} %iota_add_fusion.1), kind=kOutput, calls=%fused_computation.50 | convolution fusion | flops 2422112256 | bytes 2187288 | tf_op jit(solution)/shard_map/skq,xskc->xqc/dot_general | solution.py:287
  146.5 2.0 %collective-permute-done.2 = bf16[2,1,384,384]{2,3,0,1:T(8,128)(2,1)S(1)} collective-permute-done((bf16[2,1,384,384]{2,3,0,1:T(8,128)(2,1)}, bf16[2,1,384,384]{2,3,0,1:T(8,128)(2,1)S(1)}, u32[]{:S(2)}, u32[]{:S(2)}) %collective-permute-start.2) | collective-permute-done | bytes 589856 | tf_op jit(solution)/shard_map/ppermute | solution.py:245
  148.5 2.0 %add_convert_fusion = bf16[2,1,384,384]{2,3,0,1:T(8,128)(2,1)} fusion(bf16[2,1,384,384]{2,3,0,1:T(8,128)(2,1)S(1)} %collective-permute-done.2, bf16[2,1,384,384]{2,3,0,1:T(8,128)(2,1)} %fusion.111), kind=kLoop, calls=%fused_computation.52 | loop fusion | flops 1179648 | bytes 1769472 | tf_op jit(solution)/shard_map/convert_element_type | solution.py:246
  150.6 1.7 collective-permute-start.3
  152.3 3.5 %all-to-all-done.4 = f32[32,1,4096]{2,1,0:T(1,128)} async-done(((f32[32,1,4096]{2,1,0:T(1,128)}), f32[32,1,4096]{2,1,0:T(1,128)}, u32[]{:S(2)}, u32[]{:S(2)}) %all-to-all-start.4) | async-done | bytes 524320 | tf_op jit(solution)/shard_map/all_to_all | solution.py:226
  158.4 3.3 %all-to-all-start.5 = ((f32[32,1,4096]{2,1,0:T(1,128)}), f32[32,1,4096]{2,1,0:T(1,128)}, u32[]{:S(2)}, u32[]{:S(2)}) async-start(f32[32,1,4096]{2,1,0:T(1,128)} %broadcast_in_dim.11), calls=%async_computation.5 | async-start | bytes 1048576 | tf_op jit(solution)/shard_map/all_to_all | solution.py:233
  162.4 7.8 %collective-permute-done.3 = bf16[2,1,384,384]{2,3,0,1:T(8,128)(2,1)} collective-permute-done((bf16[2,1,384,384]{2,3,0,1:T(8,128)(2,1)}, bf16[2,1,384,384]{2,3,0,1:T(8,128)(2,1)}, u32[]{:S(2)}, u32[]{:S(2)}) %collective-permute-start.3) | collective-permute-done | bytes 589856 | tf_op jit(solution)/shard_map/ppermute | solution.py:245
  170.2 4.1 %divide_add_fusion = f32[2,1,384,384]{2,3,0,1:T(8,128)} fusion(bf16[2,1,384,384]{2,3,0,1:T(8,128)(2,1)} %collective-permute-done.3, bf16[2,1,384,384]{2,3,0,1:T(8,128)(2,1)} %add_convert_fusion, f32[]{:T(128)} %reduce_max.19, f32[2,1,384,384]{2,3,0,1:T(8,128)S(1)} %copy-done.2, f32[]{:T(128)} %reduce_max.18, ...), kind=kLoop, calls=%fused_computation.51 | loop fusion | flops 2949120 | bytes 4718600 | tf_op jit(solution)/shard_map/add | solution.py:315
  174.2 2.7 %copy.71 = f32[2,1,384,384]{3,2,1,0:T(8,128)} copy(f32[2,1,384,384]{2,3,0,1:T(8,128)} %divide_add_fusion) | data formatting | bytes 2359296
  (90 shorter events, 34.0 us)
Async XLA Ops:
  0.6 16.7 %copy-start = (bf16[32,128,128]{2,1,0:T(8,128)(2,1)S(1)}, bf16[32,128,128]{2,1,0:T(8,128)(2,1)}, u32[]{:S(2)}) copy-start(bf16[32,128,128]{2,1,0:T(8,128)(2,1)} %param.6) | copy-start | bytes 3145732
  0.6 15.3 %copy-start.4 = (f32[2,1,384,384]{3,2,1,0:T(8,128)S(1)}, f32[2,1,384,384]{3,2,1,0:T(8,128)}, u32[]{:S(2)}) copy-start(f32[2,1,384,384]{3,2,1,0:T(8,128)} %param.10) | copy-start | bytes 3538948
  5.3 14.8 %all-to-all-start = ((s32[8,2,3,4]{3,1,2,0:T(2,128)}), s32[8,2,3,4]{3,1,2,0:T(2,128)S(1)}, u32[]{:S(2)}, u32[]{:S(2)}) async-start(s32[8,2,3,4]{3,1,2,0:T(2,128)} %copy.56), calls=%async_computation | async-start | bytes 49152 | tf_op jit(solution)/shard_map/all_to_all | solution.py:328
  20.1 42.4 %all-to-all-start.1 = ((bf16[8,2,3,128,128]{4,3,2,1,0:T(8,128)(2,1)}), bf16[8,2,3,128,128]{4,3,2,1,0:T(8,128)(2,1)S(1)}, u32[]{:S(2)}, u32[]{:S(2)}) async-start(bf16[8,2,3,128,128]{4,3,2,1,0:T(8,128)(2,1)} %copy.62), calls=%async_computation.1 | async-start | bytes 3145728 | tf_op jit(solution)/shard_map/all_to_all | solution.py:329
  76.5 9.0 %copy-start.5 = (bf16[2,1,384,384]{2,3,0,1:T(8,128)(2,1)}, bf16[2,1,384,384]{2,3,0,1:T(8,128)(2,1)S(1)}, u32[]{:S(2)}) copy-start(bf16[2,1,384,384]{2,3,0,1:T(8,128)(2,1)S(1)} %fusion.104) | copy-start | bytes 1769476
  76.5 9.1 %collective-permute-start = (bf16[2,1,384,384]{2,3,0,1:T(8,128)(2,1)S(1)}, bf16[2,1,384,384]{2,3,0,1:T(8,128)(2,1)}, u32[]{:S(2)}, u32[]{:S(2)}) collective-permute-start(bf16[2,1,384,384]{2,3,0,1:T(8,128)(2,1)S(1)} %fusion.104), channel_id=1, source_target_pairs={{0,1},{1,0},{2,3},{3,2},{4,5},{5,4},{6,7},{7,6},{8,9},{9,8},{10,11... | collective-permute-start | bytes 1769480 | tf_op jit(solution)/shard_map/ppermute | solution.py:245
  78.1 22.8 %all-to-all-start.2 = ((f32[32,1,4096]{2,1,0:T(1,128)}), f32[32,1,4096]{2,1,0:T(1,128)S(1)}, u32[]{:S(2)}, u32[]{:S(2)}) async-start(f32[32,1,4096]{2,1,0:T(1,128)} %bitcast.37), calls=%async_computation.2 | async-start | bytes 1048576 | tf_op jit(solution)/shard_map/all_to_all | solution.py:226
  85.6 21.6 %copy-start.2 = (f32[2,1,384,384]{2,3,0,1:T(8,128)S(1)}, f32[2,1,384,384]{2,3,0,1:T(8,128)}, u32[]{:S(2)}) copy-start(f32[2,1,384,384]{2,3,0,1:T(8,128)} %copy.63) | copy-start | bytes 3538948
  87.1 20.0 %collective-permute-start.1 = (bf16[2,1,384,384]{2,3,0,1:T(8,128)(2,1)S(1)}, bf16[2,1,384,384]{2,3,0,1:T(8,128)(2,1)}, u32[]{:S(2)}, u32[]{:S(2)}) collective-permute-start(bf16[2,1,384,384]{2,3,0,1:T(8,128)(2,1)S(1)} %add_convert_fusion.1), channel_id=1, source_target_pairs={{0,2},{1,3},{2,0},{3,1},{4,6},{5,7},{6,4},{7,5},{8,10},{9,11},{10,... | collective-permute-start | bytes 1769480 | tf_op jit(solution)/shard_map/ppermute | solution.py:245
  102.6 18.9 %all-to-all-start.3 = ((f32[32,1,4096]{2,1,0:T(1,128)}), f32[32,1,4096]{2,1,0:T(1,128)}, u32[]{:S(2)}, u32[]{:S(2)}) async-start(f32[32,1,4096]{2,1,0:T(1,128)} %broadcast_in_dim.10), calls=%async_computation.3 | async-start | bytes 1048576 | tf_op jit(solution)/shard_map/all_to_all | solution.py:233
  112.2 11.0 %copy-start.3 = (f32[4,2,128,128]{3,2,1,0:T(8,128)S(1)}, f32[4,2,128,128]{3,2,1,0:T(8,128)}, u32[]{:S(2)}) copy-start(f32[4,2,128,128]{3,2,1,0:T(8,128)} %probe_ref.1) | copy-start | bytes 1572868
  131.5 24.2 %all-to-all-start.4 = ((f32[32,1,4096]{2,1,0:T(1,128)}), f32[32,1,4096]{2,1,0:T(1,128)}, u32[]{:S(2)}, u32[]{:S(2)}) async-start(f32[32,1,4096]{2,1,0:T(1,128)} %bitcast.158), calls=%async_computation.4 | async-start | bytes 1048576 | tf_op jit(solution)/shard_map/all_to_all | solution.py:226
  146.3 15.4 %copy-start.1 = (f32[4,2,128,128]{3,2,1,0:T(8,128)S(1)}, f32[4,2,128,128]{3,2,1,0:T(8,128)}, u32[]{:S(2)}) copy-start(f32[4,2,128,128]{3,2,1,0:T(8,128)} %add.261.probe_ref) | copy-start | bytes 1572868
  146.3 2.2 %collective-permute-start.2 = (bf16[2,1,384,384]{2,3,0,1:T(8,128)(2,1)}, bf16[2,1,384,384]{2,3,0,1:T(8,128)(2,1)S(1)}, u32[]{:S(2)}, u32[]{:S(2)}) collective-permute-start(bf16[2,1,384,384]{2,3,0,1:T(8,128)(2,1)} %fusion.111), channel_id=1, source_target_pairs={{0,1},{1,0},{2,3},{3,2},{4,5},{5,4},{6,7},{7,6},{8,9},{9,8},{10,11... | collective-permute-start | bytes 1769480 | tf_op jit(solution)/shard_map/ppermute | solution.py:245
  150.6 19.6 %collective-permute-start.3 = (bf16[2,1,384,384]{2,3,0,1:T(8,128)(2,1)}, bf16[2,1,384,384]{2,3,0,1:T(8,128)(2,1)}, u32[]{:S(2)}, u32[]{:S(2)}) collective-permute-start(bf16[2,1,384,384]{2,3,0,1:T(8,128)(2,1)} %add_convert_fusion), channel_id=1, source_target_pairs={{0,2},{1,3},{2,0},{3,1},{4,6},{5,7},{6,4},{7,5},{8,10},{9,11},{10,... | collective-permute-start | bytes 1769480 | tf_op jit(solution)/shard_map/ppermute | solution.py:245
  158.4 18.9 %all-to-all-start.5 = ((f32[32,1,4096]{2,1,0:T(1,128)}), f32[32,1,4096]{2,1,0:T(1,128)}, u32[]{:S(2)}, u32[]{:S(2)}) async-start(f32[32,1,4096]{2,1,0:T(1,128)} %broadcast_in_dim.11), calls=%async_computation.5 | async-start | bytes 1048576 | tf_op jit(solution)/shard_map/all_to_all | solution.py:233

commit v12 on v11

--- a/solution.py
+++ b/solution.py
@@ -230,8 +230,9 @@
 
 def all_sum_a2a(value, axes):
     total, count = sum_over(value, axes, value.dtype)
+    total = total.astype(jnp.bfloat16)
     spread = lax.all_to_all(jnp.broadcast_to(total, (count, total.shape[1])), axes, 0, 0, tiled=True)
-    return spread.reshape(value.shape)
+    return spread.reshape(value.shape).astype(jnp.float32)
 
 
 def all_sum_pairs(value, axis, send_type):

time: 181 us -> 190 us (1.050)
  local copies, waits for them, and re-layouts: 12.6 us -> 21 us
  other arithmetic: 27.8 us -> 32.3 us
  waiting for transfers between devices: 57.1 us -> 54.1 us
    ppermute x4, waiting for transfers between devices: 9.81 us -> 0.01 us  [all_sum_pairs(): other = lax.ppermute(total.astype(send_type), axis, pairs)]
    unnamed x21 -> x23, local copies, waits for them, and re-layouts: 5.31 us -> 14 us
    all_to_all x2, waiting for transfers between devices: 15.4 us -> 23.1 us  [sum_over(): lax.all_to_all(value.astype(send_type).reshape(count, -1), axes, 0, 0, ti...]
    broadcast_in_dim x0 -> x2, other arithmetic: none -> 6.72 us  [all_sum_a2a(): jnp.broadcast_to(total, (count, total.shape[1]))]
  transfers between devices with their start and end apart: 10 -> 10, of which waited for: 7 -> 5; matrix products, arithmetic and copies ran while one was open for 28% -> 28% of each run, Pallas kernels for 0% -> 0%
where the time goes in v12:
time: 190 us; the launch traced here: 189 us
  waiting for transfers between devices  54.1 us (28%)
  starting transfers between devices  39.2 us (21%)
  other arithmetic  32.3 us (17%)
  matrix products  25.9 us (14%)
  local copies, waits for them, and re-layouts  21 us (11%)
  Pallas kernels  15.2 us (8%)
    all_to_all x1, waiting for transfers between devices, on_device(): lax.all_to_all(jnp.swapaxes(payload, 0, 1), 'tile', 0, 0, tiled=True)  25.6 us
    all_to_all x2, waiting for transfers between devices, sum_over(): lax.all_to_all(value.astype(send_type).reshape(count, -1), axes, 0, 0, ti...  23.1 us
    all_to_all x2, starting transfers between devices, sum_over(): lax.all_to_all(value.astype(send_type).reshape(count, -1), axes, 0, 0, ti...  15.8 us
    pallas_call x2, Pallas kernels, entries_kernel(): pl.pallas_call(entry_kernel, grid_spec=grid_spec, out_shape=[jax.ShapeDty...  15.2 us
    unnamed x23, local copies, waits for them, and re-layouts  14 us
    dot_general x2, matrix products, entries_pass(): jnp.einsum('skq,xskc->xqc', pick_rows, spread, preferred_element_type=jnp...  10.6 us
    dot_general x2, matrix products, entries_pass(): jnp.einsum('skq,xqc->xskc', pick_rows, stacked, preferred_element_type=jn...  9.38 us
    all_to_all x1, starting transfers between devices, on_device(): placed = lax.all_to_all(jnp.swapaxes(meta, 0, 1), 'tile', 0, 0, tiled=True)  7.28 us
  transfers between devices with their start and end apart: 10, of which 5 were waited for; matrix products, arithmetic and copies ran while one was open for 28% of the time, Pallas kernels for 0%

profile of v12, /device:TPU:0, one launch (start us, length us, event | category | flops | bytes accessed | tf_op | source)
XLA Modules:
  0.0 188.7 jit_solution(9079715496202324789)
XLA Ops:
  5.3 7.3 %all-to-all-start = ((s32[8,2,3,4]{3,1,2,0:T(2,128)}), s32[8,2,3,4]{3,1,2,0:T(2,128)S(1)}, u32[]{:S(2)}, u32[]{:S(2)}) async-start(s32[8,2,3,4]{3,1,2,0:T(2,128)} %copy.56), calls=%async_computation | async-start | bytes 49152 | tf_op jit(solution)/shard_map/all_to_all | solution.py:329
  20.1 6.0 %all-to-all-start.1 = ((bf16[8,2,3,128,128]{4,3,2,1,0:T(8,128)(2,1)}), bf16[8,2,3,128,128]{4,3,2,1,0:T(8,128)(2,1)S(1)}, u32[]{:S(2)}, u32[]{:S(2)}) async-start(bf16[8,2,3,128,128]{4,3,2,1,0:T(8,128)(2,1)} %copy.62), calls=%async_computation.1 | async-start | bytes 3145728 | tf_op jit(solution)/shard_map/all_to_all | solution.py:330
  29.9 4.4 %convert_bitcast_fusion.1 = bf16[2,24,128,384]{3,2,0,1:T(8,128)(2,1)S(1)} fusion(s32[24,128]{1,0:T(8,128)S(1)} %get-tuple-element.38, pred[24]{0:T(512)(128)(4,1)S(1)} %reduce.4, f32[2,1,384,384]{3,2,1,0:T(8,128)} %param.10), kind=kOutput, calls=%fused_computation.14 | convolution fusion | flops 1816952832 | bytes 5910552 | tf_op jit(solution)/shard_map/skq,xqc->xskc/dot_general | solution.py:267
  34.3 2.6 %fusion.71.patch_ref = bf16[2,24,128,128]{3,2,1,0:T(8,128)(2,1)} fusion(bf16[2,24,128,384]{3,2,0,1:T(8,128)(2,1)S(1)} %convert_bitcast_fusion.1, s32[24,128]{1,0:T(8,128)S(1)} %get-tuple-element.39), kind=kOutput, calls=%fused_computation.44 | convolution fusion | flops 605945856 | bytes 6303744 | tf_op jit(solution)/shard_map/xskc,scl->xskl/dot_general | solution.py:270
  36.9 25.6 %all-to-all-done.1 = bf16[8,2,3,128,128]{4,3,2,1,0:T(8,128)(2,1)S(1)} async-done(((bf16[8,2,3,128,128]{4,3,2,1,0:T(8,128)(2,1)}), bf16[8,2,3,128,128]{4,3,2,1,0:T(8,128)(2,1)S(1)}, u32[]{:S(2)}, u32[]{:S(2)}) %all-to-all-start.1) | async-done | bytes 1572896 | tf_op jit(solution)/shard_map/all_to_all | solution.py:330
  63.8 7.5 %shard_map.77 = (bf16[2,24,128,128]{3,2,1,0:T(8,128)(2,1)}, f32[4,2,128,128]{3,2,1,0:T(8,128)}) custom-call(s32[25]{0:T(128)} %pad_add_fusion.order_ref, bf16[2,24,128,128]{3,2,1,0:T(8,128)(2,1)} %fusion.71.patch_ref, bf16[24,128,128]{2,1,0:T(8,128)(2,1)} %bitcast.157, f32[4,2,128,128]{3,2,1,0:T(8,128)} %probe_ref.1, ...), custom_call_target="tpu_custom_call" | custom-call | flops 6442450944 | bytes 4980736 | tf_op jit(solution)/shard_map/pallas_call | solution.py:169
  71.2 5.3 %fusion.104 = bf16[2,1,384,384]{2,3,0,1:T(8,128)(2,1)S(1)} fusion(s32[24,128]{1,0:T(8,128)S(1)} %get-tuple-element.38, pred[24]{0:T(512)(128)(4,1)S(1)} %reduce.4, bf16[2,24,128,128]{3,2,1,0:T(8,128)(2,1)} %get-tuple-element.6, s32[24,128]{1,0:T(8,128)S(1)} %get-tuple-element.39), kind=kOutput, calls=%fused_computation.49 | convolution fusion | flops 2422112256 | bytes 2187288 | tf_op jit(solution)/shard_map/skq,xskc->xqc/dot_general | solution.py:288
  77.4 7.4 %all-to-all-start.2 = ((f32[32,1,4096]{2,1,0:T(1,128)}), f32[32,1,4096]{2,1,0:T(1,128)S(1)}, u32[]{:S(2)}, u32[]{:S(2)}) async-start(f32[32,1,4096]{2,1,0:T(1,128)} %bitcast.37), calls=%async_computation.2 | async-start | bytes 1048576 | tf_op jit(solution)/shard_map/all_to_all | solution.py:226
  88.8 11.3 %all-to-all-done.2 = f32[32,1,4096]{2,1,0:T(1,128)S(1)} async-done(((f32[32,1,4096]{2,1,0:T(1,128)}), f32[32,1,4096]{2,1,0:T(1,128)S(1)}, u32[]{:S(2)}, u32[]{:S(2)}) %all-to-all-start.2) | async-done | bytes 524320 | tf_op jit(solution)/shard_map/all_to_all | solution.py:226
  101.5 2.8 %reduce.10 = bf16[32,4096]{1,0:T(8,128)(2,1)} reduce(bf16[32,1,4096]{2,1,0:T(2,128)(2,1)S(1)} %broadcast_in_dim.10, bf16[]{:T(256)} %broadcast.303), dimensions={1}, to_apply=%broadcast_in_dim.10.reduce_sub_computation | reduce | bytes 524290 | tf_op jit(solution)/shard_map/broadcast_in_dim | solution.py:234
  106.2 3.3 %all-to-all-start.3 = ((bf16[32,2,2048]{2,1,0:T(2,128)(2,1)}), bf16[32,2,2048]{2,1,0:T(2,128)(2,1)}, u32[]{:S(2)}, u32[]{:S(2)}) async-start(bf16[32,2,2048]{2,1,0:T(2,128)(2,1)} %reshape.318), calls=%async_computation.3 | async-start | bytes 524288 | tf_op jit(solution)/shard_map/all_to_all | solution.py:234
  109.6 5.0 %convert_bitcast_fusion = bf16[2,24,128,384]{2,3,0,1:T(8,128)(2,1)S(1)} fusion(s32[24,128]{1,0:T(8,128)S(1)} %iota_add_fusion, pred[24]{0:T(512)(128)(4,1)S(1)} %reduce.6, f32[2,1,384,384]{2,3,0,1:T(8,128)S(1)} %copy-done.2, bf16[2,1,384,384]{2,3,0,1:T(8,128)(2,1)} %collective-permute-done.1, bf16[2,1,384,384]{2,3,0,1:T(8,128)(2,1)S(1)} %add_convert_fusion.1, ...), kind=kOutput, calls=%fused_computation.10 | convolution fusion | flops 1818427392 | bytes 7090204 | tf_op jit(solution)/shard_map/skq,xqc->xskc/dot_general | solution.py:267
  114.6 3.3 %fusion.66.patch_ref = bf16[2,24,128,128]{3,2,1,0:T(8,128)(2,1)} fusion(bf16[2,24,128,384]{2,3,0,1:T(8,128)(2,1)S(1)} %convert_bitcast_fusion, s32[24,128]{1,0:T(8,128)S(1)} %iota_add_fusion.1), kind=kOutput, calls=%fused_computation.43 | convolution fusion | flops 605945856 | bytes 6303744 | tf_op jit(solution)/shard_map/xskc,scl->xskl/dot_general | solution.py:270
  117.9 2.2 %all-to-all-done.3 = bf16[32,2,2048]{2,1,0:T(2,128)(2,1)} async-done(((bf16[32,2,2048]{2,1,0:T(2,128)(2,1)}), bf16[32,2,2048]{2,1,0:T(2,128)(2,1)}, u32[]{:S(2)}, u32[]{:S(2)}) %all-to-all-start.3) | async-done | bytes 262176 | tf_op jit(solution)/shard_map/all_to_all | solution.py:234
  120.1 2.8 %reshape.319 = bf16[32,1,4096]{2,1,0:T(2,128)(2,1)} reshape(bf16[32,2,2048]{2,1,0:T(2,128)(2,1)} %all-to-all-done.3) | data formatting | bytes 524288
  125.6 7.7 %shard_map.78 = (bf16[2,24,128,128]{3,2,1,0:T(8,128)(2,1)}, f32[4,2,128,128]{3,2,1,0:T(8,128)}) custom-call(s32[25]{0:T(128)} %pad_add_fusion.1.order_ref, bf16[2,24,128,128]{3,2,1,0:T(8,128)(2,1)} %fusion.66.patch_ref, bf16[24,128,128]{2,1,0:T(8,128)(2,1)} %bitcast.156, f32[4,2,128,128]{3,2,1,0:T(8,128)} %add.261.probe_ref, ...), custom_call_target="tpu_custom_call" | custom-call | flops 6442450944 | bytes 4980736 | tf_op jit(solution)/shard_map/pallas_call | solution.py:169
  133.3 5.3 %fusion.111 = bf16[2,1,384,384]{2,3,0,1:T(8,128)(2,1)S(1)} fusion(s32[24,128]{1,0:T(8,128)S(1)} %iota_add_fusion, pred[24]{0:T(512)(128)(4,1)S(1)} %reduce.6, bf16[2,24,128,128]{3,2,1,0:T(8,128)(2,1)} %get-tuple-element.8, s32[24,128]{1,0:T(8,128)S(1)} %iota_add_fusion.1), kind=kOutput, calls=%fused_computation.50 | convolution fusion | flops 2422112256 | bytes 2187288 | tf_op jit(solution)/shard_map/skq,xskc->xqc/dot_general | solution.py:288
  138.7 8.4 %all-to-all-start.4 = ((f32[32,1,4096]{2,1,0:T(1,128)}), f32[32,1,4096]{2,1,0:T(1,128)}, u32[]{:S(2)}, u32[]{:S(2)}) async-start(f32[32,1,4096]{2,1,0:T(1,128)} %bitcast.158), calls=%async_computation.4 | async-start | bytes 1048576 | tf_op jit(solution)/shard_map/all_to_all | solution.py:226
  150.9 11.8 %all-to-all-done.4 = f32[32,1,4096]{2,1,0:T(1,128)} async-done(((f32[32,1,4096]{2,1,0:T(1,128)}), f32[32,1,4096]{2,1,0:T(1,128)}, u32[]{:S(2)}, u32[]{:S(2)}) %all-to-all-start.4) | async-done | bytes 524320 | tf_op jit(solution)/shard_map/all_to_all | solution.py:226
  165.4 3.9 %reduce.11 = bf16[32,4096]{1,0:T(8,128)(2,1)} reduce(bf16[32,1,4096]{2,1,0:T(2,128)(2,1)} %broadcast_in_dim.11, bf16[]{:T(256)} %broadcast.303), dimensions={1}, to_apply=%broadcast_in_dim.11.reduce_sub_computation | reduce | bytes 524290 | tf_op jit(solution)/shard_map/broadcast_in_dim | solution.py:234
  171.1 3.3 %all-to-all-start.5 = ((bf16[32,2,2048]{2,1,0:T(2,128)(2,1)}), bf16[32,2,2048]{2,1,0:T(2,128)(2,1)}, u32[]{:S(2)}, u32[]{:S(2)}) async-start(bf16[32,2,2048]{2,1,0:T(2,128)(2,1)} %reshape.320), calls=%async_computation.5 | async-start | bytes 524288 | tf_op jit(solution)/shard_map/all_to_all | solution.py:234
  175.1 4.1 %divide_add_fusion = f32[2,1,384,384]{2,3,0,1:T(8,128)} fusion(bf16[2,1,384,384]{2,3,0,1:T(8,128)(2,1)} %collective-permute-done.3, bf16[2,1,384,384]{2,3,0,1:T(8,128)(2,1)} %add_convert_fusion, f32[]{:T(128)} %reduce_max.19, f32[2,1,384,384]{2,3,0,1:T(8,128)S(1)} %copy-done.2, f32[]{:T(128)} %reduce_max.18, ...), kind=kLoop, calls=%fused_computation.51 | loop fusion | flops 2949120 | bytes 4718600 | tf_op jit(solution)/shard_map/add | solution.py:316
  179.1 2.7 %copy.71 = f32[2,1,384,384]{3,2,1,0:T(8,128)} copy(f32[2,1,384,384]{2,3,0,1:T(8,128)} %divide_add_fusion) | data formatting | bytes 2359296
  181.8 3.2 %all-to-all-done.5 = bf16[32,2,2048]{2,1,0:T(2,128)(2,1)} async-done(((bf16[32,2,2048]{2,1,0:T(2,128)(2,1)}), bf16[32,2,2048]{2,1,0:T(2,128)(2,1)}, u32[]{:S(2)}, u32[]{:S(2)}) %all-to-all-start.5) | async-done | bytes 262176 | tf_op jit(solution)/shard_map/all_to_all | solution.py:234
  (95 shorter events, 40.6 us)
Async XLA Ops:
  0.6 16.7 %copy-start = (bf16[32,128,128]{2,1,0:T(8,128)(2,1)S(1)}, bf16[32,128,128]{2,1,0:T(8,128)(2,1)}, u32[]{:S(2)}) copy-start(bf16[32,128,128]{2,1,0:T(8,128)(2,1)} %param.6) | copy-start | bytes 3145732
  0.6 15.3 %copy-start.4 = (f32[2,1,384,384]{3,2,1,0:T(8,128)S(1)}, f32[2,1,384,384]{3,2,1,0:T(8,128)}, u32[]{:S(2)}) copy-start(f32[2,1,384,384]{3,2,1,0:T(8,128)} %param.10) | copy-start | bytes 3538948
  5.3 14.8 %all-to-all-start = ((s32[8,2,3,4]{3,1,2,0:T(2,128)}), s32[8,2,3,4]{3,1,2,0:T(2,128)S(1)}, u32[]{:S(2)}, u32[]{:S(2)}) async-start(s32[8,2,3,4]{3,1,2,0:T(2,128)} %copy.56), calls=%async_computation | async-start | bytes 49152 | tf_op jit(solution)/shard_map/all_to_all | solution.py:329
  20.1 42.4 %all-to-all-start.1 = ((bf16[8,2,3,128,128]{4,3,2,1,0:T(8,128)(2,1)}), bf16[8,2,3,128,128]{4,3,2,1,0:T(8,128)(2,1)S(1)}, u32[]{:S(2)}, u32[]{:S(2)}) async-start(bf16[8,2,3,128,128]{4,3,2,1,0:T(8,128)(2,1)} %copy.62), calls=%async_computation.1 | async-start | bytes 3145728 | tf_op jit(solution)/shard_map/all_to_all | solution.py:330
  76.5 9.0 %collective-permute-start = (bf16[2,1,384,384]{2,3,0,1:T(8,128)(2,1)S(1)}, bf16[2,1,384,384]{2,3,0,1:T(8,128)(2,1)S(1)}, u32[]{:S(2)}, u32[]{:S(2)}) collective-permute-start(bf16[2,1,384,384]{2,3,0,1:T(8,128)(2,1)S(1)} %fusion.104), channel_id=1, source_target_pairs={{0,1},{1,0},{2,3},{3,2},{4,5},{5,4},{6,7},{7,6},{8,9},{9,8},{10,11... | collective-permute-start | bytes 1769480 | tf_op jit(solution)/shard_map/ppermute | solution.py:246
  77.4 22.8 %all-to-all-start.2 = ((f32[32,1,4096]{2,1,0:T(1,128)}), f32[32,1,4096]{2,1,0:T(1,128)S(1)}, u32[]{:S(2)}, u32[]{:S(2)}) async-start(f32[32,1,4096]{2,1,0:T(1,128)} %bitcast.37), calls=%async_computation.2 | async-start | bytes 1048576 | tf_op jit(solution)/shard_map/all_to_all | solution.py:226
  85.7 23.9 %copy-start.2 = (f32[2,1,384,384]{2,3,0,1:T(8,128)S(1)}, f32[2,1,384,384]{2,3,0,1:T(8,128)}, u32[]{:S(2)}) copy-start(f32[2,1,384,384]{2,3,0,1:T(8,128)} %copy.63) | copy-start | bytes 3538948
  85.7 23.9 %collective-permute-start.1 = (bf16[2,1,384,384]{2,3,0,1:T(8,128)(2,1)S(1)}, bf16[2,1,384,384]{2,3,0,1:T(8,128)(2,1)}, u32[]{:S(2)}, u32[]{:S(2)}) collective-permute-start(bf16[2,1,384,384]{2,3,0,1:T(8,128)(2,1)S(1)} %add_convert_fusion.1), channel_id=1, source_target_pairs={{0,2},{1,3},{2,0},{3,1},{4,6},{5,7},{6,4},{7,5},{8,10},{9,11},{10,... | collective-permute-start | bytes 1769480 | tf_op jit(solution)/shard_map/ppermute | solution.py:246
  106.2 13.9 %all-to-all-start.3 = ((bf16[32,2,2048]{2,1,0:T(2,128)(2,1)}), bf16[32,2,2048]{2,1,0:T(2,128)(2,1)}, u32[]{:S(2)}, u32[]{:S(2)}) async-start(bf16[32,2,2048]{2,1,0:T(2,128)(2,1)} %reshape.318), calls=%async_computation.3 | async-start | bytes 524288 | tf_op jit(solution)/shard_map/all_to_all | solution.py:234
  117.9 6.8 %copy-start.3 = (f32[4,2,128,128]{3,2,1,0:T(8,128)S(1)}, f32[4,2,128,128]{3,2,1,0:T(8,128)}, u32[]{:S(2)}) copy-start(f32[4,2,128,128]{3,2,1,0:T(8,128)} %probe_ref.1) | copy-start | bytes 1572868
  138.6 8.5 %collective-permute-start.2 = (bf16[2,1,384,384]{2,3,0,1:T(8,128)(2,1)S(1)}, bf16[2,1,384,384]{2,3,0,1:T(8,128)(2,1)}, u32[]{:S(2)}, u32[]{:S(2)}) collective-permute-start(bf16[2,1,384,384]{2,3,0,1:T(8,128)(2,1)S(1)} %fusion.111), channel_id=1, source_target_pairs={{0,1},{1,0},{2,3},{3,2},{4,5},{5,4},{6,7},{7,6},{8,9},{9,8},{10,11... | collective-permute-start | bytes 1769480 | tf_op jit(solution)/shard_map/ppermute | solution.py:246
  138.7 24.0 %all-to-all-start.4 = ((f32[32,1,4096]{2,1,0:T(1,128)}), f32[32,1,4096]{2,1,0:T(1,128)}, u32[]{:S(2)}, u32[]{:S(2)}) async-start(f32[32,1,4096]{2,1,0:T(1,128)} %bitcast.158), calls=%async_computation.4 | async-start | bytes 1048576 | tf_op jit(solution)/shard_map/all_to_all | solution.py:226
  149.2 25.2 %copy-start.1 = (f32[4,2,128,128]{3,2,1,0:T(8,128)S(1)}, f32[4,2,128,128]{3,2,1,0:T(8,128)}, u32[]{:S(2)}) copy-start(f32[4,2,128,128]{3,2,1,0:T(8,128)} %add.261.probe_ref) | copy-start | bytes 1572868
  149.2 25.9 %collective-permute-start.3 = (bf16[2,1,384,384]{2,3,0,1:T(8,128)(2,1)}, bf16[2,1,384,384]{2,3,0,1:T(8,128)(2,1)}, u32[]{:S(2)}, u32[]{:S(2)}) collective-permute-start(bf16[2,1,384,384]{2,3,0,1:T(8,128)(2,1)} %add_convert_fusion), channel_id=1, source_target_pairs={{0,2},{1,3},{2,0},{3,1},{4,6},{5,7},{6,4},{7,5},{8,10},{9,11},{10,... | collective-permute-start | bytes 1769480 | tf_op jit(solution)/shard_map/ppermute | solution.py:246
  171.1 13.9 %all-to-all-start.5 = ((bf16[32,2,2048]{2,1,0:T(2,128)(2,1)}), bf16[32,2,2048]{2,1,0:T(2,128)(2,1)}, u32[]{:S(2)}, u32[]{:S(2)}) async-start(bf16[32,2,2048]{2,1,0:T(2,128)(2,1)} %reshape.320), calls=%async_computation.5 | async-start | bytes 524288 | tf_op jit(solution)/shard_map/all_to_all | solution.py:234

commit v13 on v11

--- a/solution.py
+++ b/solution.py
@@ -239,12 +239,12 @@
     if count & (count - 1):
         return lax.psum(value.astype(send_type), axis).astype(jnp.float32)
     total = value.astype(send_type).astype(jnp.float32)
-    step = 1
-    while step < count:
+    step = count // 2
+    while step >= 1:
         pairs = [(i, i ^ step) for i in range(count)]
         other = lax.ppermute(total.astype(send_type), axis, pairs)
         total = total.astype(send_type).astype(jnp.float32) + other.astype(jnp.float32)
-        step *= 2
+        step //= 2
     return total
 
 

time: 181 us -> 195 us (1.077)
  waiting for transfers between devices: 57.1 us -> 68.6 us
  Pallas kernels: 15 us -> 21.9 us
  starting transfers between devices: 39.6 us -> 35.4 us
    ppermute x4, waiting for transfers between devices: 9.81 us -> 24.7 us  [all_sum_pairs(): other = lax.ppermute(total.astype(send_type), axis, pairs)]
    all_to_all x2, waiting for transfers between devices: 15.4 us -> 4.16 us  [sum_over(): lax.all_to_all(value.astype(send_type).reshape(count, -1), axes, 0, 0, ti...]
    all_to_all x2, waiting for transfers between devices: 6.32 us -> 14.1 us  [all_sum_a2a(): lax.all_to_all(jnp.broadcast_to(total, (count, total.shape[1])), axes, 0,...]
    pallas_call x2, Pallas kernels: 15 us -> 21.9 us  [entries_kernel(): pl.pallas_call(entry_kernel, grid_spec=grid_spec, out_shape=[jax.ShapeDty...]
    all_to_all x2, starting transfers between devices: 16.1 us -> 9.75 us  [sum_over(): lax.all_to_all(value.astype(send_type).reshape(count, -1), axes, 0, 0, ti...]
    all_to_all x2, starting transfers between devices: 6.66 us -> 9.09 us  [all_sum_a2a(): lax.all_to_all(jnp.broadcast_to(total, (count, total.shape[1])), axes, 0,...]
  transfers between devices with their start and end apart: 10 -> 10, of which waited for: 7 -> 6; matrix products, arithmetic and copies ran while one was open for 28% -> 26% of each run, Pallas kernels for 0% -> 0%
where the time goes in v13:
time: 195 us; the launch traced here: 194 us
  waiting for transfers between devices  68.6 us (35%)
  starting transfers between devices  35.4 us (18%)
  other arithmetic  27.7 us (14%)
  matrix products  26.8 us (14%)
  Pallas kernels  21.9 us (11%)
  local copies, waits for them, and re-layouts  12.6 us (6%)
    all_to_all x1, waiting for transfers between devices, on_device(): lax.all_to_all(jnp.swapaxes(payload, 0, 1), 'tile', 0, 0, tiled=True)  25.6 us
    ppermute x4, waiting for transfers between devices, all_sum_pairs(): other = lax.ppermute(total.astype(send_type), axis, pairs)  24.7 us
    pallas_call x2, Pallas kernels, entries_kernel(): pl.pallas_call(entry_kernel, grid_spec=grid_spec, out_shape=[jax.ShapeDty...  21.9 us
    all_to_all x2, waiting for transfers between devices, all_sum_a2a(): lax.all_to_all(jnp.broadcast_to(total, (count, total.shape[1])), axes, 0,...  14.1 us
    dot_general x2, matrix products, entries_pass(): jnp.einsum('skq,xskc->xqc', pick_rows, spread, preferred_element_type=jnp...  11.4 us
    all_to_all x2, starting transfers between devices, sum_over(): lax.all_to_all(value.astype(send_type).reshape(count, -1), axes, 0, 0, ti...  9.75 us
    dot_general x2, matrix products, entries_pass(): jnp.einsum('skq,xqc->xskc', pick_rows, stacked, preferred_element_type=jn...  9.39 us
    all_to_all x2, starting transfers between devices, all_sum_a2a(): lax.all_to_all(jnp.broadcast_to(total, (count, total.shape[1])), axes, 0,...  9.09 us
  transfers between devices with their start and end apart: 10, of which 6 were waited for; matrix products, arithmetic and copies ran while one was open for 26% of the time, Pallas kernels for 0%

profile of v13, /device:TPU:0, one launch (start us, length us, event | category | flops | bytes accessed | tf_op | source)
XLA Modules:
  0.0 193.9 jit_solution(16192699536289935383)
XLA Ops:
  5.3 7.3 %all-to-all-start = ((s32[8,2,3,4]{3,1,2,0:T(2,128)}), s32[8,2,3,4]{3,1,2,0:T(2,128)S(1)}, u32[]{:S(2)}, u32[]{:S(2)}) async-start(s32[8,2,3,4]{3,1,2,0:T(2,128)} %copy.56), calls=%async_computation | async-start | bytes 49152 | tf_op jit(solution)/shard_map/all_to_all | solution.py:328
  20.1 6.0 %all-to-all-start.1 = ((bf16[8,2,3,128,128]{4,3,2,1,0:T(8,128)(2,1)}), bf16[8,2,3,128,128]{4,3,2,1,0:T(8,128)(2,1)S(1)}, u32[]{:S(2)}, u32[]{:S(2)}) async-start(bf16[8,2,3,128,128]{4,3,2,1,0:T(8,128)(2,1)} %copy.62), calls=%async_computation.1 | async-start | bytes 3145728 | tf_op jit(solution)/shard_map/all_to_all | solution.py:329
  29.9 4.4 %convert_bitcast_fusion.1 = bf16[2,24,128,384]{3,2,0,1:T(8,128)(2,1)S(1)} fusion(s32[24,128]{1,0:T(8,128)S(1)} %get-tuple-element.38, pred[24]{0:T(512)(128)(4,1)S(1)} %reduce.4, f32[2,1,384,384]{3,2,1,0:T(8,128)} %param.10), kind=kOutput, calls=%fused_computation.14 | convolution fusion | flops 1816952832 | bytes 5910552 | tf_op jit(solution)/shard_map/skq,xqc->xskc/dot_general | solution.py:266
  34.3 2.6 %fusion.71.patch_ref = bf16[2,24,128,128]{3,2,1,0:T(8,128)(2,1)} fusion(bf16[2,24,128,384]{3,2,0,1:T(8,128)(2,1)S(1)} %convert_bitcast_fusion.1, s32[24,128]{1,0:T(8,128)S(1)} %get-tuple-element.39), kind=kOutput, calls=%fused_computation.44 | convolution fusion | flops 605945856 | bytes 6303744 | tf_op jit(solution)/shard_map/xskc,scl->xskl/dot_general | solution.py:269
  36.9 25.6 %all-to-all-done.1 = bf16[8,2,3,128,128]{4,3,2,1,0:T(8,128)(2,1)S(1)} async-done(((bf16[8,2,3,128,128]{4,3,2,1,0:T(8,128)(2,1)}), bf16[8,2,3,128,128]{4,3,2,1,0:T(8,128)(2,1)S(1)}, u32[]{:S(2)}, u32[]{:S(2)}) %all-to-all-start.1) | async-done | bytes 1572896 | tf_op jit(solution)/shard_map/all_to_all | solution.py:329
  63.8 10.9 %shard_map.77 = (bf16[2,24,128,128]{3,2,1,0:T(8,128)(2,1)}, f32[4,2,128,128]{3,2,1,0:T(8,128)}) custom-call(s32[25]{0:T(128)} %pad_add_fusion.order_ref, bf16[2,24,128,128]{3,2,1,0:T(8,128)(2,1)} %fusion.71.patch_ref, bf16[24,128,128]{2,1,0:T(8,128)(2,1)} %bitcast.157, f32[4,2,128,128]{3,2,1,0:T(8,128)} %probe_ref.1, ...), custom_call_target="tpu_custom_call" | custom-call | flops 6442450944 | bytes 4980736 | tf_op jit(solution)/shard_map/pallas_call | solution.py:169
  74.7 5.3 %fusion.104 = bf16[2,1,384,384]{2,3,0,1:T(8,128)(2,1)S(1)} fusion(s32[24,128]{1,0:T(8,128)S(1)} %get-tuple-element.38, pred[24]{0:T(512)(128)(4,1)S(1)} %reduce.4, bf16[2,24,128,128]{3,2,1,0:T(8,128)(2,1)} %get-tuple-element.6, s32[24,128]{1,0:T(8,128)S(1)} %get-tuple-element.39), kind=kOutput, calls=%fused_computation.49 | convolution fusion | flops 2422112256 | bytes 2187288 | tf_op jit(solution)/shard_map/skq,xskc->xqc/dot_general | solution.py:287
  83.1 4.5 %all-to-all-start.2 = ((f32[32,1,4096]{2,1,0:T(1,128)}), f32[32,1,4096]{2,1,0:T(1,128)S(1)}, u32[]{:S(2)}, u32[]{:S(2)}) async-start(f32[32,1,4096]{2,1,0:T(1,128)} %bitcast.37), calls=%async_computation.2 | async-start | bytes 1048576 | tf_op jit(solution)/shard_map/all_to_all | solution.py:226
  87.6 9.4 %collective-permute-done = bf16[2,1,384,384]{2,3,0,1:T(8,128)(2,1)} collective-permute-done((bf16[2,1,384,384]{2,3,0,1:T(8,128)(2,1)S(1)}, bf16[2,1,384,384]{2,3,0,1:T(8,128)(2,1)}, u32[]{:S(2)}, u32[]{:S(2)}) %collective-permute-start) | collective-permute-done | bytes 589856 | tf_op jit(solution)/shard_map/ppermute | solution.py:245
  98.8 4.2 %all-to-all-done.2 = f32[32,1,4096]{2,1,0:T(1,128)S(1)} async-done(((f32[32,1,4096]{2,1,0:T(1,128)}), f32[32,1,4096]{2,1,0:T(1,128)S(1)}, u32[]{:S(2)}, u32[]{:S(2)}) %all-to-all-start.2) | async-done | bytes 524320 | tf_op jit(solution)/shard_map/all_to_all | solution.py:226
  104.6 3.7 %all-to-all-start.3 = ((f32[32,1,4096]{2,1,0:T(1,128)}), f32[32,1,4096]{2,1,0:T(1,128)}, u32[]{:S(2)}, u32[]{:S(2)}) async-start(f32[32,1,4096]{2,1,0:T(1,128)} %broadcast_in_dim.10), calls=%async_computation.3 | async-start | bytes 1048576 | tf_op jit(solution)/shard_map/all_to_all | solution.py:233
  109.5 5.0 %convert_bitcast_fusion = bf16[2,24,128,384]{2,3,0,1:T(8,128)(2,1)S(1)} fusion(s32[24,128]{1,0:T(8,128)S(1)} %iota_add_fusion, pred[24]{0:T(512)(128)(4,1)S(1)} %reduce.6, f32[2,1,384,384]{2,3,0,1:T(8,128)S(1)} %copy-done.2, bf16[2,1,384,384]{2,3,0,1:T(8,128)(2,1)} %collective-permute-done.1, bf16[2,1,384,384]{2,3,0,1:T(8,128)(2,1)S(1)} %add_convert_fusion.1, ...), kind=kOutput, calls=%fused_computation.10 | convolution fusion | flops 1818427392 | bytes 7090204 | tf_op jit(solution)/shard_map/skq,xqc->xskc/dot_general | solution.py:266
  114.6 3.3 %fusion.66.patch_ref = bf16[2,24,128,128]{3,2,1,0:T(8,128)(2,1)} fusion(bf16[2,24,128,384]{2,3,0,1:T(8,128)(2,1)S(1)} %convert_bitcast_fusion, s32[24,128]{1,0:T(8,128)S(1)} %iota_add_fusion.1), kind=kOutput, calls=%fused_computation.43 | convolution fusion | flops 605945856 | bytes 6303744 | tf_op jit(solution)/shard_map/xskc,scl->xskl/dot_general | solution.py:269
  117.9 6.0 %all-to-all-done.3 = f32[32,1,4096]{2,1,0:T(1,128)} async-done(((f32[32,1,4096]{2,1,0:T(1,128)}), f32[32,1,4096]{2,1,0:T(1,128)}, u32[]{:S(2)}, u32[]{:S(2)}) %all-to-all-start.3) | async-done | bytes 524320 | tf_op jit(solution)/shard_map/all_to_all | solution.py:233
  126.4 11.0 %shard_map.78 = (bf16[2,24,128,128]{3,2,1,0:T(8,128)(2,1)}, f32[4,2,128,128]{3,2,1,0:T(8,128)}) custom-call(s32[25]{0:T(128)} %pad_add_fusion.1.order_ref, bf16[2,24,128,128]{3,2,1,0:T(8,128)(2,1)} %fusion.66.patch_ref, bf16[24,128,128]{2,1,0:T(8,128)(2,1)} %bitcast.156, f32[4,2,128,128]{3,2,1,0:T(8,128)} %add.261.probe_ref, ...), custom_call_target="tpu_custom_call" | custom-call | flops 6442450944 | bytes 4980736 | tf_op jit(solution)/shard_map/pallas_call | solution.py:169
  137.3 5.2 %all-to-all-start.4 = ((f32[32,1,4096]{2,1,0:T(1,128)}), f32[32,1,4096]{2,1,0:T(1,128)}, u32[]{:S(2)}, u32[]{:S(2)}) async-start(f32[32,1,4096]{2,1,0:T(1,128)} %bitcast.158), calls=%async_computation.4 | async-start | bytes 1048576 | tf_op jit(solution)/shard_map/all_to_all | solution.py:226
  142.6 6.1 %fusion.111 = bf16[2,1,384,384]{2,3,0,1:T(8,128)(2,1)} fusion(s32[24,128]{1,0:T(8,128)S(1)} %iota_add_fusion, pred[24]{0:T(512)(128)(4,1)S(1)} %reduce.6, bf16[2,24,128,128]{3,2,1,0:T(8,128)(2,1)} %get-tuple-element.8, s32[24,128]{1,0:T(8,128)S(1)} %iota_add_fusion.1), kind=kOutput, calls=%fused_computation.50 | convolution fusion | flops 2422112256 | bytes 2187288 | tf_op jit(solution)/shard_map/skq,xskc->xqc/dot_general | solution.py:287
  148.7 1.7 collective-permute-start.2
  150.4 15.3 %collective-permute-done.2 = bf16[2,1,384,384]{2,3,0,1:T(8,128)(2,1)S(1)} collective-permute-done((bf16[2,1,384,384]{2,3,0,1:T(8,128)(2,1)}, bf16[2,1,384,384]{2,3,0,1:T(8,128)(2,1)S(1)}, u32[]{:S(2)}, u32[]{:S(2)}) %collective-permute-start.2) | collective-permute-done | bytes 589856 | tf_op jit(solution)/shard_map/ppermute | solution.py:245
  165.7 2.0 %add_convert_fusion = bf16[2,1,384,384]{2,3,0,1:T(8,128)(2,1)} fusion(bf16[2,1,384,384]{2,3,0,1:T(8,128)(2,1)S(1)} %collective-permute-done.2, bf16[2,1,384,384]{2,3,0,1:T(8,128)(2,1)} %fusion.111), kind=kLoop, calls=%fused_computation.52 | loop fusion | flops 1179648 | bytes 1769472 | tf_op jit(solution)/shard_map/convert_element_type | solution.py:246
  170.4 5.4 %all-to-all-start.5 = ((f32[32,1,4096]{2,1,0:T(1,128)}), f32[32,1,4096]{2,1,0:T(1,128)}, u32[]{:S(2)}, u32[]{:S(2)}) async-start(f32[32,1,4096]{2,1,0:T(1,128)} %broadcast_in_dim.11), calls=%async_computation.5 | async-start | bytes 1048576 | tf_op jit(solution)/shard_map/all_to_all | solution.py:233
  176.5 4.1 %divide_add_fusion = f32[2,1,384,384]{2,3,0,1:T(8,128)} fusion(bf16[2,1,384,384]{2,3,0,1:T(8,128)(2,1)} %collective-permute-done.3, bf16[2,1,384,384]{2,3,0,1:T(8,128)(2,1)} %add_convert_fusion, f32[]{:T(128)} %reduce_max.19, f32[2,1,384,384]{2,3,0,1:T(8,128)S(1)} %copy-done.2, f32[]{:T(128)} %reduce_max.18, ...), kind=kLoop, calls=%fused_computation.51 | loop fusion | flops 2949120 | bytes 4718600 | tf_op jit(solution)/shard_map/add | solution.py:315
  180.6 2.7 %copy.71 = f32[2,1,384,384]{3,2,1,0:T(8,128)} copy(f32[2,1,384,384]{2,3,0,1:T(8,128)} %divide_add_fusion) | data formatting | bytes 2359296
  183.2 8.1 %all-to-all-done.5 = f32[32,1,4096]{2,1,0:T(1,128)} async-done(((f32[32,1,4096]{2,1,0:T(1,128)}), f32[32,1,4096]{2,1,0:T(1,128)}, u32[]{:S(2)}, u32[]{:S(2)}) %all-to-all-start.5) | async-done | bytes 524320 | tf_op jit(solution)/shard_map/all_to_all | solution.py:233
  (90 shorter events, 33.2 us)
Async XLA Ops:
  0.6 16.7 %copy-start = (bf16[32,128,128]{2,1,0:T(8,128)(2,1)S(1)}, bf16[32,128,128]{2,1,0:T(8,128)(2,1)}, u32[]{:S(2)}) copy-start(bf16[32,128,128]{2,1,0:T(8,128)(2,1)} %param.6) | copy-start | bytes 3145732
  0.6 15.3 %copy-start.4 = (f32[2,1,384,384]{3,2,1,0:T(8,128)S(1)}, f32[2,1,384,384]{3,2,1,0:T(8,128)}, u32[]{:S(2)}) copy-start(f32[2,1,384,384]{3,2,1,0:T(8,128)} %param.10) | copy-start | bytes 3538948
  5.3 14.8 %all-to-all-start = ((s32[8,2,3,4]{3,1,2,0:T(2,128)}), s32[8,2,3,4]{3,1,2,0:T(2,128)S(1)}, u32[]{:S(2)}, u32[]{:S(2)}) async-start(s32[8,2,3,4]{3,1,2,0:T(2,128)} %copy.56), calls=%async_computation | async-start | bytes 49152 | tf_op jit(solution)/shard_map/all_to_all | solution.py:328
  20.1 42.4 %all-to-all-start.1 = ((bf16[8,2,3,128,128]{4,3,2,1,0:T(8,128)(2,1)}), bf16[8,2,3,128,128]{4,3,2,1,0:T(8,128)(2,1)S(1)}, u32[]{:S(2)}, u32[]{:S(2)}) async-start(bf16[8,2,3,128,128]{4,3,2,1,0:T(8,128)(2,1)} %copy.62), calls=%async_computation.1 | async-start | bytes 3145728 | tf_op jit(solution)/shard_map/all_to_all | solution.py:329
  80.0 7.6 %copy-start.5 = (bf16[2,1,384,384]{2,3,0,1:T(8,128)(2,1)}, bf16[2,1,384,384]{2,3,0,1:T(8,128)(2,1)S(1)}, u32[]{:S(2)}) copy-start(bf16[2,1,384,384]{2,3,0,1:T(8,128)(2,1)S(1)} %fusion.104) | copy-start | bytes 1769476
  80.0 17.0 %collective-permute-start = (bf16[2,1,384,384]{2,3,0,1:T(8,128)(2,1)S(1)}, bf16[2,1,384,384]{2,3,0,1:T(8,128)(2,1)}, u32[]{:S(2)}, u32[]{:S(2)}) collective-permute-start(bf16[2,1,384,384]{2,3,0,1:T(8,128)(2,1)S(1)} %fusion.104), channel_id=1, source_target_pairs={{0,2},{1,3},{2,0},{3,1},{4,6},{5,7},{6,4},{7,5},{8,10},{9,11},{10,... | collective-permute-start | bytes 1769480 | tf_op jit(solution)/shard_map/ppermute | solution.py:245
  83.1 19.9 %all-to-all-start.2 = ((f32[32,1,4096]{2,1,0:T(1,128)}), f32[32,1,4096]{2,1,0:T(1,128)S(1)}, u32[]{:S(2)}, u32[]{:S(2)}) async-start(f32[32,1,4096]{2,1,0:T(1,128)} %bitcast.37), calls=%async_computation.2 | async-start | bytes 1048576 | tf_op jit(solution)/shard_map/all_to_all | solution.py:226
  87.6 21.9 %copy-start.2 = (f32[2,1,384,384]{2,3,0,1:T(8,128)S(1)}, f32[2,1,384,384]{2,3,0,1:T(8,128)}, u32[]{:S(2)}) copy-start(f32[2,1,384,384]{2,3,0,1:T(8,128)} %copy.63) | copy-start | bytes 3538948
  98.4 11.1 %collective-permute-start.1 = (bf16[2,1,384,384]{2,3,0,1:T(8,128)(2,1)S(1)}, bf16[2,1,384,384]{2,3,0,1:T(8,128)(2,1)}, u32[]{:S(2)}, u32[]{:S(2)}) collective-permute-start(bf16[2,1,384,384]{2,3,0,1:T(8,128)(2,1)S(1)} %add_convert_fusion.1), channel_id=1, source_target_pairs={{0,1},{1,0},{2,3},{3,2},{4,5},{5,4},{6,7},{7,6},{8,9},{9,8},{10,11... | collective-permute-start | bytes 1769480 | tf_op jit(solution)/shard_map/ppermute | solution.py:245
  104.6 19.2 %all-to-all-start.3 = ((f32[32,1,4096]{2,1,0:T(1,128)}), f32[32,1,4096]{2,1,0:T(1,128)}, u32[]{:S(2)}, u32[]{:S(2)}) async-start(f32[32,1,4096]{2,1,0:T(1,128)} %broadcast_in_dim.10), calls=%async_computation.3 | async-start | bytes 1048576 | tf_op jit(solution)/shard_map/all_to_all | solution.py:233
  114.5 11.0 %copy-start.3 = (f32[4,2,128,128]{3,2,1,0:T(8,128)S(1)}, f32[4,2,128,128]{3,2,1,0:T(8,128)}, u32[]{:S(2)}) copy-start(f32[4,2,128,128]{3,2,1,0:T(8,128)} %probe_ref.1) | copy-start | bytes 1572868
  137.3 30.4 %all-to-all-start.4 = ((f32[32,1,4096]{2,1,0:T(1,128)}), f32[32,1,4096]{2,1,0:T(1,128)}, u32[]{:S(2)}, u32[]{:S(2)}) async-start(f32[32,1,4096]{2,1,0:T(1,128)} %bitcast.158), calls=%async_computation.4 | async-start | bytes 1048576 | tf_op jit(solution)/shard_map/all_to_all | solution.py:226
  148.7 27.1 %copy-start.1 = (f32[4,2,128,128]{3,2,1,0:T(8,128)S(1)}, f32[4,2,128,128]{3,2,1,0:T(8,128)}, u32[]{:S(2)}) copy-start(f32[4,2,128,128]{3,2,1,0:T(8,128)} %add.261.probe_ref) | copy-start | bytes 1572868
  148.7 17.0 %collective-permute-start.2 = (bf16[2,1,384,384]{2,3,0,1:T(8,128)(2,1)}, bf16[2,1,384,384]{2,3,0,1:T(8,128)(2,1)S(1)}, u32[]{:S(2)}, u32[]{:S(2)}) collective-permute-start(bf16[2,1,384,384]{2,3,0,1:T(8,128)(2,1)} %fusion.111), channel_id=1, source_target_pairs={{0,2},{1,3},{2,0},{3,1},{4,6},{5,7},{6,4},{7,5},{8,10},{9,11},{10,... | collective-permute-start | bytes 1769480 | tf_op jit(solution)/shard_map/ppermute | solution.py:245
  167.8 8.8 %collective-permute-start.3 = (bf16[2,1,384,384]{2,3,0,1:T(8,128)(2,1)}, bf16[2,1,384,384]{2,3,0,1:T(8,128)(2,1)}, u32[]{:S(2)}, u32[]{:S(2)}) collective-permute-start(bf16[2,1,384,384]{2,3,0,1:T(8,128)(2,1)} %add_convert_fusion), channel_id=1, source_target_pairs={{0,1},{1,0},{2,3},{3,2},{4,5},{5,4},{6,7},{7,6},{8,9},{9,8},{10,11... | collective-permute-start | bytes 1769480 | tf_op jit(solution)/shard_map/ppermute | solution.py:245
  170.4 20.9 %all-to-all-start.5 = ((f32[32,1,4096]{2,1,0:T(1,128)}), f32[32,1,4096]{2,1,0:T(1,128)}, u32[]{:S(2)}, u32[]{:S(2)}) async-start(f32[32,1,4096]{2,1,0:T(1,128)} %broadcast_in_dim.11), calls=%async_computation.5 | async-start | bytes 1048576 | tf_op jit(solution)/shard_map/all_to_all | solution.py:233

commit v14 on v11

--- a/solution.py
+++ b/solution.py
@@ -53,7 +53,12 @@
     count = order_ref[slots]
     group = next(size for size in (4, 2, 1) if slots % size == 0)
     grad_ref[...] = jnp.zeros(grad_ref.shape, grad_ref.dtype)
-    update_ref[...] = jnp.zeros(update_ref.shape, update_ref.dtype)
+
+    def clear(index, carry):
+        update_ref[:, order_ref[index]] = jnp.zeros((2,) + update_ref.shape[2:], update_ref.dtype)
+        return carry
+
+    lax.fori_loop(count, slots, clear, 0)
 
     def one_group(index, carry):
         chosen = [order_ref[index * group + g] for g in range(group)]

time: 181 us -> 182 us (level)
  no operation moved by 1% of the time
where the time goes in v14:
time: 182 us; the launch traced here: 179 us
  waiting for transfers between devices  57.1 us (31%)
  starting transfers between devices  38.8 us (21%)
  other arithmetic  27.8 us (15%)
  matrix products  26.8 us (15%)
  Pallas kernels  15 us (8%)
  local copies, waits for them, and re-layouts  12.6 us (7%)
    all_to_all x1, waiting for transfers between devices, on_device(): lax.all_to_all(jnp.swapaxes(payload, 0, 1), 'tile', 0, 0, tiled=True)  25.6 us
    all_to_all x2, waiting for transfers between devices, sum_over(): lax.all_to_all(value.astype(send_type).reshape(count, -1), axes, 0, 0, ti...  15.4 us
    all_to_all x2, starting transfers between devices, sum_over(): lax.all_to_all(value.astype(send_type).reshape(count, -1), axes, 0, 0, ti...  15.3 us
    pallas_call x2, Pallas kernels, entries_kernel(): pl.pallas_call(entry_kernel, grid_spec=grid_spec, out_shape=[jax.ShapeDty...  15 us
    dot_general x2, matrix products, entries_pass(): jnp.einsum('skq,xskc->xqc', pick_rows, spread, preferred_element_type=jnp...  11.4 us
    ppermute x4, waiting for transfers between devices, all_sum_pairs(): other = lax.ppermute(total.astype(send_type), axis, pairs)  9.81 us
    dot_general x2, matrix products, entries_pass(): jnp.einsum('skq,xqc->xskc', pick_rows, stacked, preferred_element_type=jn...  9.39 us
    all_to_all x1, starting transfers between devices, on_device(): placed = lax.all_to_all(jnp.swapaxes(meta, 0, 1), 'tile', 0, 0, tiled=True)  7.28 us
  transfers between devices with their start and end apart: 10, of which 7 were waited for; matrix products, arithmetic and copies ran while one was open for 28% of the time, Pallas kernels for 0%

profile of v14, /device:TPU:0, one launch (start us, length us, event | category | flops | bytes accessed | tf_op | source)
XLA Modules:
  0.0 179.0 jit_solution(3459796093155771302)
XLA Ops:
  5.3 7.3 %all-to-all-start = ((s32[8,2,3,4]{3,1,2,0:T(2,128)}), s32[8,2,3,4]{3,1,2,0:T(2,128)S(1)}, u32[]{:S(2)}, u32[]{:S(2)}) async-start(s32[8,2,3,4]{3,1,2,0:T(2,128)} %copy.56), calls=%async_computation | async-start | bytes 49152 | tf_op jit(solution)/shard_map/all_to_all | solution.py:333
  20.1 6.0 %all-to-all-start.1 = ((bf16[8,2,3,128,128]{4,3,2,1,0:T(8,128)(2,1)}), bf16[8,2,3,128,128]{4,3,2,1,0:T(8,128)(2,1)S(1)}, u32[]{:S(2)}, u32[]{:S(2)}) async-start(bf16[8,2,3,128,128]{4,3,2,1,0:T(8,128)(2,1)} %copy.62), calls=%async_computation.1 | async-start | bytes 3145728 | tf_op jit(solution)/shard_map/all_to_all | solution.py:334
  29.9 4.4 %convert_bitcast_fusion.1 = bf16[2,24,128,384]{3,2,0,1:T(8,128)(2,1)S(1)} fusion(s32[24,128]{1,0:T(8,128)S(1)} %get-tuple-element.38, pred[24]{0:T(512)(128)(4,1)S(1)} %reduce.4, f32[2,1,384,384]{3,2,1,0:T(8,128)} %param.10), kind=kOutput, calls=%fused_computation.14 | convolution fusion | flops 1816952832 | bytes 5910552 | tf_op jit(solution)/shard_map/skq,xqc->xskc/dot_general | solution.py:271
  34.3 2.6 %fusion.71.patch_ref = bf16[2,24,128,128]{3,2,1,0:T(8,128)(2,1)} fusion(bf16[2,24,128,384]{3,2,0,1:T(8,128)(2,1)S(1)} %convert_bitcast_fusion.1, s32[24,128]{1,0:T(8,128)S(1)} %get-tuple-element.39), kind=kOutput, calls=%fused_computation.44 | convolution fusion | flops 605945856 | bytes 6303744 | tf_op jit(solution)/shard_map/xskc,scl->xskl/dot_general | solution.py:274
  36.9 25.6 %all-to-all-done.1 = bf16[8,2,3,128,128]{4,3,2,1,0:T(8,128)(2,1)S(1)} async-done(((bf16[8,2,3,128,128]{4,3,2,1,0:T(8,128)(2,1)}), bf16[8,2,3,128,128]{4,3,2,1,0:T(8,128)(2,1)S(1)}, u32[]{:S(2)}, u32[]{:S(2)}) %all-to-all-start.1) | async-done | bytes 1572896 | tf_op jit(solution)/shard_map/all_to_all | solution.py:334
  63.8 7.5 %shard_map.77 = (bf16[2,24,128,128]{3,2,1,0:T(8,128)(2,1)}, f32[4,2,128,128]{3,2,1,0:T(8,128)}) custom-call(s32[25]{0:T(128)} %pad_add_fusion.order_ref, bf16[2,24,128,128]{3,2,1,0:T(8,128)(2,1)} %fusion.71.patch_ref, bf16[24,128,128]{2,1,0:T(8,128)(2,1)} %bitcast.157, f32[4,2,128,128]{3,2,1,0:T(8,128)} %probe_ref.1, ...), custom_call_target="tpu_custom_call" | custom-call | flops 6442450944 | bytes 4980736 | tf_op jit(solution)/shard_map/pallas_call | solution.py:174
  71.2 5.3 %fusion.104 = bf16[2,1,384,384]{2,3,0,1:T(8,128)(2,1)S(1)} fusion(s32[24,128]{1,0:T(8,128)S(1)} %get-tuple-element.38, pred[24]{0:T(512)(128)(4,1)S(1)} %reduce.4, bf16[2,24,128,128]{3,2,1,0:T(8,128)(2,1)} %get-tuple-element.6, s32[24,128]{1,0:T(8,128)S(1)} %get-tuple-element.39), kind=kOutput, calls=%fused_computation.49 | convolution fusion | flops 2422112256 | bytes 2187288 | tf_op jit(solution)/shard_map/skq,xskc->xqc/dot_general | solution.py:292
  78.2 6.8 %all-to-all-start.2 = ((f32[32,1,4096]{2,1,0:T(1,128)}), f32[32,1,4096]{2,1,0:T(1,128)S(1)}, u32[]{:S(2)}, u32[]{:S(2)}) async-start(f32[32,1,4096]{2,1,0:T(1,128)} %bitcast.37), calls=%async_computation.2 | async-start | bytes 1048576 | tf_op jit(solution)/shard_map/all_to_all | solution.py:231
  88.5 11.9 %all-to-all-done.2 = f32[32,1,4096]{2,1,0:T(1,128)S(1)} async-done(((f32[32,1,4096]{2,1,0:T(1,128)}), f32[32,1,4096]{2,1,0:T(1,128)S(1)}, u32[]{:S(2)}, u32[]{:S(2)}) %all-to-all-start.2) | async-done | bytes 524320 | tf_op jit(solution)/shard_map/all_to_all | solution.py:231
  102.0 3.3 %all-to-all-start.3 = ((f32[32,1,4096]{2,1,0:T(1,128)}), f32[32,1,4096]{2,1,0:T(1,128)}, u32[]{:S(2)}, u32[]{:S(2)}) async-start(f32[32,1,4096]{2,1,0:T(1,128)} %broadcast_in_dim.10), calls=%async_computation.3 | async-start | bytes 1048576 | tf_op jit(solution)/shard_map/all_to_all | solution.py:238
  106.5 5.0 %convert_bitcast_fusion = bf16[2,24,128,384]{2,3,0,1:T(8,128)(2,1)S(1)} fusion(s32[24,128]{1,0:T(8,128)S(1)} %iota_add_fusion, pred[24]{0:T(512)(128)(4,1)S(1)} %reduce.6, f32[2,1,384,384]{2,3,0,1:T(8,128)S(1)} %copy-done.2, bf16[2,1,384,384]{2,3,0,1:T(8,128)(2,1)} %collective-permute-done.1, bf16[2,1,384,384]{2,3,0,1:T(8,128)(2,1)S(1)} %add_convert_fusion.1, ...), kind=kOutput, calls=%fused_computation.10 | convolution fusion | flops 1818427392 | bytes 7090204 | tf_op jit(solution)/shard_map/skq,xqc->xskc/dot_general | solution.py:271
  111.6 3.3 %fusion.66.patch_ref = bf16[2,24,128,128]{3,2,1,0:T(8,128)(2,1)} fusion(bf16[2,24,128,384]{2,3,0,1:T(8,128)(2,1)S(1)} %convert_bitcast_fusion, s32[24,128]{1,0:T(8,128)S(1)} %iota_add_fusion.1), kind=kOutput, calls=%fused_computation.43 | convolution fusion | flops 605945856 | bytes 6303744 | tf_op jit(solution)/shard_map/xskc,scl->xskl/dot_general | solution.py:274
  114.9 6.0 %all-to-all-done.3 = f32[32,1,4096]{2,1,0:T(1,128)} async-done(((f32[32,1,4096]{2,1,0:T(1,128)}), f32[32,1,4096]{2,1,0:T(1,128)}, u32[]{:S(2)}, u32[]{:S(2)}) %all-to-all-start.3) | async-done | bytes 524320 | tf_op jit(solution)/shard_map/all_to_all | solution.py:238
  123.4 7.5 %shard_map.78 = (bf16[2,24,128,128]{3,2,1,0:T(8,128)(2,1)}, f32[4,2,128,128]{3,2,1,0:T(8,128)}) custom-call(s32[25]{0:T(128)} %pad_add_fusion.1.order_ref, bf16[2,24,128,128]{3,2,1,0:T(8,128)(2,1)} %fusion.66.patch_ref, bf16[24,128,128]{2,1,0:T(8,128)(2,1)} %bitcast.156, f32[4,2,128,128]{3,2,1,0:T(8,128)} %add.261.probe_ref, ...), custom_call_target="tpu_custom_call" | custom-call | flops 6442450944 | bytes 4980736 | tf_op jit(solution)/shard_map/pallas_call | solution.py:174
  130.9 8.5 %all-to-all-start.4 = ((f32[32,1,4096]{2,1,0:T(1,128)}), f32[32,1,4096]{2,1,0:T(1,128)}, u32[]{:S(2)}, u32[]{:S(2)}) async-start(f32[32,1,4096]{2,1,0:T(1,128)} %bitcast.158), calls=%async_computation.4 | async-start | bytes 1048576 | tf_op jit(solution)/shard_map/all_to_all | solution.py:231
  139.4 6.1 %fusion.111 = bf16[2,1,384,384]{2,3,0,1:T(8,128)(2,1)} fusion(s32[24,128]{1,0:T(8,128)S(1)} %iota_add_fusion, pred[24]{0:T(512)(128)(4,1)S(1)} %reduce.6, bf16[2,24,128,128]{3,2,1,0:T(8,128)(2,1)} %get-tuple-element.8, s32[24,128]{1,0:T(8,128)S(1)} %iota_add_fusion.1), kind=kOutput, calls=%fused_computation.50 | convolution fusion | flops 2422112256 | bytes 2187288 | tf_op jit(solution)/shard_map/skq,xskc->xqc/dot_general | solution.py:292
  145.7 2.0 %collective-permute-done.2 = bf16[2,1,384,384]{2,3,0,1:T(8,128)(2,1)S(1)} collective-permute-done((bf16[2,1,384,384]{2,3,0,1:T(8,128)(2,1)}, bf16[2,1,384,384]{2,3,0,1:T(8,128)(2,1)S(1)}, u32[]{:S(2)}, u32[]{:S(2)}) %collective-permute-start.2) | collective-permute-done | bytes 589856 | tf_op jit(solution)/shard_map/ppermute | solution.py:250
  147.8 2.0 %add_convert_fusion = bf16[2,1,384,384]{2,3,0,1:T(8,128)(2,1)} fusion(bf16[2,1,384,384]{2,3,0,1:T(8,128)(2,1)S(1)} %collective-permute-done.2, bf16[2,1,384,384]{2,3,0,1:T(8,128)(2,1)} %fusion.111), kind=kLoop, calls=%fused_computation.52 | loop fusion | flops 1179648 | bytes 1769472 | tf_op jit(solution)/shard_map/convert_element_type | solution.py:251
  149.8 1.7 collective-permute-start.3
  151.5 3.5 %all-to-all-done.4 = f32[32,1,4096]{2,1,0:T(1,128)} async-done(((f32[32,1,4096]{2,1,0:T(1,128)}), f32[32,1,4096]{2,1,0:T(1,128)}, u32[]{:S(2)}, u32[]{:S(2)}) %all-to-all-start.4) | async-done | bytes 524320 | tf_op jit(solution)/shard_map/all_to_all | solution.py:231
  157.6 3.3 %all-to-all-start.5 = ((f32[32,1,4096]{2,1,0:T(1,128)}), f32[32,1,4096]{2,1,0:T(1,128)}, u32[]{:S(2)}, u32[]{:S(2)}) async-start(f32[32,1,4096]{2,1,0:T(1,128)} %broadcast_in_dim.11), calls=%async_computation.5 | async-start | bytes 1048576 | tf_op jit(solution)/shard_map/all_to_all | solution.py:238
  161.6 7.8 %collective-permute-done.3 = bf16[2,1,384,384]{2,3,0,1:T(8,128)(2,1)} collective-permute-done((bf16[2,1,384,384]{2,3,0,1:T(8,128)(2,1)}, bf16[2,1,384,384]{2,3,0,1:T(8,128)(2,1)}, u32[]{:S(2)}, u32[]{:S(2)}) %collective-permute-start.3) | collective-permute-done | bytes 589856 | tf_op jit(solution)/shard_map/ppermute | solution.py:250
  169.4 4.1 %divide_add_fusion = f32[2,1,384,384]{2,3,0,1:T(8,128)} fusion(bf16[2,1,384,384]{2,3,0,1:T(8,128)(2,1)} %collective-permute-done.3, bf16[2,1,384,384]{2,3,0,1:T(8,128)(2,1)} %add_convert_fusion, f32[]{:T(128)} %reduce_max.19, f32[2,1,384,384]{2,3,0,1:T(8,128)S(1)} %copy-done.2, f32[]{:T(128)} %reduce_max.18, ...), kind=kLoop, calls=%fused_computation.51 | loop fusion | flops 2949120 | bytes 4718600 | tf_op jit(solution)/shard_map/add | solution.py:320
  173.5 2.7 %copy.71 = f32[2,1,384,384]{3,2,1,0:T(8,128)} copy(f32[2,1,384,384]{2,3,0,1:T(8,128)} %divide_add_fusion) | data formatting | bytes 2359296
  (90 shorter events, 34.0 us)
Async XLA Ops:
  0.6 16.7 %copy-start = (bf16[32,128,128]{2,1,0:T(8,128)(2,1)S(1)}, bf16[32,128,128]{2,1,0:T(8,128)(2,1)}, u32[]{:S(2)}) copy-start(bf16[32,128,128]{2,1,0:T(8,128)(2,1)} %param.6) | copy-start | bytes 3145732
  0.6 15.3 %copy-start.4 = (f32[2,1,384,384]{3,2,1,0:T(8,128)S(1)}, f32[2,1,384,384]{3,2,1,0:T(8,128)}, u32[]{:S(2)}) copy-start(f32[2,1,384,384]{3,2,1,0:T(8,128)} %param.10) | copy-start | bytes 3538948
  5.3 14.8 %all-to-all-start = ((s32[8,2,3,4]{3,1,2,0:T(2,128)}), s32[8,2,3,4]{3,1,2,0:T(2,128)S(1)}, u32[]{:S(2)}, u32[]{:S(2)}) async-start(s32[8,2,3,4]{3,1,2,0:T(2,128)} %copy.56), calls=%async_computation | async-start | bytes 49152 | tf_op jit(solution)/shard_map/all_to_all | solution.py:333
  20.1 42.4 %all-to-all-start.1 = ((bf16[8,2,3,128,128]{4,3,2,1,0:T(8,128)(2,1)}), bf16[8,2,3,128,128]{4,3,2,1,0:T(8,128)(2,1)S(1)}, u32[]{:S(2)}, u32[]{:S(2)}) async-start(bf16[8,2,3,128,128]{4,3,2,1,0:T(8,128)(2,1)} %copy.62), calls=%async_computation.1 | async-start | bytes 3145728 | tf_op jit(solution)/shard_map/all_to_all | solution.py:334
  76.6 8.4 %copy-start.5 = (bf16[2,1,384,384]{2,3,0,1:T(8,128)(2,1)}, bf16[2,1,384,384]{2,3,0,1:T(8,128)(2,1)S(1)}, u32[]{:S(2)}) copy-start(bf16[2,1,384,384]{2,3,0,1:T(8,128)(2,1)S(1)} %fusion.104) | copy-start | bytes 1769476
  76.6 8.4 %collective-permute-start = (bf16[2,1,384,384]{2,3,0,1:T(8,128)(2,1)S(1)}, bf16[2,1,384,384]{2,3,0,1:T(8,128)(2,1)}, u32[]{:S(2)}, u32[]{:S(2)}) collective-permute-start(bf16[2,1,384,384]{2,3,0,1:T(8,128)(2,1)S(1)} %fusion.104), channel_id=1, source_target_pairs={{0,1},{1,0},{2,3},{3,2},{4,5},{5,4},{6,7},{7,6},{8,9},{9,8},{10,11... | collective-permute-start | bytes 1769480 | tf_op jit(solution)/shard_map/ppermute | solution.py:250
  78.2 22.2 %all-to-all-start.2 = ((f32[32,1,4096]{2,1,0:T(1,128)}), f32[32,1,4096]{2,1,0:T(1,128)S(1)}, u32[]{:S(2)}, u32[]{:S(2)}) async-start(f32[32,1,4096]{2,1,0:T(1,128)} %bitcast.37), calls=%async_computation.2 | async-start | bytes 1048576 | tf_op jit(solution)/shard_map/all_to_all | solution.py:231
  85.0 21.6 %copy-start.2 = (f32[2,1,384,384]{2,3,0,1:T(8,128)S(1)}, f32[2,1,384,384]{2,3,0,1:T(8,128)}, u32[]{:S(2)}) copy-start(f32[2,1,384,384]{2,3,0,1:T(8,128)} %copy.63) | copy-start | bytes 3538948
  86.5 20.0 %collective-permute-start.1 = (bf16[2,1,384,384]{2,3,0,1:T(8,128)(2,1)S(1)}, bf16[2,1,384,384]{2,3,0,1:T(8,128)(2,1)}, u32[]{:S(2)}, u32[]{:S(2)}) collective-permute-start(bf16[2,1,384,384]{2,3,0,1:T(8,128)(2,1)S(1)} %add_convert_fusion.1), channel_id=1, source_target_pairs={{0,2},{1,3},{2,0},{3,1},{4,6},{5,7},{6,4},{7,5},{8,10},{9,11},{10,... | collective-permute-start | bytes 1769480 | tf_op jit(solution)/shard_map/ppermute | solution.py:250
  102.0 18.9 %all-to-all-start.3 = ((f32[32,1,4096]{2,1,0:T(1,128)}), f32[32,1,4096]{2,1,0:T(1,128)}, u32[]{:S(2)}, u32[]{:S(2)}) async-start(f32[32,1,4096]{2,1,0:T(1,128)} %broadcast_in_dim.10), calls=%async_computation.3 | async-start | bytes 1048576 | tf_op jit(solution)/shard_map/all_to_all | solution.py:238
  111.6 11.0 %copy-start.3 = (f32[4,2,128,128]{3,2,1,0:T(8,128)S(1)}, f32[4,2,128,128]{3,2,1,0:T(8,128)}, u32[]{:S(2)}) copy-start(f32[4,2,128,128]{3,2,1,0:T(8,128)} %probe_ref.1) | copy-start | bytes 1572868
  130.9 24.0 %all-to-all-start.4 = ((f32[32,1,4096]{2,1,0:T(1,128)}), f32[32,1,4096]{2,1,0:T(1,128)}, u32[]{:S(2)}, u32[]{:S(2)}) async-start(f32[32,1,4096]{2,1,0:T(1,128)} %bitcast.158), calls=%async_computation.4 | async-start | bytes 1048576 | tf_op jit(solution)/shard_map/all_to_all | solution.py:231
  145.5 15.4 %copy-start.1 = (f32[4,2,128,128]{3,2,1,0:T(8,128)S(1)}, f32[4,2,128,128]{3,2,1,0:T(8,128)}, u32[]{:S(2)}) copy-start(f32[4,2,128,128]{3,2,1,0:T(8,128)} %add.261.probe_ref) | copy-start | bytes 1572868
  145.5 2.2 %collective-permute-start.2 = (bf16[2,1,384,384]{2,3,0,1:T(8,128)(2,1)}, bf16[2,1,384,384]{2,3,0,1:T(8,128)(2,1)S(1)}, u32[]{:S(2)}, u32[]{:S(2)}) collective-permute-start(bf16[2,1,384,384]{2,3,0,1:T(8,128)(2,1)} %fusion.111), channel_id=1, source_target_pairs={{0,1},{1,0},{2,3},{3,2},{4,5},{5,4},{6,7},{7,6},{8,9},{9,8},{10,11... | collective-permute-start | bytes 1769480 | tf_op jit(solution)/shard_map/ppermute | solution.py:250
  149.8 19.6 %collective-permute-start.3 = (bf16[2,1,384,384]{2,3,0,1:T(8,128)(2,1)}, bf16[2,1,384,384]{2,3,0,1:T(8,128)(2,1)}, u32[]{:S(2)}, u32[]{:S(2)}) collective-permute-start(bf16[2,1,384,384]{2,3,0,1:T(8,128)(2,1)} %add_convert_fusion), channel_id=1, source_target_pairs={{0,2},{1,3},{2,0},{3,1},{4,6},{5,7},{6,4},{7,5},{8,10},{9,11},{10,... | collective-permute-start | bytes 1769480 | tf_op jit(solution)/shard_map/ppermute | solution.py:250
  157.6 18.9 %all-to-all-start.5 = ((f32[32,1,4096]{2,1,0:T(1,128)}), f32[32,1,4096]{2,1,0:T(1,128)}, u32[]{:S(2)}, u32[]{:S(2)}) async-start(f32[32,1,4096]{2,1,0:T(1,128)} %broadcast_in_dim.11), calls=%async_computation.5 | async-start | bytes 1048576 | tf_op jit(solution)/shard_map/all_to_all | solution.py:238
